TPU v7x, 32 devices: a whole 2x2x4 slice. The times are simulated.
32 devices in a mesh: seq: 4 (over y, x), batch: 8 (over z, core).
Axes of the slice: x: 2, y: 2, z: 4, core: 2. Of those that a mesh axis runs over, the one named last changes fastest.
Arguments:
- feats: bfloat16 [768, 4096], P('seq', 'batch'), parts along dimension 1, may hold values from -6 to 6
- qkv_weight: bfloat16 [768, 2304], replicated, may hold values from -0.21875 to 0.21875
- beta_weight: bfloat16 [768, 6], replicated, may hold values from -0.21875 to 0.21875
- beta_bias: float32 [6], replicated, may hold values from -7 to 0.5
- out_gain: float32 [768], replicated, may hold values from 0.1 to 1.9
Outputs:
- mixed: bfloat16 [4096, 768], P(('batch', 'seq')), parts along dimension 0
There are 8 independent parts, one for each index of `batch`. A program takes and returns all parts, laid end to end along the dimension named above; an argument that names none is the same for every part. Nothing has to cross between parts.
All inputs are finite; a program needn't handle non-finite values.
Results may differ from a plain program's by a relative error of at most 0.012.
Values may be sent and summed in bfloat16 or wider, within the bound.
No kernel may reach another device: no remote copies, remote signals or barrier semaphores. Data moves between devices by JAX's collectives and lax.ppermute only.
A program may use at most 64 MiB of HBM per device.

v0:
```python
import jax
import jax.numpy as jnp
from jax import lax
from jax.sharding import PartitionSpec as P

HEADS = 6
HD = 128
GROUP = 64


HIGHEST_ACCURACY = lax.Precision.HIGHEST


def entering(value, axis, join, neutral):
    count, mine = (lax.axis_size(axis), lax.axis_index(axis))
    pieces = jax.tree.map(lambda part: lax.all_gather(part, axis), value)
    running = jax.tree.map(
        lambda part, zero: jnp.full_like(part, 0) + jnp.asarray(zero, part.dtype), value, neutral
    )

    def turn(position, running):
        longer = join(running, jax.tree.map(lambda part: part[position], pieces))
        return jax.tree.map(lambda new, old: jnp.where(position < mine, new, old), longer, running)

    return lax.fori_loop(0, count - 1, turn, running)


def unit_inverse(gram):
    eye_block = jnp.eye(gram.shape[-1], dtype=jnp.float32)
    negated = -jnp.tril(gram, -1)
    inverse = eye_block + negated
    power = negated
    for level in range(5):
        power = jnp.einsum("nhij,nhjk->nhik", power, power, precision=HIGHEST_ACCURACY)
        inverse = inverse + jnp.einsum(
            "nhij,nhjk->nhik", inverse, power, precision=HIGHEST_ACCURACY
        )
    return inverse


def prepare(qkv, beta):
    rows = qkv.shape[0]
    blocks_count = rows // GROUP
    pieces = qkv.astype(jnp.float32).reshape(rows, 3, HEADS, HD)
    query = pieces[:, 0]
    keys = pieces[:, 1]
    values = pieces[:, 2]
    query = query * lax.rsqrt(jnp.sum(query * query, -1, keepdims=True) + 1e-06)
    keys = keys * lax.rsqrt(jnp.sum(keys * keys, -1, keepdims=True) + 1e-06)

    def blocks(arr):
        return arr.reshape(blocks_count, GROUP, HEADS, arr.shape[-1]).transpose(0, 2, 1, 3)

    query = blocks(query)
    keys = blocks(keys)
    values = blocks(values)
    rates = blocks(beta[:, :, None])
    weighted = keys * rates
    gram = jnp.einsum("nhik,nhjk->nhij", weighted, keys, precision=HIGHEST_ACCURACY)
    inverse = unit_inverse(gram)
    right = jnp.concatenate([weighted, values * rates], -1)
    solved = jnp.einsum("nhij,nhjk->nhik", inverse, right, precision=HIGHEST_ACCURACY)
    wfac = solved[..., :HD]
    ufac = solved[..., HD:]
    scores = jnp.tril(jnp.einsum("nhik,nhjk->nhij", query, keys, precision=HIGHEST_ACCURACY))
    return (query, keys, wfac, ufac, scores)


def finish(outputs, out_gain):
    rows = outputs.shape[0] * GROUP
    flat = outputs.transpose(0, 2, 1, 3).reshape(rows, HEADS, HD)
    power = jnp.mean(flat * flat, -1, keepdims=True) + 1e-06
    normed = flat * lax.rsqrt(power) * out_gain.reshape(HEADS, HD)
    return normed.reshape(rows, HEADS * HD).astype(jnp.bfloat16)


def compose(early, late):
    first_move, first_offset = early
    second_move, second_offset = late
    move = jnp.einsum("hij,hjk->hik", second_move, first_move, precision=HIGHEST_ACCURACY)
    offset = (
        jnp.einsum("hij,hjk->hik", second_move, first_offset, precision=HIGHEST_ACCURACY)
        + second_offset
    )
    return (move, offset)


def body(feats, qkv_weight, beta_weight, beta_bias, out_gain):
    local = lax.all_to_all(feats, "seq", split_axis=1, concat_axis=0, tiled=True)
    qkv = lax.dot_general(
        local, qkv_weight, (((0,), (0,)), ((), ())), preferred_element_type=jnp.float32
    ).astype(jnp.bfloat16)
    logits = lax.dot_general(
        local, beta_weight, (((0,), (0,)), ((), ())), preferred_element_type=jnp.float32
    )
    beta = jax.nn.sigmoid(logits + beta_bias)
    query, keys, wfac, ufac, scores = prepare(qkv, beta)
    eye_heads = jnp.broadcast_to(jnp.eye(HD, dtype=jnp.float32), (HEADS, HD, HD))
    empty = jnp.zeros((HEADS, HD, HD), jnp.float32)

    def first_pass(joint_matrix, item):
        query_block, key_block, weight_block, update_block, state_block = item
        held_value = jnp.einsum(
            "rnf,rfw->rnw", weight_block, joint_matrix, precision=HIGHEST_ACCURACY
        )
        carried_state = joint_matrix[..., HD:]
        residual_value = update_block - held_value[..., HD:]
        output_rows = jnp.einsum(
            "rnf,rfw->rnw", query_block, carried_state, precision=HIGHEST_ACCURACY
        ) + jnp.einsum("fco,fop->fcp", state_block, residual_value, precision=HIGHEST_ACCURACY)
        target_value = jnp.concatenate([-held_value[..., :HD], residual_value], -1)
        joint_matrix = joint_matrix + jnp.einsum(
            "mjr,mjz->mrz", key_block, target_value, precision=HIGHEST_ACCURACY
        )
        return (joint_matrix, output_rows)

    joint_start = jnp.concatenate([eye_heads, empty], -1)
    joint_matrix, local_out = lax.scan(first_pass, joint_start, (query, keys, wfac, ufac, scores))
    moves = joint_matrix[..., :HD]
    offsets = joint_matrix[..., HD:]
    prior = entering((moves, offsets), "seq", compose, (eye_heads, empty))
    incoming = prior[1]

    def second_pass(loop_carry, item):
        query_block, key_block, weight_block, state_block = item
        held_value = jnp.einsum(
            "rnf,rfw->rnw", weight_block, loop_carry, precision=HIGHEST_ACCURACY
        )
        output_rows = jnp.einsum(
            "rnf,rfw->rnw", query_block, loop_carry, precision=HIGHEST_ACCURACY
        ) - jnp.einsum("fco,fop->fcp", state_block, held_value, precision=HIGHEST_ACCURACY)
        loop_carry = loop_carry - jnp.einsum(
            "mjr,mjz->mrz", key_block, held_value, precision=HIGHEST_ACCURACY
        )
        return (loop_carry, output_rows)

    final_carry, added_out = lax.scan(second_pass, incoming, (query, keys, wfac, scores))
    return finish(local_out + added_out, out_gain)


def solution(mesh):
    placed = (P("seq", "batch"), P(), P(), P(), P())
    return jax.shard_map(
        body, mesh=mesh, in_specs=placed, out_specs=P(("batch", "seq"), None), check_vma=False
    )
```

profile of v0, /device:TPU:0, one launch (start us, length us, event | category | flops | bytes accessed | tf_op | source)
XLA Modules:
  0.0 174.5 jit_solution(12034097138395976783)
XLA Ops:
  6.5 1.8 %copy_bitcast_fusion = bf16[192,4,128]{2,0,1:T(8,128)(2,1)} fusion(bf16[192,512]{1,0:T(8,128)(2,1)} %param.11), kind=kLoop, calls=%fused_computation.83 | loop fusion | bytes 393216 | tf_op jit(solution)/shard_map/all_to_all | solution.py:89
  8.3 5.2 %all-to-all-start = ((bf16[192,4,128]{2,0,1:T(8,128)(2,1)}), bf16[192,4,128]{2,0,1:T(8,128)(2,1)}, u32[]{:S(2)}, u32[]{:S(2)}) async-start(bf16[192,4,128]{2,0,1:T(8,128)(2,1)} %copy_bitcast_fusion), calls=%async_computation | async-start | bytes 393216 | tf_op jit(solution)/shard_map/all_to_all | solution.py:89
  17.3 1.5 all-to-all-done
  18.8 2.6 %fusion.45 = f32[128,2304]{1,0:T(8,128)} fusion(bf16[768,128]{1,0:T(8,128)(2,1)} %bitcast.12, bf16[768,2304]{1,0:T(8,128)(2,1)S(1)} %copy-done), kind=kOutput, calls=%fused_computation.53 | convolution fusion | flops 453574656 | bytes 4915200 | tf_op jit(solution)/shard_map/dot_general | solution.py:90
  21.4 2.7 %copy.50 = f32[128,2304]{0,1:T(8,128)} copy(f32[128,2304]{1,0:T(8,128)} %fusion.45) | data formatting | bytes 2359296 | tf_op jit(solution)/shard_map/reshape | solution.py:44
  24.1 2.3 %multiply_reduce_fusion.1 = (f32[128,6]{0,1:T(8,128)S(1)}, f32[128,6]{0,1:T(8,128)S(1)}, f32[128,1,6,128]{0,3,2,1:T(8,128)}, f32[128,1,6,128]{0,3,2,1:T(8,128)}, f32[128,1,6,128]{0,3,2,1:T(8,128)}) fusion(f32[128,3,6,128]{0,3,2,1:T(8,128)} %bitcast.151), kind=kLoop, calls=%fused_computation.80 | loop fusion | flops 391680 | bytes 2365440 | tf_op jit(solution)/shard_map/reduce_sum | solution.py:48
  28.3 1.9 %copy.51 = f32[128,1,6,128]{3,0,2,1:T(8,128)} copy(f32[128,1,6,128]{0,3,2,1:T(8,128)} %get-tuple-element.311) | data formatting | bytes 786432 | tf_op jit(solution)/shard_map/slice | solution.py:46
  30.2 1.9 %copy.55 = f32[128,1,6,128]{3,0,2,1:T(8,128)} copy(f32[128,1,6,128]{0,3,2,1:T(8,128)} %get-tuple-element.310) | data formatting | bytes 786432 | tf_op jit(solution)/shard_map/slice | solution.py:47
  32.2 1.7 fusion.50
  46.0 1.9 %copy.57 = f32[128,1,6,128]{3,0,2,1:T(8,128)} copy(f32[128,1,6,128]{0,3,2,1:T(8,128)} %get-tuple-element.309) | data formatting | bytes 786432 | tf_op jit(solution)/shard_map/slice | solution.py:45
  52.3 16.6 %while.38 = (s32[]{:T(128)}, f32[6,128,256]{2,1,0:T(8,128)}, f32[2,6,64,128]{3,2,1,0:T(8,128)}, f32[2,6,64,128]{3,2,1,0:T(8,128)}, f32[2,6,64,128]{3,2,1,0:T(8,1...) while((s32[]{:T(128)}, f32[6,128,256]{2,1,0:T(8,128)}, ...), condition=%wide.region_3.4_spmd, body=%wide.region_2.3_spmd.sunk | while | flops 415678464 | bytes 10029241 | solution.py:118
  52.3 1.9 %fusion.138 = f32[6,64,256]{2,1,0:T(8,128)S(1)} fusion(f32[6,128,256]{2,1,0:T(8,128)} %get-tuple-element.456, f32[2,6,64,128]{3,2,1,0:T(8,128)} %get-tuple-element.468, s32[]{:T(128)} %get-tuple-element.455), kind=kOutput, calls=%fused_computation.13.clone.1 | convolution fusion | flops 150994944 | bytes 1376768 | tf_op jit(solution)/shard_map/while/body/eval_jaxpr/rnf,rfw->rnw/dot_general | solution.py:103
  56.7 2.9 %convolution_add_fusion.10 = f32[6,128,256]{2,1,0:T(8,128)} fusion(f32[6,128,256]{2,1,0:T(8,128)} %get-tuple-element.456, f32[6,64,128]{2,1,0:T(8,128)S(1)} %get-tuple-element.432, f32[6,64,128]{2,1,0:T(8,128)S(1)} %get-tuple-element.433, f32[2,6,64,128]{3,2,1,0:T(8,128)S(1)} %copy-done.3, s32[]{:T(128)} %get-tuple-element.455), kind=kOutput, calls=%fused_computation.clone.1 | convolution fusion | flops 151289856 | bytes 2162692 | tf_op jit(solution)/shard_map/while/body/eval_jaxpr/mjr,mjz->mrz/dot_general | solution.py:112
  60.6 1.9 %fusion.138 = f32[6,64,256]{2,1,0:T(8,128)S(1)} fusion(f32[6,128,256]{2,1,0:T(8,128)} %get-tuple-element.456, f32[2,6,64,128]{3,2,1,0:T(8,128)} %get-tuple-element.468, s32[]{:T(128)} %get-tuple-element.455), kind=kOutput, calls=%fused_computation.13.clone.1 | convolution fusion | flops 150994944 | bytes 1376768 | tf_op jit(solution)/shard_map/while/body/eval_jaxpr/rnf,rfw->rnw/dot_general | solution.py:103
  65.0 2.9 %convolution_add_fusion.10 = f32[6,128,256]{2,1,0:T(8,128)} fusion(f32[6,128,256]{2,1,0:T(8,128)} %get-tuple-element.456, f32[6,64,128]{2,1,0:T(8,128)S(1)} %get-tuple-element.432, f32[6,64,128]{2,1,0:T(8,128)S(1)} %get-tuple-element.433, f32[2,6,64,128]{3,2,1,0:T(8,128)S(1)} %copy-done.3, s32[]{:T(128)} %get-tuple-element.455), kind=kOutput, calls=%fused_computation.clone.1 | convolution fusion | flops 151289856 | bytes 2162692 | tf_op jit(solution)/shard_map/while/body/eval_jaxpr/mjr,mjz->mrz/dot_general | solution.py:112
  68.9 2.1 %fusion.65 = (f32[6,128,128]{2,1,0:T(8,128)}, f32[6,128,128]{2,1,0:T(8,128)}) fusion(f32[6,128,256]{2,1,0:T(8,128)} %get-tuple-element.180), kind=kLoop, calls=%fused_computation.98 | loop fusion | bytes 1572864 | tf_op jit(solution)/shard_map/slice | solution.py:120
  71.8 30.7 %all-gather.5.cloned.1.call-done = f32[24,128,128]{2,1,0:T(8,128)} async-done(((f32[6,128,128]{2,1,0:T(8,128)}), f32[24,128,128]{2,1,0:T(8,128)}) %all-gather.5.cloned.1.call-update) | async-done | bytes 1572880 | tf_op jit(solution)/shard_map/all_gather | solution.py:16
  102.4 32.7 %all-gather.7.cloned.1.call-done = f32[24,128,128]{2,1,0:T(8,128)} async-done(((f32[6,128,128]{2,1,0:T(8,128)}), f32[24,128,128]{2,1,0:T(8,128)}) %all-gather.7.cloned.1.call-update) | async-done | bytes 1572880 | tf_op jit(solution)/shard_map/all_gather | solution.py:16
  135.1 10.2 %while.40 = (s32[]{:T(128)}, f32[6,128,128]{2,1,0:T(8,128)}, s32[]{:T(128)}, f32[4,6,128,128]{3,2,1,0:T(8,128)}, f32[4,6,128,128]{3,2,1,0:T(8,128)}, /*index=5*/s32[]{:T(128)}, s32[]{:T(128)}) while((s32[]{:T(128)}, f32[6,128,128]{2,1,0:T(8,128)}, s32[]{:T(128)}, f32[4,6,128,128]{3,2,1,0:T(8,128)}, f32[4,6,128,128]{3,2,1,0:T(8,128)}, ...), condition=%wide.region_5.6_spmd.clone, body=%wide.region_4.5_spmd.clone.sunk | while | flops 151388160 | bytes 2755167 | solution.py:25
  136.1 2.4 %fusion.154 = f32[6,128,128]{2,1,0:T(8,128)} fusion(f32[6,128,128]{2,1,0:T(8,128)S(1)} %copy.105, f32[4,6,128,128]{3,2,1,0:T(8,128)} %get-tuple-element.491, s32[]{:T(128)} %get-tuple-element.480, f32[4,6,128,128]{3,2,1,0:T(8,128)} %get-tuple-element.490, pred[]{:T(512)S(6)} %compare.4, pred[]{:T(512)S(6)} %lt.30), kind=kOutput, calls=%fused_computation.44.clone.1 | convolution fusion | flops 151388160 | bytes 1968640 | tf_op jit(solution)/shard_map/while/body/eval_jaxpr/hij,hjk->hik/dot_general | solution.py:82
  139.5 2.4 %fusion.154 = f32[6,128,128]{2,1,0:T(8,128)} fusion(f32[6,128,128]{2,1,0:T(8,128)S(1)} %copy.105, f32[4,6,128,128]{3,2,1,0:T(8,128)} %get-tuple-element.491, s32[]{:T(128)} %get-tuple-element.480, f32[4,6,128,128]{3,2,1,0:T(8,128)} %get-tuple-element.490, pred[]{:T(512)S(6)} %compare.4, pred[]{:T(512)S(6)} %lt.30), kind=kOutput, calls=%fused_computation.44.clone.1 | convolution fusion | flops 151388160 | bytes 1968640 | tf_op jit(solution)/shard_map/while/body/eval_jaxpr/hij,hjk->hik/dot_general | solution.py:82
  142.9 2.4 %fusion.154 = f32[6,128,128]{2,1,0:T(8,128)} fusion(f32[6,128,128]{2,1,0:T(8,128)S(1)} %copy.105, f32[4,6,128,128]{3,2,1,0:T(8,128)} %get-tuple-element.491, s32[]{:T(128)} %get-tuple-element.480, f32[4,6,128,128]{3,2,1,0:T(8,128)} %get-tuple-element.490, pred[]{:T(512)S(6)} %compare.4, pred[]{:T(512)S(6)} %lt.30), kind=kOutput, calls=%fused_computation.44.clone.1 | convolution fusion | flops 151388160 | bytes 1968640 | tf_op jit(solution)/shard_map/while/body/eval_jaxpr/hij,hjk->hik/dot_general | solution.py:82
  146.1 13.8 %while.39 = (s32[]{:T(128)}, f32[6,128,128]{2,1,0:T(8,128)}, f32[2,6,64,128]{3,2,1,0:T(8,128)}, f32[2,6,64,128]{3,2,1,0:T(8,128)}, f32[2,6,64,128]{3,2,1,0:T(8,1...) while((s32[]{:T(128)}, f32[6,128,128]{2,1,0:T(8,128)}, ...), condition=%wide.region_7.8_spmd, body=%wide.region_6.7_spmd.sunk | while | flops 264388608 | bytes 9046217 | solution.py:137
  146.1 1.6 fusion.149
  147.8 1.6 fusion.150
  150.5 2.6 %convolution_subtract_fusion.3 = f32[6,128,128]{2,1,0:T(8,128)} fusion(f32[6,128,128]{2,1,0:T(8,128)} %get-tuple-element.503, f32[6,64,128]{2,1,0:T(8,128)S(1)} %fusion.149, f32[2,6,64,128]{3,2,1,0:T(8,128)S(1)} %copy-done.4, s32[]{:T(128)} %get-tuple-element.502), kind=kOutput, calls=%fused_computation.25.clone.1 | convolution fusion | flops 75595776 | bytes 1179652 | tf_op jit(solution)/shard_map/while/body/eval_jaxpr/mjr,mjz->mrz/dot_general | solution.py:132
  153.0 1.6 fusion.149
  154.7 1.6 fusion.150
  157.4 2.6 %convolution_subtract_fusion.3 = f32[6,128,128]{2,1,0:T(8,128)} fusion(f32[6,128,128]{2,1,0:T(8,128)} %get-tuple-element.503, f32[6,64,128]{2,1,0:T(8,128)S(1)} %fusion.149, f32[2,6,64,128]{3,2,1,0:T(8,128)S(1)} %copy-done.4, s32[]{:T(128)} %get-tuple-element.502), kind=kOutput, calls=%fused_computation.25.clone.1 | convolution fusion | flops 75595776 | bytes 1179652 | tf_op jit(solution)/shard_map/while/body/eval_jaxpr/mjr,mjz->mrz/dot_general | solution.py:132
  160.0 1.9 %multiply_reduce_fusion = (f32[2,64,6]{1,2,0:T(8,128)S(1)}, f32[2,64,6,128]{3,1,2,0:T(8,128)}) fusion(f32[2,6,64,128]{3,2,1,0:T(8,128)} %get-tuple-element.179, f32[2,6,64,128]{3,2,1,0:T(8,128)} %get-tuple-element.182), kind=kLoop, calls=%fused_computation.77 | loop fusion | flops 294144 | bytes 1182720 | tf_op jit(solution)/shard_map/reduce_sum | solution.py:72
  162.8 1.9 %copy.63 = f32[128,768]{1,0:T(8,128)} copy(f32[128,768]{0,1:T(8,128)} %bitcast.156) | data formatting | bytes 786432 | tf_op jit(solution)/shard_map/mul | solution.py:73
  165.9 1.8 %fusion.56 = bf16[128,768]{1,0:T(8,128)(2,1)} fusion(f32[128,768]{1,0:T(8,128)} %copy.63, f32[16,8,6,128]{3,2,1,0:T(8,128)S(1)} %bitcast.154, f32[768]{0:T(1024)S(1)} %copy-done.12), kind=kLoop, calls=%fused_computation.73 | loop fusion | flops 294912 | bytes 986112 | tf_op jit(solution)/shard_map/convert_element_type | solution.py:74
  (93 shorter events, 37.9 us)
Async XLA Ops:
  6.5 12.3 %copy-start = (bf16[768,2304]{1,0:T(8,128)(2,1)S(1)}, bf16[768,2304]{1,0:T(8,128)(2,1)}, u32[]{:S(2)}) copy-start(bf16[768,2304]{1,0:T(8,128)(2,1)} %param.12) | copy-start | bytes 10616836
  8.3 10.5 %all-to-all-start = ((bf16[192,4,128]{2,0,1:T(8,128)(2,1)}), bf16[192,4,128]{2,0,1:T(8,128)(2,1)}, u32[]{:S(2)}, u32[]{:S(2)}) async-start(bf16[192,4,128]{2,0,1:T(8,128)(2,1)} %copy_bitcast_fusion), calls=%async_computation | async-start | bytes 393216 | tf_op jit(solution)/shard_map/all_to_all | solution.py:89
  13.5 88.9 %all-gather.5.cloned.1.call-start = ((), (), s32[]{:S(2)}) async-start(), calls=%async_computation.1 | async-start | bytes 1966080 | tf_op jit(solution)/shard_map/all_gather | solution.py:16
  35.2 2.1 %copy-start.11 = (pred[64,64]{1,0:T(8,128)(4,1)S(1)}, pred[64,64]{1,0:T(8,128)(4,1)}, u32[]{:S(2)}) copy-start(pred[64,64]{1,0:T(8,128)(4,1)} %iota_compare_fusion.2) | copy-start | bytes 12292
  37.3 1.9 %copy-start.1 = (f32[2,6,64,128]{3,2,1,0:T(8,128)}, f32[2,6,64,128]{3,2,1,0:T(8,128)S(1)}, u32[]{:S(2)}) copy-start(f32[2,6,64,128]{3,2,1,0:T(8,128)S(1)} %get-tuple-element.497) | copy-start | bytes 1179652
  37.3 1.9 %copy-start.10 = (f32[64,64]{1,0:T(8,128)S(1)}, f32[64,64]{1,0:T(8,128)}, u32[]{:S(2)}) copy-start(f32[64,64]{1,0:T(8,128)} %fusion.61) | copy-start | bytes 49156
  48.0 2.0 %copy-start.2 = (f32[2,6,64,128]{3,2,1,0:T(8,128)S(1)}, f32[2,6,64,128]{3,2,1,0:T(8,128)}, u32[]{:S(2)}) copy-start(f32[2,6,64,128]{3,2,1,0:T(8,128)} %copy-done.1) | copy-start | bytes 1179652
  52.3 2.9 %copy-start.5 = (f32[2,6,64,128]{3,2,1,0:T(8,128)S(1)}, f32[2,6,64,128]{3,2,1,0:T(8,128)}, u32[]{:S(2)}) copy-start(f32[2,6,64,128]{3,2,1,0:T(8,128)} %get-tuple-element.470) | copy-start | bytes 1179652 | tf_op jit(solution)/shard_map/while
  52.3 4.4 %copy-start.3 = (f32[2,6,64,128]{3,2,1,0:T(8,128)S(1)}, f32[2,6,64,128]{3,2,1,0:T(8,128)}, u32[]{:S(2)}) copy-start(f32[2,6,64,128]{3,2,1,0:T(8,128)} %get-tuple-element.467) | copy-start | bytes 1179652 | tf_op jit(solution)/shard_map/while
  55.1 4.4 %copy-start.6 = (f32[2,6,64,64]{3,2,1,0:T(8,128)S(1)}, f32[2,6,64,64]{3,2,1,0:T(8,128)}, u32[]{:S(2)}) copy-start(f32[2,6,64,64]{3,2,1,0:T(8,128)} %get-tuple-element.471) | copy-start | bytes 589828 | tf_op jit(solution)/shard_map/while
  60.6 2.9 %copy-start.5 = (f32[2,6,64,128]{3,2,1,0:T(8,128)S(1)}, f32[2,6,64,128]{3,2,1,0:T(8,128)}, u32[]{:S(2)}) copy-start(f32[2,6,64,128]{3,2,1,0:T(8,128)} %get-tuple-element.470) | copy-start | bytes 1179652 | tf_op jit(solution)/shard_map/while
  60.6 4.4 %copy-start.3 = (f32[2,6,64,128]{3,2,1,0:T(8,128)S(1)}, f32[2,6,64,128]{3,2,1,0:T(8,128)}, u32[]{:S(2)}) copy-start(f32[2,6,64,128]{3,2,1,0:T(8,128)} %get-tuple-element.467) | copy-start | bytes 1179652 | tf_op jit(solution)/shard_map/while
  63.4 4.4 %copy-start.6 = (f32[2,6,64,64]{3,2,1,0:T(8,128)S(1)}, f32[2,6,64,64]{3,2,1,0:T(8,128)}, u32[]{:S(2)}) copy-start(f32[2,6,64,64]{3,2,1,0:T(8,128)} %get-tuple-element.471) | copy-start | bytes 589828 | tf_op jit(solution)/shard_map/while
  71.0 64.1 %all-gather.7.cloned.1.call-start = ((), (), s32[]{:S(2)}) async-start(), calls=%async_computation.2 | async-start | bytes 1966080 | tf_op jit(solution)/shard_map/all_gather | solution.py:16
  146.1 3.2 %copy-start.7 = (f32[2,6,64,64]{3,2,1,0:T(8,128)S(1)}, f32[2,6,64,64]{3,2,1,0:T(8,128)}, u32[]{:S(2)}) copy-start(f32[2,6,64,64]{3,2,1,0:T(8,128)} %get-tuple-element.516) | copy-start | bytes 589828 | tf_op jit(solution)/shard_map/while
  146.1 3.3 %copy-start.8 = (f32[2,6,64,128]{3,2,1,0:T(8,128)S(1)}, f32[2,6,64,128]{3,2,1,0:T(8,128)}, u32[]{:S(2)}) copy-start(f32[2,6,64,128]{3,2,1,0:T(8,128)} %get-tuple-element.504) | copy-start | bytes 1179652 | tf_op jit(solution)/shard_map/while
  146.1 4.3 %copy-start.4 = (f32[2,6,64,128]{3,2,1,0:T(8,128)S(1)}, f32[2,6,64,128]{3,2,1,0:T(8,128)}, u32[]{:S(2)}) copy-start(f32[2,6,64,128]{3,2,1,0:T(8,128)} %get-tuple-element.513) | copy-start | bytes 1179652 | tf_op jit(solution)/shard_map/while
  149.7 0.8 copy-start.9
  153.0 3.2 %copy-start.7 = (f32[2,6,64,64]{3,2,1,0:T(8,128)S(1)}, f32[2,6,64,64]{3,2,1,0:T(8,128)}, u32[]{:S(2)}) copy-start(f32[2,6,64,64]{3,2,1,0:T(8,128)} %get-tuple-element.516) | copy-start | bytes 589828 | tf_op jit(solution)/shard_map/while
  153.0 3.3 %copy-start.8 = (f32[2,6,64,128]{3,2,1,0:T(8,128)S(1)}, f32[2,6,64,128]{3,2,1,0:T(8,128)}, u32[]{:S(2)}) copy-start(f32[2,6,64,128]{3,2,1,0:T(8,128)} %get-tuple-element.504) | copy-start | bytes 1179652 | tf_op jit(solution)/shard_map/while
  153.0 4.3 %copy-start.4 = (f32[2,6,64,128]{3,2,1,0:T(8,128)S(1)}, f32[2,6,64,128]{3,2,1,0:T(8,128)}, u32[]{:S(2)}) copy-start(f32[2,6,64,128]{3,2,1,0:T(8,128)} %get-tuple-element.513) | copy-start | bytes 1179652 | tf_op jit(solution)/shard_map/while
  156.6 0.8 copy-start.9
  160.0 6.0 %copy-start.12 = (f32[768]{0:T(1024)S(1)}, f32[768]{0:T(1024)}, u32[]{:S(2)}) copy-start(f32[768]{0:T(1024)} %param.15) | copy-start | bytes 9220
Sparse Core Ops, SparseCore 0:
  71.1 31.2 all-gather.4
  104.3 30.8 all-gather.6
where the time goes:
time: 176 us; the launch traced here: 175 us
  waiting for transfers between devices  65.4 us (37%)
  matrix products  46.7 us (27%)
  local copies, waits for them, and re-layouts  30.2 us (17%)
  between operations  13.6 us (8%)
  other arithmetic  13 us (7%)
  starting transfers between devices  5.42 us (3%)
    all_gather x2, waiting for transfers between devices, entering(): pieces = jax.tree.map(lambda part: lax.all_gather(part, axis), value)  63.4 us
    dot_general x3, matrix products, compose(): jnp.einsum('hij,hjk->hik', second_move, first_offset, precision=HIGHEST_A...  7.21 us
    dot_general x2, matrix products, first_pass(): jnp.einsum('mjr,mjz->mrz', key_block, target_value, precision=HIGHEST_ACC...  5.78 us
    all_to_all x1, starting transfers between devices, body(): lax.all_to_all(feats, 'seq', split_axis=1, concat_axis=0, tiled=True)  5.19 us
    dot_general x2, matrix products, second_pass(): jnp.einsum('mjr,mjz->mrz', key_block, held_value, precision=HIGHEST_ACCUR...  5.12 us
    while x31, local copies, waits for them, and re-layouts  4.53 us
    dot_general x2, matrix products, first_pass(): jnp.einsum('rnf,rfw->rnw', weight_block, joint_matrix, precision=HIGHEST_...  3.72 us
  transfers between devices with their start and end apart: 3, of which 3 were waited for; matrix products, arithmetic and copies ran while one was open for 2% of the time, Pallas kernels for 0%

commit v1 on v0

v1 whole, which is shorter than its diff:
```python
import functools

import jax
import jax.numpy as jnp
from jax import lax
from jax.experimental import pallas as pl
from jax.experimental.pallas import tpu as pltpu
from jax.sharding import PartitionSpec as P

HEADS = 6
HD = 128
GROUP = 64

HIGHEST_ACCURACY = lax.Precision.HIGHEST


def mm(a, b):
    return lax.dot_general(
        a, b, (((1,), (0,)), ((), ())), precision=HIGHEST_ACCURACY,
        preferred_element_type=jnp.float32,
    )


def mm_nt(a, b):
    return lax.dot_general(
        a, b, (((1,), (1,)), ((), ())), precision=HIGHEST_ACCURACY,
        preferred_element_type=jnp.float32,
    )


def mm_tn(a, b):
    return lax.dot_general(
        a, b, (((0,), (0,)), ((), ())), precision=HIGHEST_ACCURACY,
        preferred_element_type=jnp.float32,
    )


def unit_normed(x):
    return x * lax.rsqrt(jnp.sum(x * x, -1, keepdims=True) + 1e-06)


def delta_kernel(qkv_ref, beta_ref, gain_ref, out_ref, state_ref):
    frames = qkv_ref.shape[0]
    width = HEADS * HD
    state_ref[...] = jnp.zeros_like(state_ref)
    row = lax.broadcasted_iota(jnp.int32, (GROUP, GROUP), 0)
    col = lax.broadcasted_iota(jnp.int32, (GROUP, GROUP), 1)
    eye = jnp.where(row == col, 1.0, 0.0).astype(jnp.float32)

    def step(c, carry):
        r0 = pl.multiple_of(c * GROUP, GROUP)
        rows = pl.ds(r0, GROUP)
        for h in range(HEADS):
            query = unit_normed(qkv_ref[rows, pl.ds(h * HD, HD)].astype(jnp.float32))
            keys = unit_normed(qkv_ref[rows, pl.ds(width + h * HD, HD)].astype(jnp.float32))
            values = qkv_ref[rows, pl.ds(2 * width + h * HD, HD)].astype(jnp.float32)
            rates = beta_ref[rows, pl.ds(h, 1)]
            weighted = keys * rates
            gram = mm_nt(weighted, keys)
            negated = jnp.where(row > col, -gram, 0.0)
            inverse = eye + negated
            power = negated
            for level in range(5):
                power = mm(power, power)
                inverse = inverse + mm(inverse, power)
            wfac = mm(inverse, weighted)
            ufac = mm(inverse, values * rates)
            scores = jnp.where(row >= col, mm_nt(query, keys), 0.0)
            state = state_ref[h]
            residual = ufac - mm(wfac, state)
            output = mm(query, state) + mm(scores, residual)
            state_ref[h] = state + mm_tn(keys, residual)
            power_mean = jnp.mean(output * output, -1, keepdims=True) + 1e-06
            gain = gain_ref[:, pl.ds(h * HD, HD)]
            out_ref[rows, pl.ds(h * HD, HD)] = (output * lax.rsqrt(power_mean) * gain).astype(
                out_ref.dtype
            )
        return carry

    lax.fori_loop(0, frames // GROUP, step, 0)


def delta_layer(qkv, beta, gain):
    frames = qkv.shape[0]
    return pl.pallas_call(
        delta_kernel,
        out_shape=jax.ShapeDtypeStruct((frames, HEADS * HD), jnp.bfloat16),
        in_specs=[
            pl.BlockSpec(memory_space=pltpu.VMEM),
            pl.BlockSpec(memory_space=pltpu.VMEM),
            pl.BlockSpec(memory_space=pltpu.VMEM),
        ],
        out_specs=pl.BlockSpec(memory_space=pltpu.VMEM),
        scratch_shapes=[pltpu.VMEM((HEADS, HD, HD), jnp.float32)],
    )(qkv, beta, gain)


def body(feats, qkv_weight, beta_weight, beta_bias, out_gain):
    full = lax.all_gather(feats, "seq", axis=0, tiled=True)
    qkv = lax.dot_general(
        full, qkv_weight, (((0,), (0,)), ((), ())), preferred_element_type=jnp.float32
    ).astype(jnp.bfloat16)
    logits = lax.dot_general(
        full, beta_weight, (((0,), (0,)), ((), ())), preferred_element_type=jnp.float32
    )
    beta = jax.nn.sigmoid(logits + beta_bias)
    mixed = delta_layer(qkv, beta, out_gain.reshape(1, -1))
    count = lax.axis_size("seq")
    mine = lax.axis_index("seq")
    rows = mixed.shape[0] // count
    return lax.dynamic_slice_in_dim(mixed, mine * rows, rows, 0)


def solution(mesh):
    placed = (P("seq", "batch"), P(), P(), P(), P())
    return jax.shard_map(
        body, mesh=mesh, in_specs=placed, out_specs=P(("batch", "seq"), None), check_vma=False
    )
```

time: 176 us -> 114 us (0.65); the launches traced: 175 us -> 114 us
  Pallas kernels: 0 us -> 93.4 us
  waiting for transfers between devices: 65.4 us -> 0 us
  matrix products: 46.7 us -> 4.57 us
  local copies, waits for them, and re-layouts: 30.2 us -> 2.22 us
  blocking collectives: 0 us -> 14.1 us
  between operations: 13.6 us -> 0.03 us
  other arithmetic: 13 us -> 0 us
  starting transfers between devices: 5.42 us -> 0 us
    pallas_call x0 -> x1, Pallas kernels: none -> 93.4 us  [delta_layer(): pl.pallas_call(delta_kernel, out_shape=jax.ShapeDtypeStruct((frames, HEAD...]
    all_gather x2 -> x0, waiting for transfers between devices: 63.4 us -> none  [entering(): pieces = jax.tree.map(lambda part: lax.all_gather(part, axis), value)]
    dot_general x34 -> x2, matrix products: 46.7 us -> 4.57 us  [the longest x1 3.46 us: body(): lax.dot_general(full, qkv_weight, (((0,), (0,)), ((), ())), preferred_ele...]
    all_gather x0 -> x1, blocking collectives: none -> 14.1 us  [body(): full = lax.all_gather(feats, 'seq', axis=0, tiled=True)]
    slice x5 -> x0, local copies, waits for them, and re-layouts: 8.78 us -> none  [the longest x1 2.06 us: body(): offsets = joint_matrix[..., HD:]]
    while x32 -> x0, local copies, waits for them, and re-layouts: 5.31 us -> none
    all_to_all x1 -> x0, starting transfers between devices: 5.19 us -> none  [body(): lax.all_to_all(feats, 'seq', split_axis=1, concat_axis=0, tiled=True)]
    reduce_sum x2 -> x0, other arithmetic: 4.2 us -> none  [the longest x1 2.27 us: prepare(): query = query * lax.rsqrt(jnp.sum(query * query, -1, keepdims=True) + 1e-06)]
  transfers between devices with their start and end apart: 3 -> 0, of which waited for: 3 -> 0; matrix products, arithmetic and copies ran while one was open for 2% -> 0% of each run, Pallas kernels for 0% -> 0%
where the time goes in v1:
time: 114 us
  Pallas kernels  93.4 us (82%)
  blocking collectives  14.1 us (12%)
  matrix products  4.57 us (4%)
  local copies, waits for them, and re-layouts  2.22 us (2%)
    pallas_call x1, Pallas kernels, delta_layer(): pl.pallas_call(delta_kernel, out_shape=jax.ShapeDtypeStruct((frames, HEAD...  93.4 us
    all_gather x1, blocking collectives, body(): full = lax.all_gather(feats, 'seq', axis=0, tiled=True)  14.1 us
    dot_general x1, matrix products, body(): lax.dot_general(full, qkv_weight, (((0,), (0,)), ((), ())), preferred_ele...  3.46 us

profile of v1, /device:TPU:0, one launch (start us, length us, event | category | flops | bytes accessed | tf_op | source)
XLA Modules:
  0.0 114.3 jit_solution(18100373942093956274)
XLA Ops:
  0.0 0.0 copy-start
  0.0 14.1 %all_gather.3 = bf16[768,512]{1,0:T(8,128)(2,1)S(1)} all-gather(bf16[192,512]{1,0:T(8,128)(2,1)} %param.5), channel_id=1, replica_groups=mesh['seq'=4,'batch'=8] {'seq'}, dimensions={0}, use_global_device_ids=true | all-gather | bytes 983040 | tf_op jit(solution)/shard_map/all_gather | solution.py:99
  14.1 0.0 copy-done
  14.1 0.0 copy-start.2
  14.1 0.0 copy-start.3
  14.1 0.0 copy-start.1
  14.1 3.5 %convolution_convert_fusion.qkv_ref = bf16[512,2304]{1,0:T(8,128)(2,1)} fusion(bf16[768,512]{1,0:T(8,128)(2,1)S(1)} %all_gather.3, bf16[768,2304]{1,0:T(8,128)(2,1)S(1)} %copy-done), kind=kOutput, calls=%fused_computation | convolution fusion | flops 1813118976 | bytes 6684672 | tf_op jit(solution)/shard_map/dot_general | solution.py:100
  17.6 0.0 copy-done.2
  17.6 0.0 copy-done.3
  17.6 1.1 fusion.3.beta_ref
  18.7 0.0 copy-done.1
  18.7 0.6 reshape.4.gain_ref
  19.3 93.4 %shard_map.55 = bf16[512,768]{1,0:T(8,128)(2,1)} custom-call(bf16[512,2304]{1,0:T(8,128)(2,1)} %convolution_convert_fusion.qkv_ref, f32[512,6]{1,0:T(8,128)} %fusion.3.beta_ref, f32[1,768]{1,0:T(1,128)} %reshape.4.gain_ref), custom_call_target="tpu_custom_call" | custom-call | tf_op jit(solution)/shard_map/pallas_call | solution.py:85
  112.7 1.6 %constant_dynamic-slice_fusion = bf16[128,768]{1,0:T(8,128)(2,1)} fusion(bf16[512,768]{1,0:T(8,128)(2,1)} %shard_map.55, s32[]{:T(128)S(6)} %select_n.3), kind=kLoop, calls=%fused_computation.6 | loop fusion | bytes 393220 | tf_op jit(solution)/shard_map/dynamic_slice | solution.py:111
Async XLA Ops:
  0.0 14.1 %copy-start = (bf16[768,2304]{1,0:T(8,128)(2,1)S(1)}, bf16[768,2304]{1,0:T(8,128)(2,1)}, u32[]{:S(2)}) copy-start(bf16[768,2304]{1,0:T(8,128)(2,1)} %param.6) | copy-start | bytes 10616836
  14.1 3.5 %copy-start.2 = (bf16[768,6]{0,1:T(8,128)(2,1)S(1)}, bf16[768,6]{0,1:T(8,128)(2,1)}, u32[]{:S(2)}) copy-start(bf16[768,6]{0,1:T(8,128)(2,1)} %param.7) | copy-start | bytes 27652
  14.1 3.5 %copy-start.3 = (f32[6]{0:T(128)S(1)}, f32[6]{0:T(128)}, u32[]{:S(2)}) copy-start(f32[6]{0:T(128)} %param.8) | copy-start | bytes 76
  14.1 4.6 %copy-start.1 = (f32[768]{0:T(1024)S(1)}, f32[768]{0:T(1024)}, u32[]{:S(2)}) copy-start(f32[768]{0:T(1024)} %param.9) | copy-start | bytes 9220

commit v2 on v1

--- a/solution.py
+++ b/solution.py
@@ -11,26 +11,26 @@
 HD = 128
 GROUP = 64
 
-HIGHEST_ACCURACY = lax.Precision.HIGHEST
+MATMUL_PRECISION = lax.Precision.HIGH
 
 
 def mm(a, b):
     return lax.dot_general(
-        a, b, (((1,), (0,)), ((), ())), precision=HIGHEST_ACCURACY,
+        a, b, (((1,), (0,)), ((), ())), precision=MATMUL_PRECISION,
         preferred_element_type=jnp.float32,
     )
 
 
 def mm_nt(a, b):
     return lax.dot_general(
-        a, b, (((1,), (1,)), ((), ())), precision=HIGHEST_ACCURACY,
+        a, b, (((1,), (1,)), ((), ())), precision=MATMUL_PRECISION,
         preferred_element_type=jnp.float32,
     )
 
 
 def mm_tn(a, b):
     return lax.dot_general(
-        a, b, (((0,), (0,)), ((), ())), precision=HIGHEST_ACCURACY,
+        a, b, (((0,), (0,)), ((), ())), precision=MATMUL_PRECISION,
         preferred_element_type=jnp.float32,
     )
 

time: 114 us -> 94.4 us (0.83)
  Pallas kernels: 93.4 us -> 73.4 us
    pallas_call x1, Pallas kernels: 93.4 us -> 73.4 us  [delta_layer(): pl.pallas_call(delta_kernel, out_shape=jax.ShapeDtypeStruct((frames, HEAD...]
where the time goes in v2:
time: 94.4 us; the launch traced here: 94.2 us
  Pallas kernels  73.4 us (78%)
  blocking collectives  14.1 us (15%)
  matrix products  4.57 us (5%)
  local copies, waits for them, and re-layouts  2.22 us (2%)
    pallas_call x1, Pallas kernels, delta_layer(): pl.pallas_call(delta_kernel, out_shape=jax.ShapeDtypeStruct((frames, HEAD...  73.4 us
    all_gather x1, blocking collectives, body(): full = lax.all_gather(feats, 'seq', axis=0, tiled=True)  14.1 us
    dot_general x1, matrix products, body(): lax.dot_general(full, qkv_weight, (((0,), (0,)), ((), ())), preferred_ele...  3.46 us

profile of v2, /device:TPU:0, one launch (start us, length us, event | category | flops | bytes accessed | tf_op | source)
XLA Modules:
  0.0 94.2 jit_solution(7244943166627000448)
XLA Ops:
  0.0 0.0 copy-start
  0.0 14.1 %all_gather.3 = bf16[768,512]{1,0:T(8,128)(2,1)S(1)} all-gather(bf16[192,512]{1,0:T(8,128)(2,1)} %param.5), channel_id=1, replica_groups=mesh['seq'=4,'batch'=8] {'seq'}, dimensions={0}, use_global_device_ids=true | all-gather | bytes 983040 | tf_op jit(solution)/shard_map/all_gather | solution.py:99
  14.1 0.0 copy-done
  14.1 0.0 copy-start.2
  14.1 0.0 copy-start.3
  14.1 0.0 copy-start.1
  14.1 3.5 %convolution_convert_fusion.qkv_ref = bf16[512,2304]{1,0:T(8,128)(2,1)} fusion(bf16[768,512]{1,0:T(8,128)(2,1)S(1)} %all_gather.3, bf16[768,2304]{1,0:T(8,128)(2,1)S(1)} %copy-done), kind=kOutput, calls=%fused_computation | convolution fusion | flops 1813118976 | bytes 6684672 | tf_op jit(solution)/shard_map/dot_general | solution.py:100
  17.6 0.0 copy-done.2
  17.6 0.0 copy-done.3
  17.6 1.1 %fusion.3.beta_ref = f32[512,6]{1,0:T(8,128)} fusion(bf16[768,512]{1,0:T(8,128)(2,1)S(1)} %all_gather.3, bf16[768,6]{0,1:T(8,128)(2,1)S(1)} %copy-done.2, f32[6]{0:T(128)S(1)} %copy-done.3), kind=kOutput, calls=%fused_computation.5 | convolution fusion | flops 4730880 | bytes 807960 | tf_op jit(solution)/shard_map/dot_general | solution.py:103
  18.7 0.0 copy-done.1
  18.7 0.6 reshape.4.gain_ref
  19.3 73.4 %shard_map.55 = bf16[512,768]{1,0:T(8,128)(2,1)} custom-call(bf16[512,2304]{1,0:T(8,128)(2,1)} %convolution_convert_fusion.qkv_ref, f32[512,6]{1,0:T(8,128)} %fusion.3.beta_ref, f32[1,768]{1,0:T(1,128)} %reshape.4.gain_ref), custom_call_target="tpu_custom_call" | custom-call | tf_op jit(solution)/shard_map/pallas_call | solution.py:85
  92.6 1.6 %constant_dynamic-slice_fusion = bf16[128,768]{1,0:T(8,128)(2,1)} fusion(bf16[512,768]{1,0:T(8,128)(2,1)} %shard_map.55, s32[]{:T(128)S(6)} %select_n.3), kind=kLoop, calls=%fused_computation.6 | loop fusion | bytes 393220 | tf_op jit(solution)/shard_map/dynamic_slice | solution.py:111
Async XLA Ops:
  0.0 14.1 %copy-start = (bf16[768,2304]{1,0:T(8,128)(2,1)S(1)}, bf16[768,2304]{1,0:T(8,128)(2,1)}, u32[]{:S(2)}) copy-start(bf16[768,2304]{1,0:T(8,128)(2,1)} %param.6) | copy-start | bytes 10616836
  14.1 3.5 %copy-start.2 = (bf16[768,6]{0,1:T(8,128)(2,1)S(1)}, bf16[768,6]{0,1:T(8,128)(2,1)}, u32[]{:S(2)}) copy-start(bf16[768,6]{0,1:T(8,128)(2,1)} %param.7) | copy-start | bytes 27652
  14.1 3.5 %copy-start.3 = (f32[6]{0:T(128)S(1)}, f32[6]{0:T(128)}, u32[]{:S(2)}) copy-start(f32[6]{0:T(128)} %param.8) | copy-start | bytes 76
  14.1 4.6 %copy-start.1 = (f32[768]{0:T(1024)S(1)}, f32[768]{0:T(1024)}, u32[]{:S(2)}) copy-start(f32[768]{0:T(1024)} %param.9) | copy-start | bytes 9220

commit v3 on v2

--- a/solution.py
+++ b/solution.py
@@ -39,37 +39,59 @@
     return x * lax.rsqrt(jnp.sum(x * x, -1, keepdims=True) + 1e-06)
 
 
-def delta_kernel(qkv_ref, beta_ref, gain_ref, out_ref, state_ref):
+def bmm(a, b):
+    return lax.dot_general(
+        a, b, (((2,), (1,)), ((0,), (0,))), precision=MATMUL_PRECISION,
+        preferred_element_type=jnp.float32,
+    )
+
+
+def bmm_nt(a, b):
+    return lax.dot_general(
+        a, b, (((2,), (2,)), ((0,), (0,))), precision=MATMUL_PRECISION,
+        preferred_element_type=jnp.float32,
+    )
+
+
+def delta_kernel(qkv_ref, beta_ref, gain_ref, out_ref, q_ref, k_ref, w_ref, u_ref, p_ref, state_ref):
     frames = qkv_ref.shape[0]
+    chunks = frames // GROUP
     width = HEADS * HD
-    state_ref[...] = jnp.zeros_like(state_ref)
-    row = lax.broadcasted_iota(jnp.int32, (GROUP, GROUP), 0)
-    col = lax.broadcasted_iota(jnp.int32, (GROUP, GROUP), 1)
+    row = lax.broadcasted_iota(jnp.int32, (chunks, GROUP, GROUP), 1)
+    col = lax.broadcasted_iota(jnp.int32, (chunks, GROUP, GROUP), 2)
     eye = jnp.where(row == col, 1.0, 0.0).astype(jnp.float32)
 
+    for h in range(HEADS):
+        query = unit_normed(qkv_ref[:, pl.ds(h * HD, HD)].astype(jnp.float32))
+        keys = unit_normed(qkv_ref[:, pl.ds(width + h * HD, HD)].astype(jnp.float32))
+        values = qkv_ref[:, pl.ds(2 * width + h * HD, HD)].astype(jnp.float32)
+        rates = beta_ref[:, pl.ds(h, 1)]
+        q_ref[h] = query
+        k_ref[h] = keys
+        query = query.reshape(chunks, GROUP, HD)
+        keys = keys.reshape(chunks, GROUP, HD)
+        weighted = (keys.reshape(frames, HD) * rates).reshape(chunks, GROUP, HD)
+        scaled = (values * rates).reshape(chunks, GROUP, HD)
+        gram = bmm_nt(weighted, keys)
+        negated = jnp.where(row > col, -gram, 0.0)
+        inverse = eye + negated
+        power = negated
+        for level in range(5):
+            power = bmm(power, power)
+            inverse = inverse + bmm(inverse, power)
+        w_ref[h] = bmm(inverse, weighted).reshape(frames, HD)
+        u_ref[h] = bmm(inverse, scaled).reshape(frames, HD)
+        p_ref[h] = jnp.where(row >= col, bmm_nt(query, keys), 0.0).reshape(frames, GROUP)
+
+    state_ref[...] = jnp.zeros_like(state_ref)
+
     def step(c, carry):
-        r0 = pl.multiple_of(c * GROUP, GROUP)
-        rows = pl.ds(r0, GROUP)
+        rows = pl.ds(pl.multiple_of(c * GROUP, GROUP), GROUP)
         for h in range(HEADS):
-            query = unit_normed(qkv_ref[rows, pl.ds(h * HD, HD)].astype(jnp.float32))
-            keys = unit_normed(qkv_ref[rows, pl.ds(width + h * HD, HD)].astype(jnp.float32))
-            values = qkv_ref[rows, pl.ds(2 * width + h * HD, HD)].astype(jnp.float32)
-            rates = beta_ref[rows, pl.ds(h, 1)]
-            weighted = keys * rates
-            gram = mm_nt(weighted, keys)
-            negated = jnp.where(row > col, -gram, 0.0)
-            inverse = eye + negated
-            power = negated
-            for level in range(5):
-                power = mm(power, power)
-                inverse = inverse + mm(inverse, power)
-            wfac = mm(inverse, weighted)
-            ufac = mm(inverse, values * rates)
-            scores = jnp.where(row >= col, mm_nt(query, keys), 0.0)
             state = state_ref[h]
-            residual = ufac - mm(wfac, state)
-            output = mm(query, state) + mm(scores, residual)
-            state_ref[h] = state + mm_tn(keys, residual)
+            residual = u_ref[h, rows, :] - mm(w_ref[h, rows, :], state)
+            state_ref[h] = state + mm_tn(k_ref[h, rows, :], residual)
+            output = mm(q_ref[h, rows, :], state) + mm(p_ref[h, rows, :], residual)
             power_mean = jnp.mean(output * output, -1, keepdims=True) + 1e-06
             gain = gain_ref[:, pl.ds(h * HD, HD)]
             out_ref[rows, pl.ds(h * HD, HD)] = (output * lax.rsqrt(power_mean) * gain).astype(
@@ -77,7 +99,7 @@
             )
         return carry
 
-    lax.fori_loop(0, frames // GROUP, step, 0)
+    lax.fori_loop(0, chunks, step, 0, unroll=chunks <= 8)
 
 
 def delta_layer(qkv, beta, gain):
@@ -91,7 +113,14 @@
             pl.BlockSpec(memory_space=pltpu.VMEM),
         ],
         out_specs=pl.BlockSpec(memory_space=pltpu.VMEM),
-        scratch_shapes=[pltpu.VMEM((HEADS, HD, HD), jnp.float32)],
+        scratch_shapes=[
+            pltpu.VMEM((HEADS, frames, HD), jnp.float32),
+            pltpu.VMEM((HEADS, frames, HD), jnp.float32),
+            pltpu.VMEM((HEADS, frames, HD), jnp.float32),
+            pltpu.VMEM((HEADS, frames, HD), jnp.float32),
+            pltpu.VMEM((HEADS, frames, GROUP), jnp.float32),
+            pltpu.VMEM((HEADS, HD, HD), jnp.float32),
+        ],
     )(qkv, beta, gain)
 
 

time: 94.4 us -> 46.9 us (0.50)
  Pallas kernels: 73.4 us -> 25.8 us
    pallas_call x1, Pallas kernels: 73.4 us -> 25.8 us  [delta_layer(): pl.pallas_call(delta_kernel, out_shape=jax.ShapeDtypeStruct((frames, HEAD...]
where the time goes in v3:
time: 46.9 us; the launch traced here: 46.7 us
  Pallas kernels  25.8 us (55%)
  blocking collectives  14.1 us (30%)
  matrix products  4.57 us (10%)
  local copies, waits for them, and re-layouts  2.22 us (5%)
    pallas_call x1, Pallas kernels, delta_layer(): pl.pallas_call(delta_kernel, out_shape=jax.ShapeDtypeStruct((frames, HEAD...  25.8 us
    all_gather x1, blocking collectives, body(): full = lax.all_gather(feats, 'seq', axis=0, tiled=True)  14.1 us
    dot_general x1, matrix products, body(): lax.dot_general(full, qkv_weight, (((0,), (0,)), ((), ())), preferred_ele...  3.46 us
    dynamic_slice x1, local copies, waits for them, and re-layouts, body(): return lax.dynamic_slice_in_dim(mixed, mine * rows, rows, 0)  1.62 us
    dot_general x1, matrix products, body(): lax.dot_general(full, beta_weight, (((0,), (0,)), ((), ())), preferred_el...  1.11 us

profile of v3, /device:TPU:0, one launch (start us, length us, event | category | flops | bytes accessed | tf_op | source)
XLA Modules:
  0.0 46.7 jit_solution(5014249106247838037)
XLA Ops:
  0.0 0.0 copy-start
  0.0 14.1 %all_gather.3 = bf16[768,512]{1,0:T(8,128)(2,1)S(1)} all-gather(bf16[192,512]{1,0:T(8,128)(2,1)} %param.5), channel_id=1, replica_groups=mesh['seq'=4,'batch'=8] {'seq'}, dimensions={0}, use_global_device_ids=true | all-gather | bytes 983040 | tf_op jit(solution)/shard_map/all_gather | solution.py:128
  14.1 0.0 copy-done
  14.1 0.0 copy-start.2
  14.1 0.0 copy-start.3
  14.1 0.0 copy-start.1
  14.1 3.5 %convolution_convert_fusion.qkv_ref = bf16[512,2304]{1,0:T(8,128)(2,1)} fusion(bf16[768,512]{1,0:T(8,128)(2,1)S(1)} %all_gather.3, bf16[768,2304]{1,0:T(8,128)(2,1)S(1)} %copy-done), kind=kOutput, calls=%fused_computation | convolution fusion | flops 1813118976 | bytes 6684672 | tf_op jit(solution)/shard_map/dot_general | solution.py:129
  17.6 0.0 copy-done.2
  17.6 0.0 copy-done.3
  17.6 1.1 %fusion.3.beta_ref = f32[512,6]{1,0:T(8,128)} fusion(bf16[768,512]{1,0:T(8,128)(2,1)S(1)} %all_gather.3, bf16[768,6]{0,1:T(8,128)(2,1)S(1)} %copy-done.2, f32[6]{0:T(128)S(1)} %copy-done.3), kind=kOutput, calls=%fused_computation.5 | convolution fusion | flops 4730880 | bytes 807960 | tf_op jit(solution)/shard_map/dot_general | solution.py:132
  18.7 0.0 copy-done.1
  18.7 0.6 %reshape.4.gain_ref = f32[1,768]{1,0:T(1,128)} reshape(f32[768]{0:T(1024)S(1)} %copy-done.1) | data formatting | bytes 6144 | tf_op jit(solution)/shard_map/reshape | solution.py:136
  19.3 25.8 %shard_map.55 = bf16[512,768]{1,0:T(8,128)(2,1)} custom-call(bf16[512,2304]{1,0:T(8,128)(2,1)} %convolution_convert_fusion.qkv_ref, f32[512,6]{1,0:T(8,128)} %fusion.3.beta_ref, f32[1,768]{1,0:T(1,128)} %reshape.4.gain_ref), custom_call_target="tpu_custom_call" | custom-call | tf_op jit(solution)/shard_map/pallas_call | solution.py:107
  45.1 1.6 %constant_dynamic-slice_fusion = bf16[128,768]{1,0:T(8,128)(2,1)} fusion(bf16[512,768]{1,0:T(8,128)(2,1)} %shard_map.55, s32[]{:T(128)S(6)} %select_n.3), kind=kLoop, calls=%fused_computation.6 | loop fusion | bytes 393220 | tf_op jit(solution)/shard_map/dynamic_slice | solution.py:140
Async XLA Ops:
  0.0 14.1 %copy-start = (bf16[768,2304]{1,0:T(8,128)(2,1)S(1)}, bf16[768,2304]{1,0:T(8,128)(2,1)}, u32[]{:S(2)}) copy-start(bf16[768,2304]{1,0:T(8,128)(2,1)} %param.6) | copy-start | bytes 10616836
  14.1 3.5 %copy-start.2 = (bf16[768,6]{0,1:T(8,128)(2,1)S(1)}, bf16[768,6]{0,1:T(8,128)(2,1)}, u32[]{:S(2)}) copy-start(bf16[768,6]{0,1:T(8,128)(2,1)} %param.7) | copy-start | bytes 27652
  14.1 3.5 %copy-start.3 = (f32[6]{0:T(128)S(1)}, f32[6]{0:T(128)}, u32[]{:S(2)}) copy-start(f32[6]{0:T(128)} %param.8) | copy-start | bytes 76
  14.1 4.6 %copy-start.1 = (f32[768]{0:T(1024)S(1)}, f32[768]{0:T(1024)}, u32[]{:S(2)}) copy-start(f32[768]{0:T(1024)} %param.9) | copy-start | bytes 9220

commit v4 on v3

--- a/solution.py
+++ b/solution.py
@@ -56,12 +56,13 @@
 def delta_kernel(qkv_ref, beta_ref, gain_ref, out_ref, q_ref, k_ref, w_ref, u_ref, p_ref, state_ref):
     frames = qkv_ref.shape[0]
     chunks = frames // GROUP
-    width = HEADS * HD
+    heads = beta_ref.shape[1]
+    width = heads * HD
     row = lax.broadcasted_iota(jnp.int32, (chunks, GROUP, GROUP), 1)
     col = lax.broadcasted_iota(jnp.int32, (chunks, GROUP, GROUP), 2)
     eye = jnp.where(row == col, 1.0, 0.0).astype(jnp.float32)
 
-    for h in range(HEADS):
+    for h in range(heads):
         query = unit_normed(qkv_ref[:, pl.ds(h * HD, HD)].astype(jnp.float32))
         keys = unit_normed(qkv_ref[:, pl.ds(width + h * HD, HD)].astype(jnp.float32))
         values = qkv_ref[:, pl.ds(2 * width + h * HD, HD)].astype(jnp.float32)
@@ -87,7 +88,7 @@
 
     def step(c, carry):
         rows = pl.ds(pl.multiple_of(c * GROUP, GROUP), GROUP)
-        for h in range(HEADS):
+        for h in range(heads):
             state = state_ref[h]
             residual = u_ref[h, rows, :] - mm(w_ref[h, rows, :], state)
             state_ref[h] = state + mm_tn(k_ref[h, rows, :], residual)
@@ -103,10 +104,10 @@
 
 
 def delta_layer(qkv, beta, gain):
-    frames = qkv.shape[0]
+    frames, heads = beta.shape
     return pl.pallas_call(
         delta_kernel,
-        out_shape=jax.ShapeDtypeStruct((frames, HEADS * HD), jnp.bfloat16),
+        out_shape=jax.ShapeDtypeStruct((frames, heads * HD), jnp.bfloat16),
         in_specs=[
             pl.BlockSpec(memory_space=pltpu.VMEM),
             pl.BlockSpec(memory_space=pltpu.VMEM),
@@ -114,30 +115,41 @@
         ],
         out_specs=pl.BlockSpec(memory_space=pltpu.VMEM),
         scratch_shapes=[
-            pltpu.VMEM((HEADS, frames, HD), jnp.float32),
-            pltpu.VMEM((HEADS, frames, HD), jnp.float32),
-            pltpu.VMEM((HEADS, frames, HD), jnp.float32),
-            pltpu.VMEM((HEADS, frames, HD), jnp.float32),
-            pltpu.VMEM((HEADS, frames, GROUP), jnp.float32),
-            pltpu.VMEM((HEADS, HD, HD), jnp.float32),
+            pltpu.VMEM((heads, frames, HD), jnp.float32),
+            pltpu.VMEM((heads, frames, HD), jnp.float32),
+            pltpu.VMEM((heads, frames, HD), jnp.float32),
+            pltpu.VMEM((heads, frames, HD), jnp.float32),
+            pltpu.VMEM((heads, frames, GROUP), jnp.float32),
+            pltpu.VMEM((heads, HD, HD), jnp.float32),
         ],
     )(qkv, beta, gain)
 
 
 def body(feats, qkv_weight, beta_weight, beta_bias, out_gain):
+    count = lax.axis_size("seq")
+    mine = lax.axis_index("seq")
+    slots = -(-HEADS // count)
+    heads = jnp.minimum(mine + count * jnp.arange(slots), HEADS - 1)
     full = lax.all_gather(feats, "seq", axis=0, tiled=True)
+    channels = qkv_weight.shape[0]
+    picked = jnp.take(qkv_weight.reshape(channels, 3, HEADS, HD), heads, axis=2)
     qkv = lax.dot_general(
-        full, qkv_weight, (((0,), (0,)), ((), ())), preferred_element_type=jnp.float32
+        full, picked.reshape(channels, 3 * slots * HD), (((0,), (0,)), ((), ())),
+        preferred_element_type=jnp.float32,
     ).astype(jnp.bfloat16)
     logits = lax.dot_general(
         full, beta_weight, (((0,), (0,)), ((), ())), preferred_element_type=jnp.float32
     )
-    beta = jax.nn.sigmoid(logits + beta_bias)
-    mixed = delta_layer(qkv, beta, out_gain.reshape(1, -1))
-    count = lax.axis_size("seq")
-    mine = lax.axis_index("seq")
-    rows = mixed.shape[0] // count
-    return lax.dynamic_slice_in_dim(mixed, mine * rows, rows, 0)
+    beta = jnp.take(jax.nn.sigmoid(logits + beta_bias), heads, axis=1)
+    gain = jnp.take(out_gain.reshape(HEADS, HD), heads, axis=0).reshape(1, slots * HD)
+    mixed = delta_layer(qkv, beta, gain)
+    frames = mixed.shape[0]
+    rows = frames // count
+    parts = lax.all_to_all(
+        mixed.reshape(count, rows, slots * HD), "seq", split_axis=0, concat_axis=0, tiled=True
+    )
+    ordered = parts.reshape(count, rows, slots, HD).transpose(1, 2, 0, 3)
+    return ordered.reshape(rows, slots * count, HD)[:, :HEADS].reshape(rows, HEADS * HD)
 
 
 def solution(mesh):

time: 46.9 us -> 51.1 us (1.090)
  Pallas kernels: 25.8 us -> 9.85 us
  local copies, waits for them, and re-layouts: 2.22 us -> 15 us
  blocking collectives: 14.1 us -> 21.8 us
  matrix products: 4.57 us -> 1.95 us
  other arithmetic: 0 us -> 2.14 us
    pallas_call x1, Pallas kernels: 25.8 us -> 9.85 us  [delta_layer(): pl.pallas_call(delta_kernel, out_shape=jax.ShapeDtypeStruct((frames, head...]
    all_to_all x0 -> x1, blocking collectives: none -> 9.1 us  [body(): lax.all_to_all(mixed.reshape(count, rows, slots * HD), 'seq', split_axis=...]
    unnamed x8 -> x9, local copies, waits for them, and re-layouts: 0.02 us -> 4.76 us
    gather x0 -> x4, local copies, waits for them, and re-layouts: none -> 4.5 us  [the longest x2 3.38 us: body(): picked = jnp.take(qkv_weight.reshape(channels, 3, HEADS, HD), heads, axis=2)]
    reshape x1 -> x4, local copies, waits for them, and re-layouts: 0.58 us -> 4.73 us  [the longest x1 3.64 us: body(): picked = jnp.take(qkv_weight.reshape(channels, 3, HEADS, HD), heads, axis=2)]
    dot_general x1, matrix products: 3.46 us -> 1.73 us  [body(): lax.dot_general(full, picked.reshape(channels, 3 * slots * HD), (((0,), (...]
    dynamic_slice x1 -> x0, local copies, waits for them, and re-layouts: 1.62 us -> none  [body(): return lax.dynamic_slice_in_dim(mixed, mine * rows, rows, 0)]
    select_n x0 -> x4, other arithmetic: none -> 1.47 us  [the longest x2 0.76 us: body(): picked = jnp.take(qkv_weight.reshape(channels, 3, HEADS, HD), heads, axis=2)]
where the time goes in v4:
time: 51.1 us; the launch traced here: 50.7 us
  blocking collectives  21.8 us (43%)
  local copies, waits for them, and re-layouts  15 us (29%)
  Pallas kernels  9.85 us (19%)
  other arithmetic  2.14 us (4%)
  matrix products  1.95 us (4%)
    all_gather x1, blocking collectives, body(): full = lax.all_gather(feats, 'seq', axis=0, tiled=True)  12.7 us
    pallas_call x1, Pallas kernels, delta_layer(): pl.pallas_call(delta_kernel, out_shape=jax.ShapeDtypeStruct((frames, head...  9.85 us
    all_to_all x1, blocking collectives, body(): lax.all_to_all(mixed.reshape(count, rows, slots * HD), 'seq', split_axis=...  9.1 us
    unnamed x9, local copies, waits for them, and re-layouts  4.76 us
    reshape x1, local copies, waits for them, and re-layouts, body(): picked = jnp.take(qkv_weight.reshape(channels, 3, HEADS, HD), heads, axis=2)  3.64 us
    gather x2, local copies, waits for them, and re-layouts, body(): picked = jnp.take(qkv_weight.reshape(channels, 3, HEADS, HD), heads, axis=2)  3.38 us
    dot_general x1, matrix products, body(): lax.dot_general(full, picked.reshape(channels, 3 * slots * HD), (((0,), (...  1.73 us

profile of v4, /device:TPU:0, one launch (start us, length us, event | category | flops | bytes accessed | tf_op | source)
XLA Modules:
  0.0 50.7 jit_solution(16222441919067024731)
XLA Ops:
  0.0 0.0 copy-start
  0.0 0.5 %fusion.5 = s32[2]{0:T(128)} fusion(s32[]{:T(128)S(6)} %axis_index.15), kind=kLoop, calls=%fused_computation.17 | loop fusion | flops 12 | bytes 12 | tf_op jit(solution)/shard_map/jit(_take)/jit(_where)/select_n | solution.py:135
  0.5 4.5 %copy.28 = bf16[768,2304]{0,1:T(8,128)(2,1)S(1)} copy(bf16[768,2304]{1,0:T(8,128)(2,1)} %param.6) | data formatting | bytes 7077888 | tf_op args[1]
  5.1 3.6 %copy.29 = bf16[768,3,6,128]{3,0,2,1:T(8,128)(2,1)} copy(bf16[768,3,6,128]{0,3,2,1:T(8,128)(2,1)S(1)} %bitcast.20) | data formatting | bytes 7077888 | tf_op jit(solution)/shard_map/reshape | solution.py:135
  8.7 0.7 %pad_clamp_fusion = s32[1024]{0:T(1024)S(1)} fusion(s32[2]{0:T(128)} %fusion.5), kind=kLoop, calls=%fused_computation.11 | loop fusion | flops 1024 | bytes 4104 | tf_op jit(solution)/shard_map/jit(_take)/gather | solution.py:135
  9.4 2.8 %gather_fusion = bf16[2,768,3,128]{3,1,2,0:T(8,128)(2,1)S(1)} fusion(bf16[768,3,6,128]{3,0,2,1:T(8,128)(2,1)} %copy.29, s32[1024]{0:T(1024)S(1)} %pad_clamp_fusion), kind=kCustom, calls=%fused_computation | custom fusion | bytes 2359304 | tf_op jit(solution)/shard_map/jit(_take)/gather | solution.py:135
  12.1 0.0 copy-start.1
  12.2 0.6 %copy.30 = bf16[768,3,2,128]{0,3,2,1:T(8,128)(2,1)S(1)} copy(bf16[768,3,2,128]{3,0,1,2:T(8,128)(2,1)S(1)} %bitcast.21) | data formatting | bytes 2359296 | tf_op jit(solution)/shard_map/jit(_take)/gather | solution.py:135
  12.8 0.1 broadcast_in_dim.35
  12.9 0.2 copy-done.1
  13.1 12.7 %all_gather.3 = bf16[768,512]{1,0:T(8,128)(2,1)S(1)} all-gather(bf16[192,512]{1,0:T(8,128)(2,1)S(1)} %copy-done.1), channel_id=1, replica_groups=mesh['seq'=4,'batch'=8] {'seq'}, dimensions={0}, use_global_device_ids=true | all-gather | bytes 983040 | tf_op jit(solution)/shard_map/all_gather | solution.py:133
  25.7 0.2 bitcast_select_fusion
  26.0 0.0 copy-start.3
  26.0 1.7 %fusion.qkv_ref = bf16[512,768]{1,0:T(8,128)(2,1)} fusion(bf16[768,768]{0,1:T(8,128)(2,1)S(1)} %bitcast_select_fusion, bf16[768,512]{1,0:T(8,128)(2,1)S(1)} %all_gather.3), kind=kOutput, calls=%fused_computation.4 | convolution fusion | flops 604372992 | bytes 2752512 | tf_op jit(solution)/shard_map/dot_general | solution.py:136
  27.7 0.0 copy-done
  27.7 0.0 copy-done.3
  27.7 0.2 fusion.4
  28.0 0.0 copy-start.2
  28.0 0.6 %gather_fusion.1 = f32[2,512]{1,0:T(2,128)S(1)} fusion(f32[512,6]{0,1:T(8,128)S(1)} %fusion.4, s32[1024]{0:T(1024)S(1)} %pad_clamp_fusion), kind=kCustom, calls=%fused_computation.1 | custom fusion | bytes 8200 | tf_op jit(solution)/shard_map/jit(_take)/gather | solution.py:143
  28.5 0.1 broadcast_select_fusion
  28.6 0.9 %copy.32 = f32[2,512]{0,1:T(8,128)} copy(f32[2,512]{1,0:T(2,128)S(1)} %broadcast_select_fusion) | data formatting | bytes 8192 | tf_op jit(solution)/shard_map/jit(_take)/select_n | solution.py:143
  29.5 0.0 copy-done.2
  29.5 0.6 %gather_fusion.2 = f32[2,128]{1,0:T(2,128)S(1)} fusion(f32[6,128]{1,0:T(8,128)S(1)} %bitcast.26, s32[1024]{0:T(1024)S(1)} %pad_clamp_fusion), kind=kCustom, calls=%fused_computation.2 | custom fusion | bytes 2056 | tf_op jit(solution)/shard_map/jit(_take)/gather | solution.py:144
  30.0 0.6 %broadcast_select_fusion.1 = f32[2,128]{1,0:T(2,128)} fusion(f32[2,128]{1,0:T(2,128)S(1)} %gather_fusion.2, pred[2]{0:T(512)(128)(4,1)S(1)} %compare_and_fusion), kind=kLoop, calls=%fused_computation.16 | loop fusion | flops 256 | bytes 2050 | tf_op jit(solution)/shard_map/jit(_take)/select_n | solution.py:144
  30.7 9.9 %shard_map.55 = bf16[512,256]{1,0:T(8,128)(2,1)} custom-call(bf16[512,768]{1,0:T(8,128)(2,1)} %fusion.qkv_ref, f32[512,2]{1,0:T(8,128)} %bitcast.22, f32[1,256]{1,0:T(1,128)} %bitcast.27), custom_call_target="tpu_custom_call" | custom-call | tf_op jit(solution)/shard_map/pallas_call | solution.py:108
  40.5 9.1 %all_to_all.5 = bf16[4,128,256]{2,1,0:T(8,128)(2,1)S(1)} all-to-all(bf16[4,128,256]{2,1,0:T(8,128)(2,1)} %bitcast.23), channel_id=1, replica_groups=mesh['seq'=4,'batch'=8] {'seq'}, dimensions={0} | all-to-all | bytes 524288 | tf_op jit(solution)/shard_map/all_to_all | solution.py:148
  49.6 0.1 reshape.74
  49.7 0.2 copy.33
  49.9 0.8 %copy.34 = bf16[128,768]{1,0:T(8,128)(2,1)} copy(bf16[128,768]{0,1:T(8,128)(2,1)S(1)} %bitcast.25) | data formatting | bytes 393216 | tf_op jit(solution)/shard_map/reshape | solution.py:152
  (3 shorter events, 0.0 us)
Async XLA Ops:
  0.0 27.7 %copy-start = (bf16[768,6]{0,1:T(8,128)(2,1)S(1)}, bf16[768,6]{0,1:T(8,128)(2,1)}, u32[]{:S(2)}) copy-start(bf16[768,6]{0,1:T(8,128)(2,1)} %param.7) | copy-start | bytes 27652
  12.1 0.9 %copy-start.1 = (bf16[192,512]{1,0:T(8,128)(2,1)S(1)}, bf16[192,512]{1,0:T(8,128)(2,1)}, u32[]{:S(2)}) copy-start(bf16[192,512]{1,0:T(8,128)(2,1)} %param.5) | copy-start | bytes 589828
  26.0 1.8 %copy-start.3 = (f32[6]{0:T(128)S(1)}, f32[6]{0:T(128)}, u32[]{:S(2)}) copy-start(f32[6]{0:T(128)} %param.8) | copy-start | bytes 76
  28.0 1.5 %copy-start.2 = (f32[768]{0:T(1024)S(1)}, f32[768]{0:T(1024)}, u32[]{:S(2)}) copy-start(f32[768]{0:T(1024)} %param.9) | copy-start | bytes 9220

commit v5 on v4

--- a/solution.py
+++ b/solution.py
@@ -131,11 +131,16 @@
     slots = -(-HEADS // count)
     heads = jnp.minimum(mine + count * jnp.arange(slots), HEADS - 1)
     full = lax.all_gather(feats, "seq", axis=0, tiled=True)
-    channels = qkv_weight.shape[0]
-    picked = jnp.take(qkv_weight.reshape(channels, 3, HEADS, HD), heads, axis=2)
+    picked = jnp.concatenate(
+        [
+            lax.dynamic_slice_in_dim(qkv_weight, (part * HEADS + heads[j]) * HD, HD, axis=1)
+            for part in range(3)
+            for j in range(slots)
+        ],
+        axis=1,
+    )
     qkv = lax.dot_general(
-        full, picked.reshape(channels, 3 * slots * HD), (((0,), (0,)), ((), ())),
-        preferred_element_type=jnp.float32,
+        full, picked, (((0,), (0,)), ((), ())), preferred_element_type=jnp.float32
     ).astype(jnp.bfloat16)
     logits = lax.dot_general(
         full, beta_weight, (((0,), (0,)), ((), ())), preferred_element_type=jnp.float32

time: 51.1 us -> 49.2 us (0.963)
  local copies, waits for them, and re-layouts: 15 us -> 9.55 us
  between operations: 0.09 us -> 3.76 us
  other arithmetic: 2.14 us -> 0.74 us
  blocking collectives: 21.8 us -> 22.9 us
    reshape x1 -> x0, local copies, waits for them, and re-layouts: 3.64 us -> none  [body(): picked = jnp.take(qkv_weight.reshape(channels, 3, HEADS, HD), heads, axis=2)]
    gather x2 -> x0, local copies, waits for them, and re-layouts: 3.38 us -> none  [body(): picked = jnp.take(qkv_weight.reshape(channels, 3, HEADS, HD), heads, axis=2)]
    all_gather x1, blocking collectives: 12.7 us -> 13.8 us  [body(): full = lax.all_gather(feats, 'seq', axis=0, tiled=True)]
    concatenate x0 -> x1, local copies, waits for them, and re-layouts: none -> 0.98 us  [body(): jnp.concatenate([lax.dynamic_slice_in_dim(qkv_weight, (part * HEADS + hea...]
    select_n x2 -> x0, other arithmetic: 0.76 us -> none  [body(): picked = jnp.take(qkv_weight.reshape(channels, 3, HEADS, HD), heads, axis=2)]
    gather x1, other arithmetic: 0.66 us -> 0.01 us  [body(): beta = jnp.take(jax.nn.sigmoid(logits + beta_bias), heads, axis=1)]
    slice x0 -> x1, local copies, waits for them, and re-layouts: none -> 0.59 us  [body(): heads[j]]
    unnamed x9 -> x11, local copies, waits for them, and re-layouts: 4.76 us -> 4.9 us
where the time goes in v5:
time: 49.2 us; the launch traced here: 48.8 us
  blocking collectives  22.9 us (47%)
  Pallas kernels  9.85 us (20%)
  local copies, waits for them, and re-layouts  9.55 us (19%)
  between operations  3.76 us (8%)
  matrix products  1.95 us (4%)
  other arithmetic  0.74 us (2%)
    all_gather x1, blocking collectives, body(): full = lax.all_gather(feats, 'seq', axis=0, tiled=True)  13.8 us
    pallas_call x1, Pallas kernels, delta_layer(): pl.pallas_call(delta_kernel, out_shape=jax.ShapeDtypeStruct((frames, head...  9.85 us
    all_to_all x1, blocking collectives, body(): lax.all_to_all(mixed.reshape(count, rows, slots * HD), 'seq', split_axis=...  9.1 us
    unnamed x11, local copies, waits for them, and re-layouts  4.9 us
    dot_general x1, matrix products, body(): lax.dot_general(full, picked, (((0,), (0,)), ((), ())), preferred_element...  1.73 us

profile of v5, /device:TPU:0, one launch (start us, length us, event | category | flops | bytes accessed | tf_op | source)
XLA Modules:
  0.0 48.8 jit_solution(783814470048787458)
XLA Ops:
  0.0 0.0 copy-start
  0.0 0.6 %fusion.6 = (s32[1]{0:T(128)}, s32[1]{0:T(128)}) fusion(s32[2]{0:T(128)S(1)} %add_minimum_fusion), kind=kLoop, calls=%fused_computation.23 | loop fusion | bytes 16 | tf_op jit(solution)/shard_map/slice | solution.py:136
  4.3 13.8 %all_gather.3 = bf16[768,512]{1,0:T(8,128)(2,1)S(1)} all-gather(bf16[192,512]{1,0:T(8,128)(2,1)} %param.5), channel_id=1, replica_groups=mesh['seq'=4,'batch'=8] {'seq'}, dimensions={0}, use_global_device_ids=true | all-gather | bytes 983040 | tf_op jit(solution)/shard_map/all_gather | solution.py:133
  18.1 1.0 %dynamic-slice_dynamic-update-slice_fusion.5 = bf16[768,768]{1,0:T(8,128)(2,1)S(1)} fusion(bf16[768,2304]{1,0:T(8,128)(2,1)} %param.6, s32[]{:T(128)S(6)} %select_n.54), kind=kLoop, calls=%fused_computation.14 | loop fusion | bytes 393220
  19.1 1.0 %dynamic-slice_dynamic-update-slice_fusion.4 = bf16[768,768]{1,0:T(8,128)(2,1)S(1)} fusion(bf16[768,768]{1,0:T(8,128)(2,1)S(1)} %dynamic-slice_dynamic-update-slice_fusion.5, bf16[768,2304]{1,0:T(8,128)(2,1)} %param.6, s32[]{:T(128)S(6)} %select_n.55), kind=kLoop, calls=%fused_computation.13 | loop fusion | bytes 393220
  20.1 1.0 %dynamic-slice_dynamic-update-slice_fusion.3 = bf16[768,768]{1,0:T(8,128)(2,1)S(1)} fusion(bf16[768,768]{1,0:T(8,128)(2,1)S(1)} %dynamic-slice_dynamic-update-slice_fusion.4, bf16[768,2304]{1,0:T(8,128)(2,1)} %param.6, s32[]{:T(128)S(6)} %select_n.56), kind=kLoop, calls=%fused_computation.12 | loop fusion | bytes 393220
  21.1 1.0 %dynamic-slice_dynamic-update-slice_fusion.2 = bf16[768,768]{1,0:T(8,128)(2,1)S(1)} fusion(bf16[768,768]{1,0:T(8,128)(2,1)S(1)} %dynamic-slice_dynamic-update-slice_fusion.3, bf16[768,2304]{1,0:T(8,128)(2,1)} %param.6, s32[]{:T(128)S(6)} %select_n.57), kind=kLoop, calls=%fused_computation.11 | loop fusion | bytes 393220
  22.0 1.0 %dynamic-slice_dynamic-update-slice_fusion.1 = bf16[768,768]{1,0:T(8,128)(2,1)S(1)} fusion(bf16[768,768]{1,0:T(8,128)(2,1)S(1)} %dynamic-slice_dynamic-update-slice_fusion.2, bf16[768,2304]{1,0:T(8,128)(2,1)} %param.6, s32[]{:T(128)S(6)} %select_n.58), kind=kLoop, calls=%fused_computation.10 | loop fusion | bytes 393220
  23.0 1.0 %dynamic-slice_dynamic-update-slice_fusion = bf16[768,768]{1,0:T(8,128)(2,1)S(1)} fusion(bf16[768,768]{1,0:T(8,128)(2,1)S(1)} %dynamic-slice_dynamic-update-slice_fusion.1, bf16[768,2304]{1,0:T(8,128)(2,1)} %param.6, s32[]{:T(128)S(6)} %select_n.59), kind=kLoop, calls=%fused_computation.9 | loop fusion | bytes 393220 | tf_op jit(solution)/shard_map/concatenate | solution.py:134
  24.0 0.0 copy-start.2
  24.0 1.7 %fusion.qkv_ref = bf16[512,768]{1,0:T(8,128)(2,1)} fusion(bf16[768,768]{1,0:T(8,128)(2,1)S(1)} %dynamic-slice_dynamic-update-slice_fusion, bf16[768,512]{1,0:T(8,128)(2,1)S(1)} %all_gather.3), kind=kOutput, calls=%fused_computation.3 | convolution fusion | flops 604372992 | bytes 2752512 | tf_op jit(solution)/shard_map/dot_general | solution.py:142
  25.8 0.0 copy-done
  25.8 0.0 copy-done.2
  25.8 0.2 fusion.4
  26.0 0.0 copy-start.1
  26.0 0.6 %gather_fusion = f32[2,512]{1,0:T(2,128)S(1)} fusion(f32[512,6]{0,1:T(8,128)S(1)} %fusion.4, s32[1024]{0:T(1024)S(1)} %pad_clamp_fusion), kind=kCustom, calls=%fused_computation | custom fusion | bytes 8200 | tf_op jit(solution)/shard_map/jit(_take)/gather | solution.py:148
  26.6 0.1 broadcast_select_fusion
  26.6 0.9 %copy.18 = f32[2,512]{0,1:T(8,128)} copy(f32[2,512]{1,0:T(2,128)S(1)} %broadcast_select_fusion) | data formatting | bytes 8192 | tf_op jit(solution)/shard_map/jit(_take)/select_n | solution.py:148
  27.5 0.0 copy-done.1
  27.5 0.6 %gather_fusion.1 = f32[2,128]{1,0:T(2,128)S(1)} fusion(f32[6,128]{1,0:T(8,128)S(1)} %bitcast.26, s32[1024]{0:T(1024)S(1)} %pad_clamp_fusion), kind=kCustom, calls=%fused_computation.1 | custom fusion | bytes 2056 | tf_op jit(solution)/shard_map/jit(_take)/gather | solution.py:149
  28.1 0.6 %broadcast_select_fusion.1 = f32[2,128]{1,0:T(2,128)} fusion(f32[2,128]{1,0:T(2,128)S(1)} %gather_fusion.1, pred[2]{0:T(512)(128)(4,1)S(1)} %compare_and_fusion), kind=kLoop, calls=%fused_computation.20 | loop fusion | flops 256 | bytes 2050 | tf_op jit(solution)/shard_map/jit(_take)/select_n | solution.py:149
  28.7 9.9 %shard_map.55 = bf16[512,256]{1,0:T(8,128)(2,1)} custom-call(bf16[512,768]{1,0:T(8,128)(2,1)} %fusion.qkv_ref, f32[512,2]{1,0:T(8,128)} %bitcast.22, f32[1,256]{1,0:T(1,128)} %bitcast.27), custom_call_target="tpu_custom_call" | custom-call | tf_op jit(solution)/shard_map/pallas_call | solution.py:108
  38.5 9.1 %all_to_all.5 = bf16[4,128,256]{2,1,0:T(8,128)(2,1)S(1)} all-to-all(bf16[4,128,256]{2,1,0:T(8,128)(2,1)} %bitcast.23), channel_id=1, replica_groups=mesh['seq'=4,'batch'=8] {'seq'}, dimensions={0} | all-to-all | bytes 524288 | tf_op jit(solution)/shard_map/all_to_all | solution.py:153
  47.6 0.1 reshape.87
  47.7 0.2 copy.19
  47.9 0.8 %copy.20 = bf16[128,768]{1,0:T(8,128)(2,1)} copy(bf16[128,768]{0,1:T(8,128)(2,1)S(1)} %bitcast.25) | data formatting | bytes 393216 | tf_op jit(solution)/shard_map/reshape | solution.py:157
  (5 shorter events, 0.0 us)
Async XLA Ops:
  0.0 25.8 %copy-start = (bf16[768,6]{0,1:T(8,128)(2,1)S(1)}, bf16[768,6]{0,1:T(8,128)(2,1)}, u32[]{:S(2)}) copy-start(bf16[768,6]{0,1:T(8,128)(2,1)} %param.7) | copy-start | bytes 27652
  24.0 1.7 %copy-start.2 = (f32[6]{0:T(128)S(1)}, f32[6]{0:T(128)}, u32[]{:S(2)}) copy-start(f32[6]{0:T(128)} %param.8) | copy-start | bytes 76
  26.0 1.5 %copy-start.1 = (f32[768]{0:T(1024)S(1)}, f32[768]{0:T(1024)}, u32[]{:S(2)}) copy-start(f32[768]{0:T(1024)} %param.9) | copy-start | bytes 9220

commit v6 on v4

--- a/solution.py
+++ b/solution.py
@@ -53,20 +53,34 @@
     )
 
 
-def delta_kernel(qkv_ref, beta_ref, gain_ref, out_ref, q_ref, k_ref, w_ref, u_ref, p_ref, state_ref):
-    frames = qkv_ref.shape[0]
+def delta_kernel(head_ref, feats_ref, *refs):
+    slots = (len(refs) - 10) // 4
+    weight_refs = refs[: 3 * slots]
+    bw_ref, bias_ref = refs[3 * slots], refs[3 * slots + 1]
+    gain_refs = refs[3 * slots + 2 : 4 * slots + 2]
+    out_ref, qkv_ref, q_ref, k_ref, w_ref, u_ref, p_ref, state_ref = refs[4 * slots + 2 :]
+    frames = feats_ref.shape[1]
     chunks = frames // GROUP
-    heads = beta_ref.shape[1]
-    width = heads * HD
+    width = slots * HD
+
+    full = feats_ref[...].T
+    qkv_ref[...] = jnp.dot(
+        full, jnp.concatenate([ref[...] for ref in weight_refs], axis=1),
+        preferred_element_type=jnp.float32,
+    ).astype(qkv_ref.dtype)
+    logits = jnp.dot(full, bw_ref[...], preferred_element_type=jnp.float32) + bias_ref[...]
+    beta_all = 1.0 / (1.0 + jnp.exp(-logits))
+    lane = lax.broadcasted_iota(jnp.int32, beta_all.shape, 1)
+
     row = lax.broadcasted_iota(jnp.int32, (chunks, GROUP, GROUP), 1)
     col = lax.broadcasted_iota(jnp.int32, (chunks, GROUP, GROUP), 2)
     eye = jnp.where(row == col, 1.0, 0.0).astype(jnp.float32)
 
-    for h in range(heads):
+    for h in range(slots):
         query = unit_normed(qkv_ref[:, pl.ds(h * HD, HD)].astype(jnp.float32))
         keys = unit_normed(qkv_ref[:, pl.ds(width + h * HD, HD)].astype(jnp.float32))
         values = qkv_ref[:, pl.ds(2 * width + h * HD, HD)].astype(jnp.float32)
-        rates = beta_ref[:, pl.ds(h, 1)]
+        rates = jnp.sum(jnp.where(lane == head_ref[h], beta_all, 0.0), -1, keepdims=True)
         q_ref[h] = query
         k_ref[h] = keys
         query = query.reshape(chunks, GROUP, HD)
@@ -88,14 +102,13 @@
 
     def step(c, carry):
         rows = pl.ds(pl.multiple_of(c * GROUP, GROUP), GROUP)
-        for h in range(heads):
+        for h in range(slots):
             state = state_ref[h]
             residual = u_ref[h, rows, :] - mm(w_ref[h, rows, :], state)
             state_ref[h] = state + mm_tn(k_ref[h, rows, :], residual)
             output = mm(q_ref[h, rows, :], state) + mm(p_ref[h, rows, :], residual)
             power_mean = jnp.mean(output * output, -1, keepdims=True) + 1e-06
-            gain = gain_ref[:, pl.ds(h * HD, HD)]
-            out_ref[rows, pl.ds(h * HD, HD)] = (output * lax.rsqrt(power_mean) * gain).astype(
+            out_ref[rows, pl.ds(h * HD, HD)] = (output * lax.rsqrt(power_mean) * gain_refs[h][0]).astype(
                 out_ref.dtype
             )
         return carry
@@ -103,46 +116,54 @@
     lax.fori_loop(0, chunks, step, 0, unroll=chunks <= 8)
 
 
-def delta_layer(qkv, beta, gain):
-    frames, heads = beta.shape
+def delta_layer(heads, full, qkv_weight, beta_weight, beta_bias, out_gain):
+    channels, frames = full.shape
+    slots = heads.shape[0]
+    whole = lambda shape: pl.BlockSpec(shape, lambda i, head: (0,) * len(shape))
+    weight_specs = [
+        pl.BlockSpec((channels, HD), lambda i, head, p=p, j=j: (0, p * HEADS + head[j]))
+        for p in range(3)
+        for j in range(slots)
+    ]
+    gain_specs = [
+        pl.BlockSpec((1, 1, HD), lambda i, head, j=j: (head[j], 0, 0)) for j in range(slots)
+    ]
+    grid_spec = pltpu.PrefetchScalarGridSpec(
+        num_scalar_prefetch=1,
+        grid=(1,),
+        in_specs=[whole((channels, frames))]
+        + weight_specs
+        + [whole((channels, HEADS)), whole((1, HEADS))]
+        + gain_specs,
+        out_specs=whole((frames, slots * HD)),
+        scratch_shapes=[
+            pltpu.VMEM((frames, 3 * slots * HD), jnp.bfloat16),
+            pltpu.VMEM((slots, frames, HD), jnp.float32),
+            pltpu.VMEM((slots, frames, HD), jnp.float32),
+            pltpu.VMEM((slots, frames, HD), jnp.float32),
+            pltpu.VMEM((slots, frames, HD), jnp.float32),
+            pltpu.VMEM((slots, frames, GROUP), jnp.float32),
+            pltpu.VMEM((slots, HD, HD), jnp.float32),
+        ],
+    )
+    gains = out_gain.reshape(HEADS, 1, HD)
     return pl.pallas_call(
         delta_kernel,
-        out_shape=jax.ShapeDtypeStruct((frames, heads * HD), jnp.bfloat16),
-        in_specs=[
-            pl.BlockSpec(memory_space=pltpu.VMEM),
-            pl.BlockSpec(memory_space=pltpu.VMEM),
-            pl.BlockSpec(memory_space=pltpu.VMEM),
-        ],
-        out_specs=pl.BlockSpec(memory_space=pltpu.VMEM),
-        scratch_shapes=[
-            pltpu.VMEM((heads, frames, HD), jnp.float32),
-            pltpu.VMEM((heads, frames, HD), jnp.float32),
-            pltpu.VMEM((heads, frames, HD), jnp.float32),
-            pltpu.VMEM((heads, frames, HD), jnp.float32),
-            pltpu.VMEM((heads, frames, GROUP), jnp.float32),
-            pltpu.VMEM((heads, HD, HD), jnp.float32),
-        ],
-    )(qkv, beta, gain)
+        out_shape=jax.ShapeDtypeStruct((frames, slots * HD), jnp.bfloat16),
+        grid_spec=grid_spec,
+    )(
+        heads, full, *([qkv_weight] * (3 * slots)), beta_weight, beta_bias.reshape(1, HEADS),
+        *([gains] * slots),
+    )
 
 
 def body(feats, qkv_weight, beta_weight, beta_bias, out_gain):
     count = lax.axis_size("seq")
     mine = lax.axis_index("seq")
     slots = -(-HEADS // count)
-    heads = jnp.minimum(mine + count * jnp.arange(slots), HEADS - 1)
+    heads = jnp.minimum(mine + count * jnp.arange(slots, dtype=jnp.int32), HEADS - 1)
     full = lax.all_gather(feats, "seq", axis=0, tiled=True)
-    channels = qkv_weight.shape[0]
-    picked = jnp.take(qkv_weight.reshape(channels, 3, HEADS, HD), heads, axis=2)
-    qkv = lax.dot_general(
-        full, picked.reshape(channels, 3 * slots * HD), (((0,), (0,)), ((), ())),
-        preferred_element_type=jnp.float32,
-    ).astype(jnp.bfloat16)
-    logits = lax.dot_general(
-        full, beta_weight, (((0,), (0,)), ((), ())), preferred_element_type=jnp.float32
-    )
-    beta = jnp.take(jax.nn.sigmoid(logits + beta_bias), heads, axis=1)
-    gain = jnp.take(out_gain.reshape(HEADS, HD), heads, axis=0).reshape(1, slots * HD)
-    mixed = delta_layer(qkv, beta, gain)
+    mixed = delta_layer(heads, full, qkv_weight, beta_weight, beta_bias, out_gain)
     frames = mixed.shape[0]
     rows = frames // count
     parts = lax.all_to_all(

time: 51.1 us -> 40.8 us (0.80)
  local copies, waits for them, and re-layouts: 15 us -> 3.93 us
  blocking collectives: 21.8 us -> 24.2 us
  Pallas kernels: 9.85 us -> 11.8 us
  matrix products: 1.95 us -> 0 us
  other arithmetic: 2.14 us -> 0.51 us
    gather x4 -> x0, local copies, waits for them, and re-layouts: 4.5 us -> none  [the longest x2 3.38 us: body(): picked = jnp.take(qkv_weight.reshape(channels, 3, HEADS, HD), heads, axis=2)]
    unnamed x9 -> x1, local copies, waits for them, and re-layouts: 4.76 us -> 1.54 us
    all_gather x1, blocking collectives: 12.7 us -> 15.1 us  [body(): full = lax.all_gather(feats, 'seq', axis=0, tiled=True)]
    reshape x1, local copies, waits for them, and re-layouts: 3.64 us -> 1.28 us  [delta_layer(): gains = out_gain.reshape(HEADS, 1, HD)]
    dot_general x2 -> x0, matrix products: 1.95 us -> none  [the longest x1 1.73 us: body(): lax.dot_general(full, picked.reshape(channels, 3 * slots * HD), (((0,), (...]
    pallas_call x1, Pallas kernels: 9.85 us -> 11.8 us  [delta_layer(): pl.pallas_call(delta_kernel, out_shape=jax.ShapeDtypeStruct((frames, slot...]
    select_n x4 -> x0, other arithmetic: 1.47 us -> none  [the longest x2 0.76 us: body(): picked = jnp.take(qkv_weight.reshape(channels, 3, HEADS, HD), heads, axis=2)]
    select_n x1 -> x0, local copies, waits for them, and re-layouts: 0.85 us -> none  [body(): beta = jnp.take(jax.nn.sigmoid(logits + beta_bias), heads, axis=1)]
where the time goes in v6:
time: 40.8 us; the launch traced here: 40.5 us
  blocking collectives  24.2 us (59%)
  Pallas kernels  11.8 us (29%)
  local copies, waits for them, and re-layouts  3.93 us (10%)
  other arithmetic  0.51 us (1%)
    all_gather x1, blocking collectives, body(): full = lax.all_gather(feats, 'seq', axis=0, tiled=True)  15.1 us
    pallas_call x1, Pallas kernels, delta_layer(): pl.pallas_call(delta_kernel, out_shape=jax.ShapeDtypeStruct((frames, slot...  11.8 us
    all_to_all x1, blocking collectives, body(): lax.all_to_all(mixed.reshape(count, rows, slots * HD), 'seq', split_axis=...  9.1 us
    unnamed x1, local copies, waits for them, and re-layouts  1.54 us
    reshape x1, local copies, waits for them, and re-layouts, delta_layer(): gains = out_gain.reshape(HEADS, 1, HD)  1.28 us
    reshape x1, local copies, waits for them, and re-layouts, body(): ordered.reshape(rows, slots * count, HD)[:, :HEADS]  0.83 us

profile of v6, /device:TPU:0, one launch (start us, length us, event | category | flops | bytes accessed | tf_op | source)
XLA Modules:
  0.0 40.5 jit_solution(2420098277418884266)
XLA Ops:
  0.0 0.5 %add_minimum_fusion.head_ref = s32[2]{0:T(128)} fusion(s32[]{:T(128)S(6)} %axis_index.15), kind=kLoop, calls=%fused_computation | loop fusion | flops 6 | bytes 12 | tf_op jit(solution)/shard_map/min | solution.py:164
  0.5 1.3 %reshape.19.refs_8_.refs_9_ = f32[6,1,128]{2,1,0:T(1,128)} reshape(f32[768]{0:T(1024)} %param.9) | data formatting | bytes 6144 | tf_op jit(solution)/shard_map/reshape | solution.py:149
  1.8 1.5 %copy.8.refs_6_ = bf16[768,6]{1,0:T(8,128)(2,1)} copy(bf16[768,6]{0,1:T(8,128)(2,1)} %param.7) | data formatting | bytes 18432 | tf_op args[2]
  3.3 15.1 %all_gather.3.feats_ref = bf16[768,512]{1,0:T(8,128)(2,1)} all-gather(bf16[192,512]{1,0:T(8,128)(2,1)} %param.5), channel_id=1, replica_groups=mesh['seq'=4,'batch'=8] {'seq'}, dimensions={0}, use_global_device_ids=true | all-gather | bytes 983040 | tf_op jit(solution)/shard_map/all_gather | solution.py:165
  18.5 11.8 %shard_map.55 = bf16[512,256]{1,0:T(8,128)(2,1)} custom-call(s32[2]{0:T(128)} %add_minimum_fusion.head_ref, bf16[768,512]{1,0:T(8,128)(2,1)} %all_gather.3.feats_ref, bf16[768,2304]{1,0:T(8,128)(2,1)} %refs_5_.1, bf16[768,2304]{1,0:T(8,128)(2,1)} %refs_5_.1, bf16[768,2304]{1,0:T(8,128)(2,1)} %refs_5_.1, bf16[768,2304]{1,0:T(8,128)(2,1)} %refs_5_.1, ...), custom_call_target="tpu_custom_call" | custom-call | tf_op jit(solution)/shard_map/pallas_call | solution.py:150
  30.3 9.1 %all_to_all.5 = bf16[4,128,256]{2,1,0:T(8,128)(2,1)S(1)} all-to-all(bf16[4,128,256]{2,1,0:T(8,128)(2,1)} %bitcast.6), channel_id=1, replica_groups=mesh['seq'=4,'batch'=8] {'seq'}, dimensions={0} | all-to-all | bytes 524288 | tf_op jit(solution)/shard_map/all_to_all | solution.py:169
  39.4 0.1 reshape.21
  39.4 0.2 copy.9
  39.7 0.8 %copy.10 = bf16[128,768]{1,0:T(8,128)(2,1)} copy(bf16[128,768]{0,1:T(8,128)(2,1)S(1)} %bitcast.8) | data formatting | bytes 393216 | tf_op jit(solution)/shard_map/reshape | solution.py:173
  (1 shorter events, 0.0 us)

commit v7 on v6

--- a/solution.py
+++ b/solution.py
@@ -68,7 +68,9 @@
         full, jnp.concatenate([ref[...] for ref in weight_refs], axis=1),
         preferred_element_type=jnp.float32,
     ).astype(qkv_ref.dtype)
-    logits = jnp.dot(full, bw_ref[...], preferred_element_type=jnp.float32) + bias_ref[...]
+    logits = lax.dot_general(
+        full, bw_ref[...], (((1,), (1,)), ((), ())), preferred_element_type=jnp.float32
+    ) + bias_ref[...]
     beta_all = 1.0 / (1.0 + jnp.exp(-logits))
     lane = lax.broadcasted_iota(jnp.int32, beta_all.shape, 1)
 
@@ -108,7 +110,7 @@
             state_ref[h] = state + mm_tn(k_ref[h, rows, :], residual)
             output = mm(q_ref[h, rows, :], state) + mm(p_ref[h, rows, :], residual)
             power_mean = jnp.mean(output * output, -1, keepdims=True) + 1e-06
-            out_ref[rows, pl.ds(h * HD, HD)] = (output * lax.rsqrt(power_mean) * gain_refs[h][0]).astype(
+            out_ref[rows, pl.ds(h * HD, HD)] = (output * lax.rsqrt(power_mean) * gain_refs[h][...]).astype(
                 out_ref.dtype
             )
         return carry
@@ -126,14 +128,14 @@
         for j in range(slots)
     ]
     gain_specs = [
-        pl.BlockSpec((1, 1, HD), lambda i, head, j=j: (head[j], 0, 0)) for j in range(slots)
+        pl.BlockSpec((HD,), lambda i, head, j=j: (head[j],)) for j in range(slots)
     ]
     grid_spec = pltpu.PrefetchScalarGridSpec(
         num_scalar_prefetch=1,
         grid=(1,),
         in_specs=[whole((channels, frames))]
         + weight_specs
-        + [whole((channels, HEADS)), whole((1, HEADS))]
+        + [whole((HEADS, channels)), whole((1, HEADS))]
         + gain_specs,
         out_specs=whole((frames, slots * HD)),
         scratch_shapes=[
@@ -146,13 +148,13 @@
             pltpu.VMEM((slots, HD, HD), jnp.float32),
         ],
     )
-    gains = out_gain.reshape(HEADS, 1, HD)
+    gains = out_gain
     return pl.pallas_call(
         delta_kernel,
         out_shape=jax.ShapeDtypeStruct((frames, slots * HD), jnp.bfloat16),
         grid_spec=grid_spec,
     )(
-        heads, full, *([qkv_weight] * (3 * slots)), beta_weight, beta_bias.reshape(1, HEADS),
+        heads, full, *([qkv_weight] * (3 * slots)), beta_weight.T, beta_bias.reshape(1, HEADS),
         *([gains] * slots),
     )
 
@@ -161,16 +163,13 @@
     count = lax.axis_size("seq")
     mine = lax.axis_index("seq")
     slots = -(-HEADS // count)
-    heads = jnp.minimum(mine + count * jnp.arange(slots, dtype=jnp.int32), HEADS - 1)
+    heads = jnp.minimum(mine * slots + jnp.arange(slots, dtype=jnp.int32), HEADS - 1)
     full = lax.all_gather(feats, "seq", axis=0, tiled=True)
     mixed = delta_layer(heads, full, qkv_weight, beta_weight, beta_bias, out_gain)
     frames = mixed.shape[0]
     rows = frames // count
-    parts = lax.all_to_all(
-        mixed.reshape(count, rows, slots * HD), "seq", split_axis=0, concat_axis=0, tiled=True
-    )
-    ordered = parts.reshape(count, rows, slots, HD).transpose(1, 2, 0, 3)
-    return ordered.reshape(rows, slots * count, HD)[:, :HEADS].reshape(rows, HEADS * HD)
+    parts = lax.all_to_all(mixed, "seq", split_axis=0, concat_axis=1, tiled=True)
+    return parts[:, : HEADS * HD]
 
 
 def solution(mesh):

time: 40.8 us -> 37.5 us (0.919)
  local copies, waits for them, and re-layouts: 3.93 us -> 0.71 us
    reshape x4 -> x0, local copies, waits for them, and re-layouts: 2.37 us -> none  [the longest x1 1.28 us: delta_layer(): gains = out_gain.reshape(HEADS, 1, HD)]
    unnamed x1 -> x0, local copies, waits for them, and re-layouts: 1.54 us -> none
    slice x1, local copies, waits for them, and re-layouts: 0.01 us -> 0.7 us  [body(): return parts[:, :HEADS * HD]]
where the time goes in v7:
time: 37.5 us; the launch traced here: 37.2 us
  blocking collectives  24.2 us (65%)
  Pallas kernels  11.8 us (31%)
  local copies, waits for them, and re-layouts  0.71 us (2%)
  other arithmetic  0.51 us (1%)
    all_gather x1, blocking collectives, body(): full = lax.all_gather(feats, 'seq', axis=0, tiled=True)  15.1 us
    pallas_call x1, Pallas kernels, delta_layer(): pl.pallas_call(delta_kernel, out_shape=jax.ShapeDtypeStruct((frames, slot...  11.8 us
    all_to_all x1, blocking collectives, body(): lax.all_to_all(mixed, 'seq', split_axis=0, concat_axis=1, tiled=True)  9.1 us

profile of v7, /device:TPU:0, one launch (start us, length us, event | category | flops | bytes accessed | tf_op | source)
XLA Modules:
  0.0 37.2 jit_solution(3702485392945979242)
XLA Ops:
  0.0 0.5 %add_minimum_fusion.head_ref = s32[2]{0:T(128)} fusion(s32[]{:T(128)S(6)} %mul.3), kind=kLoop, calls=%fused_computation | loop fusion | flops 4 | bytes 12 | tf_op jit(solution)/shard_map/min | solution.py:166
  0.5 15.1 %all_gather.3.feats_ref = bf16[768,512]{1,0:T(8,128)(2,1)} all-gather(bf16[192,512]{1,0:T(8,128)(2,1)} %param.5), channel_id=1, replica_groups=mesh['seq'=4,'batch'=8] {'seq'}, dimensions={0}, use_global_device_ids=true | all-gather | bytes 983040 | tf_op jit(solution)/shard_map/all_gather | solution.py:167
  15.6 11.8 %shard_map.55 = bf16[512,256]{1,0:T(8,128)(2,1)} custom-call(s32[2]{0:T(128)} %add_minimum_fusion.head_ref, bf16[768,512]{1,0:T(8,128)(2,1)} %all_gather.3.feats_ref, bf16[768,2304]{1,0:T(8,128)(2,1)} %refs_5_.1, bf16[768,2304]{1,0:T(8,128)(2,1)} %refs_5_.1, bf16[768,2304]{1,0:T(8,128)(2,1)} %refs_5_.1, bf16[768,2304]{1,0:T(8,128)(2,1)} %refs_5_.1, ...), custom_call_target="tpu_custom_call" | custom-call | tf_op jit(solution)/shard_map/pallas_call | solution.py:152
  27.4 9.1 %all_to_all.19 = bf16[4,128,256]{2,1,0:T(8,128)(2,1)S(1)} all-to-all(bf16[4,128,256]{2,1,0:T(8,128)(2,1)} %bitcast.6), channel_id=1, replica_groups=mesh['seq'=4,'batch'=8] {'seq'}, dimensions={0} | all-to-all | bytes 524288 | tf_op jit(solution)/shard_map/all_to_all | solution.py:171
  36.5 0.7 %slice.4 = bf16[128,768]{1,0:T(8,128)(2,1)} slice(bf16[128,1024]{1,0:T(8,128)(2,1)S(1)} %bitcast.8), slice={[0:128], [0:768]} | slice | bytes 393216 | tf_op jit(solution)/shard_map/slice | solution.py:172
  (1 shorter events, 0.0 us)

commit v8 on v7

--- a/solution.py
+++ b/solution.py
@@ -54,11 +54,11 @@
 
 
 def delta_kernel(head_ref, feats_ref, *refs):
-    slots = (len(refs) - 10) // 4
+    slots = (len(refs) - 9) // 4
     weight_refs = refs[: 3 * slots]
     bw_ref, bias_ref = refs[3 * slots], refs[3 * slots + 1]
     gain_refs = refs[3 * slots + 2 : 4 * slots + 2]
-    out_ref, qkv_ref, q_ref, k_ref, w_ref, u_ref, p_ref, state_ref = refs[4 * slots + 2 :]
+    out_ref, qkv_ref, k_ref, w_ref, u_ref, p_ref, state_ref = refs[4 * slots + 2 :]
     frames = feats_ref.shape[1]
     chunks = frames // GROUP
     width = slots * HD
@@ -78,17 +78,16 @@
     col = lax.broadcasted_iota(jnp.int32, (chunks, GROUP, GROUP), 2)
     eye = jnp.where(row == col, 1.0, 0.0).astype(jnp.float32)
 
+    pairs = chunks // 2
     for h in range(slots):
         query = unit_normed(qkv_ref[:, pl.ds(h * HD, HD)].astype(jnp.float32))
         keys = unit_normed(qkv_ref[:, pl.ds(width + h * HD, HD)].astype(jnp.float32))
         values = qkv_ref[:, pl.ds(2 * width + h * HD, HD)].astype(jnp.float32)
         rates = jnp.sum(jnp.where(lane == head_ref[h], beta_all, 0.0), -1, keepdims=True)
-        q_ref[h] = query
-        k_ref[h] = keys
+        weighted = (keys * rates).reshape(chunks, GROUP, HD)
+        scaled = (values * rates).reshape(chunks, GROUP, HD)
         query = query.reshape(chunks, GROUP, HD)
         keys = keys.reshape(chunks, GROUP, HD)
-        weighted = (keys.reshape(frames, HD) * rates).reshape(chunks, GROUP, HD)
-        scaled = (values * rates).reshape(chunks, GROUP, HD)
         gram = bmm_nt(weighted, keys)
         negated = jnp.where(row > col, -gram, 0.0)
         inverse = eye + negated
@@ -96,26 +95,47 @@
         for level in range(5):
             power = bmm(power, power)
             inverse = inverse + bmm(inverse, power)
-        w_ref[h] = bmm(inverse, weighted).reshape(frames, HD)
-        u_ref[h] = bmm(inverse, scaled).reshape(frames, HD)
-        p_ref[h] = jnp.where(row >= col, bmm_nt(query, keys), 0.0).reshape(frames, GROUP)
+        wfac = bmm(inverse, weighted).reshape(pairs, 2, GROUP, HD)
+        ufac = bmm(inverse, scaled).reshape(pairs, 2, GROUP, HD)
+        scores = jnp.where(row >= col, bmm_nt(query, keys), 0.0).reshape(pairs, 2, GROUP, GROUP)
+        query = query.reshape(pairs, 2, GROUP, HD)
+        keys = keys.reshape(pairs, 2, GROUP, HD)
+        w1, w2 = wfac[:, 0], wfac[:, 1]
+        u1, u2 = ufac[:, 0], ufac[:, 1]
+        k1 = keys[:, 0]
+        q2 = query[:, 1]
+        carry = bmm_nt(w2, k1)
+        cross = bmm_nt(q2, k1)
+        w_ref[h] = jnp.concatenate([w1, w2 - bmm(carry, w1), query[:, 0], q2], axis=1)
+        u_ref[h] = jnp.concatenate([u1, u2 - bmm(carry, u1)], axis=1)
+        k_ref[h] = jnp.swapaxes(keys.reshape(pairs, 2 * GROUP, HD), 1, 2)
+        zero = jnp.zeros_like(cross)
+        p_ref[h] = jnp.concatenate(
+            [
+                jnp.concatenate([scores[:, 0], zero], axis=2),
+                jnp.concatenate([cross, scores[:, 1]], axis=2),
+            ],
+            axis=1,
+        )
 
     state_ref[...] = jnp.zeros_like(state_ref)
+    span = 2 * GROUP
 
     def step(c, carry):
-        rows = pl.ds(pl.multiple_of(c * GROUP, GROUP), GROUP)
+        rows = pl.ds(pl.multiple_of(c * span, span), span)
         for h in range(slots):
             state = state_ref[h]
-            residual = u_ref[h, rows, :] - mm(w_ref[h, rows, :], state)
-            state_ref[h] = state + mm_tn(k_ref[h, rows, :], residual)
-            output = mm(q_ref[h, rows, :], state) + mm(p_ref[h, rows, :], residual)
+            both = mm(w_ref[h, c], state)
+            residual = u_ref[h, c] - both[:span]
+            state_ref[h] = state + mm(k_ref[h, c], residual)
+            output = both[span:] + mm(p_ref[h, c], residual)
             power_mean = jnp.mean(output * output, -1, keepdims=True) + 1e-06
             out_ref[rows, pl.ds(h * HD, HD)] = (output * lax.rsqrt(power_mean) * gain_refs[h][...]).astype(
                 out_ref.dtype
             )
         return carry
 
-    lax.fori_loop(0, chunks, step, 0, unroll=chunks <= 8)
+    lax.fori_loop(0, pairs, step, 0, unroll=pairs <= 8)
 
 
 def delta_layer(heads, full, qkv_weight, beta_weight, beta_bias, out_gain):
@@ -140,11 +160,10 @@
         out_specs=whole((frames, slots * HD)),
         scratch_shapes=[
             pltpu.VMEM((frames, 3 * slots * HD), jnp.bfloat16),
-            pltpu.VMEM((slots, frames, HD), jnp.float32),
-            pltpu.VMEM((slots, frames, HD), jnp.float32),
-            pltpu.VMEM((slots, frames, HD), jnp.float32),
-            pltpu.VMEM((slots, frames, HD), jnp.float32),
-            pltpu.VMEM((slots, frames, GROUP), jnp.float32),
+            pltpu.VMEM((slots, frames // (2 * GROUP), HD, 2 * GROUP), jnp.float32),
+            pltpu.VMEM((slots, frames // (2 * GROUP), 4 * GROUP, HD), jnp.float32),
+            pltpu.VMEM((slots, frames // (2 * GROUP), 2 * GROUP, HD), jnp.float32),
+            pltpu.VMEM((slots, frames // (2 * GROUP), 2 * GROUP, 2 * GROUP), jnp.float32),
             pltpu.VMEM((slots, HD, HD), jnp.float32),
         ],
     )

time: 37.5 us -> 36.8 us (0.981)
  Pallas kernels: 11.8 us -> 11.1 us
    pallas_call x1, Pallas kernels: 11.8 us -> 11.1 us  [delta_layer(): pl.pallas_call(delta_kernel, out_shape=jax.ShapeDtypeStruct((frames, slot...]
where the time goes in v8:
time: 36.8 us; the launch traced here: 36.5 us
  blocking collectives  24.2 us (66%)
  Pallas kernels  11.1 us (30%)
  local copies, waits for them, and re-layouts  0.71 us (2%)
  other arithmetic  0.51 us (1%)
    all_gather x1, blocking collectives, body(): full = lax.all_gather(feats, 'seq', axis=0, tiled=True)  15.1 us
    pallas_call x1, Pallas kernels, delta_layer(): pl.pallas_call(delta_kernel, out_shape=jax.ShapeDtypeStruct((frames, slot...  11.1 us
    all_to_all x1, blocking collectives, body(): lax.all_to_all(mixed, 'seq', split_axis=0, concat_axis=1, tiled=True)  9.1 us

profile of v8, /device:TPU:0, one launch (start us, length us, event | category | flops | bytes accessed | tf_op | source)
XLA Modules:
  0.0 36.5 jit_solution(2212402832613926287)
XLA Ops:
  0.0 0.5 %add_minimum_fusion.head_ref = s32[2]{0:T(128)} fusion(s32[]{:T(128)S(6)} %mul.3), kind=kLoop, calls=%fused_computation | loop fusion | flops 4 | bytes 12 | tf_op jit(solution)/shard_map/min | solution.py:185
  0.5 15.1 %all_gather.3.feats_ref = bf16[768,512]{1,0:T(8,128)(2,1)} all-gather(bf16[192,512]{1,0:T(8,128)(2,1)} %param.5), channel_id=1, replica_groups=mesh['seq'=4,'batch'=8] {'seq'}, dimensions={0}, use_global_device_ids=true | all-gather | bytes 983040 | tf_op jit(solution)/shard_map/all_gather | solution.py:186
  15.6 11.1 %shard_map.55 = bf16[512,256]{1,0:T(8,128)(2,1)} custom-call(s32[2]{0:T(128)} %add_minimum_fusion.head_ref, bf16[768,512]{1,0:T(8,128)(2,1)} %all_gather.3.feats_ref, bf16[768,2304]{1,0:T(8,128)(2,1)} %refs_5_.1, bf16[768,2304]{1,0:T(8,128)(2,1)} %refs_5_.1, bf16[768,2304]{1,0:T(8,128)(2,1)} %refs_5_.1, bf16[768,2304]{1,0:T(8,128)(2,1)} %refs_5_.1, ...), custom_call_target="tpu_custom_call" | custom-call | tf_op jit(solution)/shard_map/pallas_call | solution.py:171
  26.7 9.1 %all_to_all.19 = bf16[4,128,256]{2,1,0:T(8,128)(2,1)S(1)} all-to-all(bf16[4,128,256]{2,1,0:T(8,128)(2,1)} %bitcast.6), channel_id=1, replica_groups=mesh['seq'=4,'batch'=8] {'seq'}, dimensions={0} | all-to-all | bytes 524288 | tf_op jit(solution)/shard_map/all_to_all | solution.py:190
  35.8 0.7 %slice.4 = bf16[128,768]{1,0:T(8,128)(2,1)} slice(bf16[128,1024]{1,0:T(8,128)(2,1)S(1)} %bitcast.8), slice={[0:128], [0:768]} | slice | bytes 393216 | tf_op jit(solution)/shard_map/slice | solution.py:191
  (1 shorter events, 0.0 us)

commit v9 on v8

--- a/solution.py
+++ b/solution.py
@@ -181,14 +181,19 @@
 def body(feats, qkv_weight, beta_weight, beta_bias, out_gain):
     count = lax.axis_size("seq")
     mine = lax.axis_index("seq")
-    slots = -(-HEADS // count)
-    heads = jnp.minimum(mine * slots + jnp.arange(slots, dtype=jnp.int32), HEADS - 1)
+    slots = HEADS // 2
+    group = mine % 2
+    heads = group * slots + jnp.arange(slots, dtype=jnp.int32)
     full = lax.all_gather(feats, "seq", axis=0, tiled=True)
     mixed = delta_layer(heads, full, qkv_weight, beta_weight, beta_bias, out_gain)
-    frames = mixed.shape[0]
-    rows = frames // count
-    parts = lax.all_to_all(mixed, "seq", split_axis=0, concat_axis=1, tiled=True)
-    return parts[:, : HEADS * HD]
+    rows = mixed.shape[0] // count
+    partner = mine + 1 - 2 * group
+    own = lax.dynamic_slice_in_dim(mixed, mine * rows, rows, 0)
+    sent = lax.dynamic_slice_in_dim(mixed, partner * rows, rows, 0)
+    got = lax.ppermute(sent, "seq", [(s, s + 1 - 2 * (s % 2)) for s in range(count)])
+    return jnp.where(
+        group == 0, jnp.concatenate([own, got], axis=1), jnp.concatenate([got, own], axis=1)
+    )
 
 
 def solution(mesh):

time: 36.8 us -> 37.2 us (1.011)
  blocking collectives: 24.2 us -> 15.1 us
  waiting for transfers between devices: 0 us -> 4.07 us
  Pallas kernels: 11.1 us -> 15 us
  other arithmetic: 0.51 us -> 1.24 us
  starting transfers between devices: 0 us -> 0.61 us
    all_to_all x1 -> x0, blocking collectives: 9.1 us -> none  [body(): lax.all_to_all(mixed, 'seq', split_axis=0, concat_axis=1, tiled=True)]
    ppermute x0 -> x1, waiting for transfers between devices: none -> 4.07 us  [body(): lax.ppermute(sent, 'seq', [(s, s + 1 - 2 * (s % 2)) for s in range(count)])]
    pallas_call x1, Pallas kernels: 11.1 us -> 15 us  [delta_layer(): pl.pallas_call(delta_kernel, out_shape=jax.ShapeDtypeStruct((frames, slot...]
    dynamic_slice x0 -> x1, local copies, waits for them, and re-layouts: none -> 0.96 us  [body(): own = lax.dynamic_slice_in_dim(mixed, mine * rows, rows, 0)]
    select_n x0 -> x1, other arithmetic: none -> 0.73 us  [body(): jnp.where(group == 0, jnp.concatenate([own, got], axis=1), jnp.concatenat...]
    slice x1 -> x0, local copies, waits for them, and re-layouts: 0.7 us -> none  [body(): return parts[:, :HEADS * HD]]
    ppermute x0 -> x1, starting transfers between devices: none -> 0.61 us  [body(): lax.ppermute(sent, 'seq', [(s, s + 1 - 2 * (s % 2)) for s in range(count)])]
    min x1 -> x0, other arithmetic: 0.51 us -> none  [body(): jnp.minimum(mine * slots + jnp.arange(slots, dtype=jnp.int32), HEADS - 1)]
  transfers between devices with their start and end apart: 0 -> 1, of which waited for: 0 -> 1; matrix products, arithmetic and copies ran while one was open for 0% -> 0% of each run, Pallas kernels for 0% -> 0%
where the time goes in v9:
time: 37.2 us; the launch traced here: 37 us
  blocking collectives  15.1 us (41%)
  Pallas kernels  15 us (40%)
  waiting for transfers between devices  4.07 us (11%)
  other arithmetic  1.24 us (3%)
  local copies, waits for them, and re-layouts  0.96 us (3%)
  starting transfers between devices  0.61 us (2%)
    all_gather x1, blocking collectives, body(): full = lax.all_gather(feats, 'seq', axis=0, tiled=True)  15.1 us
    pallas_call x1, Pallas kernels, delta_layer(): pl.pallas_call(delta_kernel, out_shape=jax.ShapeDtypeStruct((frames, slot...  15 us
    ppermute x1, waiting for transfers between devices, body(): lax.ppermute(sent, 'seq', [(s, s + 1 - 2 * (s % 2)) for s in range(count)])  4.07 us
    dynamic_slice x1, local copies, waits for them, and re-layouts, body(): own = lax.dynamic_slice_in_dim(mixed, mine * rows, rows, 0)  0.96 us
  transfers between devices with their start and end apart: 1, of which 1 were waited for; matrix products, arithmetic and copies ran while one was open for 0% of the time, Pallas kernels for 0%

profile of v9, /device:TPU:0, one launch (start us, length us, event | category | flops | bytes accessed | tf_op | source)
XLA Modules:
  0.0 37.0 jit_solution(14477723830825327556)
XLA Ops:
  0.0 0.5 %iota_add_fusion.head_ref = s32[3]{0:T(128)} fusion(s32[]{:T(128)S(6)} %mul.12), kind=kLoop, calls=%fused_computation.1 | loop fusion | flops 3 | bytes 16 | tf_op jit(solution)/shard_map/add | solution.py:186
  0.5 15.1 %all_gather.3.feats_ref = bf16[768,512]{1,0:T(8,128)(2,1)} all-gather(bf16[192,512]{1,0:T(8,128)(2,1)} %param.5), channel_id=1, replica_groups=mesh['seq'=4,'batch'=8] {'seq'}, dimensions={0}, use_global_device_ids=true | all-gather | bytes 983040 | tf_op jit(solution)/shard_map/all_gather | solution.py:187
  15.6 15.0 %shard_map.55 = bf16[512,384]{1,0:T(8,128)(2,1)} custom-call(s32[3]{0:T(128)} %iota_add_fusion.head_ref, bf16[768,512]{1,0:T(8,128)(2,1)} %all_gather.3.feats_ref, bf16[768,2304]{1,0:T(8,128)(2,1)} %refs_8_.1, bf16[768,2304]{1,0:T(8,128)(2,1)} %refs_8_.1, bf16[768,2304]{1,0:T(8,128)(2,1)} %refs_8_.1, bf16[768,2304]{1,0:T(8,128)(2,1)} %refs_8_.1, ...), custom_call_target="tpu_custom_call" | custom-call | tf_op jit(solution)/shard_map/pallas_call | solution.py:171
  30.6 1.0 %constant_dynamic-slice_fusion.1 = (bf16[128,384]{1,0:T(8,128)(2,1)S(1)}, bf16[128,384]{1,0:T(8,128)(2,1)S(1)}) fusion(bf16[512,384]{1,0:T(8,128)(2,1)} %shard_map.55, s32[]{:T(128)S(6)} %select_n.23, s32[]{:T(128)S(6)} %select_n.24), kind=kLoop, calls=%fused_computation.3 | loop fusion | bytes 393224 | tf_op jit(solution)/shard_map/dynamic_slice | solution.py:191
  31.6 0.6 %collective-permute-start = (bf16[128,384]{1,0:T(8,128)(2,1)S(1)}, bf16[128,384]{1,0:T(8,128)(2,1)S(1)}, u32[]{:S(2)}, u32[]{:S(2)}) collective-permute-start(bf16[128,384]{1,0:T(8,128)(2,1)S(1)} %get-tuple-element.6), channel_id=1, source_target_pairs={{0,8},{8,0},{16,24},{24,16},{1,9},{9,1},{17,25},{25,17},{2,10},{10... | collective-permute-start | bytes 294920 | tf_op jit(solution)/shard_map/ppermute | solution.py:193
  32.2 4.1 %collective-permute-done = bf16[128,384]{1,0:T(8,128)(2,1)S(1)} collective-permute-done((bf16[128,384]{1,0:T(8,128)(2,1)S(1)}, bf16[128,384]{1,0:T(8,128)(2,1)S(1)}, u32[]{:S(2)}, u32[]{:S(2)}) %collective-permute-start) | collective-permute-done | bytes 98336 | tf_op jit(solution)/shard_map/ppermute | solution.py:193
  36.3 0.7 %maximum_select_fusion = bf16[128,768]{1,0:T(8,128)(2,1)} fusion(bf16[128,384]{1,0:T(8,128)(2,1)S(1)} %collective-permute-done, bf16[128,384]{1,0:T(8,128)(2,1)S(1)} %get-tuple-element.5, pred[]{:T(512)S(6)} %eq.5), kind=kLoop, calls=%fused_computation | loop fusion | flops 884736 | bytes 393217 | tf_op jit(solution)/shard_map/jit(_where)/select_n | solution.py:194
Async XLA Ops:
  31.6 4.7 %collective-permute-start = (bf16[128,384]{1,0:T(8,128)(2,1)S(1)}, bf16[128,384]{1,0:T(8,128)(2,1)S(1)}, u32[]{:S(2)}, u32[]{:S(2)}) collective-permute-start(bf16[128,384]{1,0:T(8,128)(2,1)S(1)} %get-tuple-element.6), channel_id=1, source_target_pairs={{0,8},{8,0},{16,24},{24,16},{1,9},{9,1},{17,25},{25,17},{2,10},{10... | collective-permute-start | bytes 294920 | tf_op jit(solution)/shard_map/ppermute | solution.py:193

commit v10 on v9

v10 whole, which is shorter than its diff:
```python
import functools

import jax
import jax.numpy as jnp
from jax import lax
from jax.experimental import pallas as pl
from jax.experimental.pallas import tpu as pltpu
from jax.sharding import PartitionSpec as P

HEADS = 6
HD = 128
GROUP = 64

MATMUL_PRECISION = lax.Precision.HIGH


def mm(a, b):
    return lax.dot_general(
        a, b, (((1,), (0,)), ((), ())), precision=MATMUL_PRECISION,
        preferred_element_type=jnp.float32,
    )


def mm_nt(a, b):
    return lax.dot_general(
        a, b, (((1,), (1,)), ((), ())), precision=MATMUL_PRECISION,
        preferred_element_type=jnp.float32,
    )


def mm_tn(a, b):
    return lax.dot_general(
        a, b, (((0,), (0,)), ((), ())), precision=MATMUL_PRECISION,
        preferred_element_type=jnp.float32,
    )


def unit_normed(x):
    return x * lax.rsqrt(jnp.sum(x * x, -1, keepdims=True) + 1e-06)


def bmm(a, b):
    return lax.dot_general(
        a, b, (((2,), (1,)), ((0,), (0,))), precision=MATMUL_PRECISION,
        preferred_element_type=jnp.float32,
    )


def bmm_nt(a, b):
    return lax.dot_general(
        a, b, (((2,), (2,)), ((0,), (0,))), precision=MATMUL_PRECISION,
        preferred_element_type=jnp.float32,
    )


def delta_kernel(head_ref, feats_ref, *refs):
    slots = (len(refs) - 10) // 4
    weight_refs = refs[: 3 * slots]
    bw_ref, bias_ref = refs[3 * slots], refs[3 * slots + 1]
    gain_refs = refs[3 * slots + 2 : 4 * slots + 2]
    own_ref, sent_ref, qkv_ref, k_ref, w_ref, u_ref, p_ref, state_ref = refs[4 * slots + 2 :]
    block = own_ref.shape[0]
    frames = feats_ref.shape[1]
    chunks = frames // GROUP
    width = slots * HD

    full = feats_ref[...].T
    qkv_ref[...] = jnp.dot(
        full, jnp.concatenate([ref[...] for ref in weight_refs], axis=1),
        preferred_element_type=jnp.float32,
    ).astype(qkv_ref.dtype)
    logits = lax.dot_general(
        full, bw_ref[...], (((1,), (1,)), ((), ())), preferred_element_type=jnp.float32
    ) + bias_ref[...]
    beta_all = 1.0 / (1.0 + jnp.exp(-logits))
    lane = lax.broadcasted_iota(jnp.int32, beta_all.shape, 1)

    pairs = chunks // 2
    batch = slots * chunks
    row = lax.broadcasted_iota(jnp.int32, (batch, GROUP, GROUP), 1)
    col = lax.broadcasted_iota(jnp.int32, (batch, GROUP, GROUP), 2)
    eye = jnp.where(row == col, 1.0, 0.0).astype(jnp.float32)
    query = jnp.concatenate(
        [unit_normed(qkv_ref[:, pl.ds(h * HD, HD)].astype(jnp.float32)) for h in range(slots)]
    )
    keys = jnp.concatenate(
        [unit_normed(qkv_ref[:, pl.ds(width + h * HD, HD)].astype(jnp.float32)) for h in range(slots)]
    )
    values = jnp.concatenate(
        [qkv_ref[:, pl.ds(2 * width + h * HD, HD)].astype(jnp.float32) for h in range(slots)]
    )
    rates = jnp.concatenate(
        [
            jnp.sum(jnp.where(lane == head_ref[h], beta_all, 0.0), -1, keepdims=True)
            for h in range(slots)
        ]
    )
    weighted = (keys * rates).reshape(batch, GROUP, HD)
    scaled = (values * rates).reshape(batch, GROUP, HD)
    query = query.reshape(batch, GROUP, HD)
    keys = keys.reshape(batch, GROUP, HD)
    gram = bmm_nt(weighted, keys)
    negated = jnp.where(row > col, -gram, 0.0)
    inverse = eye + negated
    power = negated
    for level in range(5):
        power = bmm(power, power)
        inverse = inverse + bmm(inverse, power)
    wfac = bmm(inverse, weighted).reshape(slots * pairs, 2, GROUP, HD)
    ufac = bmm(inverse, scaled).reshape(slots * pairs, 2, GROUP, HD)
    scores = jnp.where(row >= col, bmm_nt(query, keys), 0.0).reshape(slots * pairs, 2, GROUP, GROUP)
    query = query.reshape(slots * pairs, 2, GROUP, HD)
    keys = keys.reshape(slots * pairs, 2, GROUP, HD)
    w1, w2 = wfac[:, 0], wfac[:, 1]
    u1, u2 = ufac[:, 0], ufac[:, 1]
    k1 = keys[:, 0]
    q2 = query[:, 1]
    carry = bmm_nt(w2, k1)
    cross = bmm_nt(q2, k1)
    stacked = jnp.concatenate([w1, w2 - bmm(carry, w1), query[:, 0], q2], axis=1)
    corrected = jnp.concatenate([u1, u2 - bmm(carry, u1)], axis=1)
    flipped = jnp.swapaxes(keys.reshape(slots * pairs, 2 * GROUP, HD), 1, 2)
    zero = jnp.zeros_like(cross)
    blocks = jnp.concatenate(
        [
            jnp.concatenate([scores[:, 0], zero], axis=2),
            jnp.concatenate([cross, scores[:, 1]], axis=2),
        ],
        axis=1,
    )
    for h in range(slots):
        part = slice(h * pairs, (h + 1) * pairs)
        w_ref[h] = stacked[part]
        u_ref[h] = corrected[part]
        k_ref[h] = flipped[part]
        p_ref[h] = blocks[part]

    state_ref[...] = jnp.zeros_like(state_ref)
    span = 2 * GROUP

    def step(c, carry):
        rows = pl.ds(pl.multiple_of(c * span, span), span)
        for h in range(slots):
            state = state_ref[h]
            both = mm(w_ref[h, c], state)
            residual = u_ref[h, c] - both[:span]
            state_ref[h] = state + mm(k_ref[h, c], residual)
            output = both[span:] + mm(p_ref[h, c], residual)
            power_mean = jnp.mean(output * output, -1, keepdims=True) + 1e-06
            mixed = (output * lax.rsqrt(power_mean) * gain_refs[h][...]).astype(own_ref.dtype)
            local = pl.ds(pl.multiple_of((c * span) % block, span), span)

            @pl.when((c * span) // block == head_ref[slots])
            def _():
                own_ref[local, pl.ds(h * HD, HD)] = mixed

            @pl.when((c * span) // block == head_ref[slots + 1])
            def _():
                sent_ref[local, pl.ds(h * HD, HD)] = mixed

        return carry

    lax.fori_loop(0, pairs, step, 0, unroll=pairs <= 8)


def delta_layer(heads, full, qkv_weight, beta_weight, beta_bias, out_gain, block):
    channels, frames = full.shape
    slots = heads.shape[0] - 2
    whole = lambda shape: pl.BlockSpec(shape, lambda i, head: (0,) * len(shape))
    weight_specs = [
        pl.BlockSpec((channels, HD), lambda i, head, p=p, j=j: (0, p * HEADS + head[j]))
        for p in range(3)
        for j in range(slots)
    ]
    gain_specs = [
        pl.BlockSpec((HD,), lambda i, head, j=j: (head[j],)) for j in range(slots)
    ]
    grid_spec = pltpu.PrefetchScalarGridSpec(
        num_scalar_prefetch=1,
        grid=(1,),
        in_specs=[whole((channels, frames))]
        + weight_specs
        + [whole((HEADS, channels)), whole((1, HEADS))]
        + gain_specs,
        out_specs=[whole((block, slots * HD)), whole((block, slots * HD))],
        scratch_shapes=[
            pltpu.VMEM((frames, 3 * slots * HD), jnp.bfloat16),
            pltpu.VMEM((slots, frames // (2 * GROUP), HD, 2 * GROUP), jnp.float32),
            pltpu.VMEM((slots, frames // (2 * GROUP), 4 * GROUP, HD), jnp.float32),
            pltpu.VMEM((slots, frames // (2 * GROUP), 2 * GROUP, HD), jnp.float32),
            pltpu.VMEM((slots, frames // (2 * GROUP), 2 * GROUP, 2 * GROUP), jnp.float32),
            pltpu.VMEM((slots, HD, HD), jnp.float32),
        ],
    )
    gains = out_gain
    return pl.pallas_call(
        delta_kernel,
        out_shape=[
            jax.ShapeDtypeStruct((block, slots * HD), jnp.bfloat16),
            jax.ShapeDtypeStruct((block, slots * HD), jnp.bfloat16),
        ],
        grid_spec=grid_spec,
    )(
        heads, full, *([qkv_weight] * (3 * slots)), beta_weight.T, beta_bias.reshape(1, HEADS),
        *([gains] * slots),
    )


def body(feats, qkv_weight, beta_weight, beta_bias, out_gain):
    count = lax.axis_size("seq")
    mine = lax.axis_index("seq")
    slots = HEADS // 2
    group = mine % 2
    partner = mine + 1 - 2 * group
    meta = jnp.concatenate(
        [group * slots + jnp.arange(slots, dtype=jnp.int32), jnp.stack([mine, partner]).astype(jnp.int32)]
    )
    full = lax.all_gather(feats, "seq", axis=0, tiled=True)
    rows = feats.shape[1] // count
    own, sent = delta_layer(meta, full, qkv_weight, beta_weight, beta_bias, out_gain, rows)
    got = lax.ppermute(sent, "seq", [(s, s + 1 - 2 * (s % 2)) for s in range(count)])
    return jnp.where(
        group == 0, jnp.concatenate([own, got], axis=1), jnp.concatenate([got, own], axis=1)
    )


def solution(mesh):
    placed = (P("seq", "batch"), P(), P(), P(), P())
    return jax.shard_map(
        body, mesh=mesh, in_specs=placed, out_specs=P(("batch", "seq"), None), check_vma=False
    )
```

time: 37.2 us -> 39.5 us (1.062)
  Pallas kernels: 15 us -> 17 us
  other arithmetic: 1.24 us -> 2.31 us
  local copies, waits for them, and re-layouts: 0.96 us -> 0 us
    pallas_call x1, Pallas kernels: 15 us -> 17 us  [delta_layer(): pl.pallas_call(delta_kernel, out_shape=[jax.ShapeDtypeStruct((block, slot...]
    select_n x1, other arithmetic: 0.73 us -> 1.69 us  [body(): jnp.where(group == 0, jnp.concatenate([own, got], axis=1), jnp.concatenat...]
    dynamic_slice x1 -> x0, local copies, waits for them, and re-layouts: 0.96 us -> none  [body(): own = lax.dynamic_slice_in_dim(mixed, mine * rows, rows, 0)]
    concatenate x0 -> x1, other arithmetic: none -> 0.62 us  [body(): jnp.concatenate([group * slots + jnp.arange(slots, dtype=jnp.int32), jnp....]
    add x1, other arithmetic: 0.51 us -> 0.01 us  [body(): group * slots + jnp.arange(slots, dtype=jnp.int32)]
where the time goes in v10:
time: 39.5 us; the launch traced here: 39.3 us
  Pallas kernels  17 us (43%)
  blocking collectives  15.1 us (38%)
  waiting for transfers between devices  4.28 us (11%)
  other arithmetic  2.31 us (6%)
  starting transfers between devices  0.55 us (1%)
    pallas_call x1, Pallas kernels, delta_layer(): pl.pallas_call(delta_kernel, out_shape=[jax.ShapeDtypeStruct((block, slot...  17 us
    all_gather x1, blocking collectives, body(): full = lax.all_gather(feats, 'seq', axis=0, tiled=True)  15.1 us
    ppermute x1, waiting for transfers between devices, body(): lax.ppermute(sent, 'seq', [(s, s + 1 - 2 * (s % 2)) for s in range(count)])  4.28 us
    select_n x1, other arithmetic, body(): jnp.where(group == 0, jnp.concatenate([own, got], axis=1), jnp.concatenat...  1.69 us
  transfers between devices with their start and end apart: 1, of which 1 were waited for; matrix products, arithmetic and copies ran while one was open for 0% of the time, Pallas kernels for 0%

profile of v10, /device:TPU:0, one launch (start us, length us, event | category | flops | bytes accessed | tf_op | source)
XLA Modules:
  0.0 39.3 jit_solution(1571801726368303245)
XLA Ops:
  0.0 15.1 %all_gather.3.feats_ref = bf16[768,512]{1,0:T(8,128)(2,1)} all-gather(bf16[192,512]{1,0:T(8,128)(2,1)} %param.5), channel_id=1, replica_groups=mesh['seq'=4,'batch'=8] {'seq'}, dimensions={0}, use_global_device_ids=true | all-gather | bytes 983040 | tf_op jit(solution)/shard_map/all_gather | solution.py:218
  15.1 0.6 %pad_add_fusion.head_ref = s32[5]{0:T(128)} fusion(s32[1]{0:T(128)} %bitcast.1, s32[1]{0:T(128)} %bitcast, s32[3]{0:T(128)S(1)} %iota_add_fusion), kind=kLoop, calls=%fused_computation.1 | loop fusion | flops 10 | bytes 40 | tf_op jit(solution)/shard_map/concatenate | solution.py:215
  15.7 17.0 %shard_map.55 = (bf16[128,384]{1,0:T(8,128)(2,1)}, bf16[128,384]{1,0:T(8,128)(2,1)}) custom-call(s32[5]{0:T(128)} %pad_add_fusion.head_ref, bf16[768,512]{1,0:T(8,128)(2,1)} %all_gather.3.feats_ref, bf16[768,2304]{1,0:T(8,128)(2,1)} %refs_8_.1, bf16[768,2304]{1,0:T(8,128)(2,1)} %refs_8_.1, bf16[768,2304]{1,0:T(8,128)(2,1)} %refs_8_.1, ...), custom_call_target="tpu_custom_call" | custom-call | tf_op jit(solution)/shard_map/pallas_call | solution.py:196
  32.7 0.5 %collective-permute-start = (bf16[128,384]{1,0:T(8,128)(2,1)}, bf16[128,384]{1,0:T(8,128)(2,1)S(1)}, u32[]{:S(2)}, u32[]{:S(2)}) collective-permute-start(bf16[128,384]{1,0:T(8,128)(2,1)} %get-tuple-element.8), channel_id=1, source_target_pairs={{0,8},{8,0},{16,24},{24,16},{1,9},{9,1},{17,25},{25,17},{2,10},{10... | collective-permute-start | bytes 294920 | tf_op jit(solution)/shard_map/ppermute | solution.py:221
  33.3 4.3 %collective-permute-done = bf16[128,384]{1,0:T(8,128)(2,1)S(1)} collective-permute-done((bf16[128,384]{1,0:T(8,128)(2,1)}, bf16[128,384]{1,0:T(8,128)(2,1)S(1)}, u32[]{:S(2)}, u32[]{:S(2)}) %collective-permute-start) | collective-permute-done | bytes 98336 | tf_op jit(solution)/shard_map/ppermute | solution.py:221
  37.6 1.7 %maximum_select_fusion = bf16[128,768]{1,0:T(8,128)(2,1)} fusion(bf16[128,384]{1,0:T(8,128)(2,1)S(1)} %collective-permute-done, bf16[128,384]{1,0:T(8,128)(2,1)} %get-tuple-element.7, pred[]{:T(512)S(6)} %eq.5), kind=kLoop, calls=%fused_computation | loop fusion | flops 884736 | bytes 393217 | tf_op jit(solution)/shard_map/jit(_where)/select_n | solution.py:222
  (1 shorter events, 0.0 us)
Async XLA Ops:
  32.7 4.8 %collective-permute-start = (bf16[128,384]{1,0:T(8,128)(2,1)}, bf16[128,384]{1,0:T(8,128)(2,1)S(1)}, u32[]{:S(2)}, u32[]{:S(2)}) collective-permute-start(bf16[128,384]{1,0:T(8,128)(2,1)} %get-tuple-element.8), channel_id=1, source_target_pairs={{0,8},{8,0},{16,24},{24,16},{1,9},{9,1},{17,25},{25,17},{2,10},{10... | collective-permute-start | bytes 294920 | tf_op jit(solution)/shard_map/ppermute | solution.py:221

commit v11 on v8

--- a/solution.py
+++ b/solution.py
@@ -187,8 +187,19 @@
     mixed = delta_layer(heads, full, qkv_weight, beta_weight, beta_bias, out_gain)
     frames = mixed.shape[0]
     rows = frames // count
-    parts = lax.all_to_all(mixed, "seq", split_axis=0, concat_axis=1, tiled=True)
-    return parts[:, : HEADS * HD]
+    blocks = mixed.reshape(count, rows, slots * HD)
+    got = [lax.dynamic_index_in_dim(blocks, mine, 0, keepdims=False)]
+    for d in range(1, count):
+        part = lax.dynamic_index_in_dim(blocks, (mine + d) % count, 0, keepdims=False)
+        got.append(lax.ppermute(part, "seq", [(s, (s + d) % count) for s in range(count)]))
+    needed = -(-HEADS // slots)
+    placed = []
+    for k in range(needed):
+        pick = got[0]
+        for d in range(1, count):
+            pick = jnp.where((mine - d) % count == k, got[d], pick)
+        placed.append(pick)
+    return jnp.concatenate(placed, axis=1)[:, : HEADS * HD]
 
 
 def solution(mesh):

time: 36.8 us -> 36.7 us (level)
  blocking collectives: 24.2 us -> 15.1 us
  waiting for transfers between devices: 0 us -> 4.6 us
  starting transfers between devices: 0 us -> 2.63 us
  other arithmetic: 0.51 us -> 2.07 us
    all_to_all x1 -> x0, blocking collectives: 9.1 us -> none  [body(): lax.all_to_all(mixed, 'seq', split_axis=0, concat_axis=1, tiled=True)]
    ppermute x0 -> x3, waiting for transfers between devices: none -> 4.6 us  [body(): lax.ppermute(part, 'seq', [(s, (s + d) % count) for s in range(count)])]
    ppermute x0 -> x3, starting transfers between devices: none -> 2.63 us  [body(): lax.ppermute(part, 'seq', [(s, (s + d) % count) for s in range(count)])]
    squeeze x0 -> x1, local copies, waits for them, and re-layouts: none -> 0.92 us  [body(): lax.dynamic_index_in_dim(blocks, (mine + d) % count, 0, keepdims=False)]
    select_n x0 -> x1, other arithmetic: none -> 0.87 us  [body(): pick = jnp.where((mine - d) % count == k, got[d], pick)]
    slice x1 -> x0, local copies, waits for them, and re-layouts: 0.7 us -> none  [body(): return parts[:, :HEADS * HD]]
    concatenate x0 -> x1, other arithmetic: none -> 0.69 us  [body(): return jnp.concatenate(placed, axis=1)[:, :HEADS * HD]]
  transfers between devices with their start and end apart: 0 -> 3, of which waited for: 0 -> 3; matrix products, arithmetic and copies ran while one was open for 0% -> 0% of each run, Pallas kernels for 0% -> 0%
where the time goes in v11:
time: 36.7 us; the launch traced here: 36.4 us
  blocking collectives  15.1 us (41%)
  Pallas kernels  11 us (30%)
  waiting for transfers between devices  4.6 us (13%)
  starting transfers between devices  2.63 us (7%)
  other arithmetic  2.07 us (6%)
  local copies, waits for them, and re-layouts  0.92 us (3%)
    all_gather x1, blocking collectives, body(): full = lax.all_gather(feats, 'seq', axis=0, tiled=True)  15.1 us
    pallas_call x1, Pallas kernels, delta_layer(): pl.pallas_call(delta_kernel, out_shape=jax.ShapeDtypeStruct((frames, slot...  11 us
    ppermute x3, waiting for transfers between devices, body(): lax.ppermute(part, 'seq', [(s, (s + d) % count) for s in range(count)])  4.6 us
    ppermute x3, starting transfers between devices, body(): lax.ppermute(part, 'seq', [(s, (s + d) % count) for s in range(count)])  2.63 us
    squeeze x1, local copies, waits for them, and re-layouts, body(): lax.dynamic_index_in_dim(blocks, (mine + d) % count, 0, keepdims=False)  0.92 us
    select_n x1, other arithmetic, body(): pick = jnp.where((mine - d) % count == k, got[d], pick)  0.87 us
  transfers between devices with their start and end apart: 3, of which 3 were waited for; matrix products, arithmetic and copies ran while one was open for 0% of the time, Pallas kernels for 0%

profile of v11, /device:TPU:0, one launch (start us, length us, event | category | flops | bytes accessed | tf_op | source)
XLA Modules:
  0.0 36.4 jit_solution(8639309842853105887)
XLA Ops:
  0.0 0.5 %add_minimum_fusion.head_ref = s32[2]{0:T(128)} fusion(s32[]{:T(128)S(6)} %mul.3), kind=kLoop, calls=%fused_computation.13 | loop fusion | flops 4 | bytes 12 | tf_op jit(solution)/shard_map/min | solution.py:185
  0.5 15.1 %all_gather.3.feats_ref = bf16[768,512]{1,0:T(8,128)(2,1)} all-gather(bf16[192,512]{1,0:T(8,128)(2,1)} %param.5), channel_id=1, replica_groups=mesh['seq'=4,'batch'=8] {'seq'}, dimensions={0}, use_global_device_ids=true | all-gather | bytes 983040 | tf_op jit(solution)/shard_map/all_gather | solution.py:186
  15.6 11.0 %shard_map.55 = bf16[512,256]{1,0:T(8,128)(2,1)} custom-call(s32[2]{0:T(128)} %add_minimum_fusion.head_ref, bf16[768,512]{1,0:T(8,128)(2,1)} %all_gather.3.feats_ref, bf16[768,2304]{1,0:T(8,128)(2,1)} %refs_5_.1, bf16[768,2304]{1,0:T(8,128)(2,1)} %refs_5_.1, bf16[768,2304]{1,0:T(8,128)(2,1)} %refs_5_.1, bf16[768,2304]{1,0:T(8,128)(2,1)} %refs_5_.1, ...), custom_call_target="tpu_custom_call" | custom-call | tf_op jit(solution)/shard_map/pallas_call | solution.py:171
  26.7 0.9 %dynamic-slice_bitcast_fusion = (bf16[128,256]{1,0:T(8,128)(2,1)S(1)}, bf16[128,256]{1,0:T(8,128)(2,1)S(1)}, bf16[128,256]{1,0:T(8,128)(2,1)S(1)}) fusion(bf16[4,128,256]{2,1,0:T(8,128)(2,1)} %bitcast.25, s32[]{:T(128)S(6)} %select_n.119, s32[]{:T(128)S(6)} %select_n.115, s32[]{:T(128)S(6)} %select_n.111), kind=kLoop, calls=%fused_computation.10 | loop fusion | bytes 393228 | tf_op jit(solution)/shard_map/jit(dynamic_index_in_dim)/squeeze | solution.py:193
  27.6 1.5 %collective-permute-start = (bf16[128,256]{1,0:T(8,128)(2,1)S(1)}, bf16[128,256]{1,0:T(8,128)(2,1)S(1)}, u32[]{:S(2)}, u32[]{:S(2)}) collective-permute-start(bf16[128,256]{1,0:T(8,128)(2,1)S(1)} %get-tuple-element.10), channel_id=1, source_target_pairs={{0,24},{8,0},{16,8},{24,16},{1,25},{9,1},{17,9},{25,17},{2,26},{10... | collective-permute-start | bytes 196616 | tf_op jit(solution)/shard_map/ppermute | solution.py:194
  29.1 0.6 %collective-permute-start.1 = (bf16[128,256]{1,0:T(8,128)(2,1)S(1)}, bf16[128,256]{1,0:T(8,128)(2,1)S(1)}, u32[]{:S(2)}, u32[]{:S(2)}) collective-permute-start(bf16[128,256]{1,0:T(8,128)(2,1)S(1)} %get-tuple-element.9), channel_id=1, source_target_pairs={{0,16},{8,24},{16,0},{24,8},{1,17},{9,25},{17,1},{25,9},{2,18},{10... | collective-permute-start | bytes 196616 | tf_op jit(solution)/shard_map/ppermute | solution.py:194
  29.7 0.6 %collective-permute-start.2 = (bf16[128,256]{1,0:T(8,128)(2,1)S(1)}, bf16[128,256]{1,0:T(8,128)(2,1)S(1)}, u32[]{:S(2)}, u32[]{:S(2)}) collective-permute-start(bf16[128,256]{1,0:T(8,128)(2,1)S(1)} %get-tuple-element.8), channel_id=1, source_target_pairs={{0,8},{8,16},{16,24},{24,0},{1,9},{9,17},{17,25},{25,1},{2,10},{10... | collective-permute-start | bytes 196616 | tf_op jit(solution)/shard_map/ppermute | solution.py:194
  30.2 2.3 %collective-permute-done = bf16[128,256]{1,0:T(8,128)(2,1)S(1)} collective-permute-done((bf16[128,256]{1,0:T(8,128)(2,1)S(1)}, bf16[128,256]{1,0:T(8,128)(2,1)S(1)}, u32[]{:S(2)}, u32[]{:S(2)}) %collective-permute-start) | collective-permute-done | bytes 65568 | tf_op jit(solution)/shard_map/ppermute | solution.py:194
  32.5 0.8 %collective-permute-done.1 = bf16[128,256]{1,0:T(8,128)(2,1)S(1)} collective-permute-done((bf16[128,256]{1,0:T(8,128)(2,1)S(1)}, bf16[128,256]{1,0:T(8,128)(2,1)S(1)}, u32[]{:S(2)}, u32[]{:S(2)}) %collective-permute-start.1) | collective-permute-done | bytes 65568 | tf_op jit(solution)/shard_map/ppermute | solution.py:194
  33.4 1.5 %collective-permute-done.2 = bf16[128,256]{1,0:T(8,128)(2,1)S(1)} collective-permute-done((bf16[128,256]{1,0:T(8,128)(2,1)S(1)}, bf16[128,256]{1,0:T(8,128)(2,1)S(1)}, u32[]{:S(2)}, u32[]{:S(2)}) %collective-permute-start.2) | collective-permute-done | bytes 65568 | tf_op jit(solution)/shard_map/ppermute | solution.py:194
  34.8 0.9 %fusion.1 = (bf16[128,256]{1,0:T(8,128)(2,1)S(1)}, bf16[128,256]{1,0:T(8,128)(2,1)S(1)}, bf16[128,256]{1,0:T(8,128)(2,1)S(1)}) fusion(bf16[128,256]{1,0:T(8,128)(2,1)S(1)} %collective-permute-done, bf16[128,256]{1,0:T(8,128)(2,1)S(1)} %collective-permute-done.1, bf16[128,256]{1,0:T(8,128)(2,1)S(1)} %collective-permute-done.2, pred[]{:T(512)S(6)} %eq.42, ...), kind=kLoop, calls=%fused_computation.5 | loop fusion | flops 294912 | bytes 458765 | tf_op jit(solution)/shard_map/jit(_where)/select_n | solution.py:200
  35.7 0.7 %pad_maximum_fusion = bf16[128,768]{1,0:T(8,128)(2,1)} fusion(bf16[128,256]{1,0:T(8,128)(2,1)S(1)} %get-tuple-element.6, bf16[128,256]{1,0:T(8,128)(2,1)S(1)} %get-tuple-element.7, bf16[128,256]{1,0:T(8,128)(2,1)S(1)} %get-tuple-element.5), kind=kLoop, calls=%fused_computation | loop fusion | flops 589824 | bytes 393216 | tf_op jit(solution)/shard_map/concatenate | solution.py:202
Async XLA Ops:
  27.6 4.9 %collective-permute-start = (bf16[128,256]{1,0:T(8,128)(2,1)S(1)}, bf16[128,256]{1,0:T(8,128)(2,1)S(1)}, u32[]{:S(2)}, u32[]{:S(2)}) collective-permute-start(bf16[128,256]{1,0:T(8,128)(2,1)S(1)} %get-tuple-element.10), channel_id=1, source_target_pairs={{0,24},{8,0},{16,8},{24,16},{1,25},{9,1},{17,9},{25,17},{2,26},{10... | collective-permute-start | bytes 196616 | tf_op jit(solution)/shard_map/ppermute | solution.py:194
  29.1 4.3 %collective-permute-start.1 = (bf16[128,256]{1,0:T(8,128)(2,1)S(1)}, bf16[128,256]{1,0:T(8,128)(2,1)S(1)}, u32[]{:S(2)}, u32[]{:S(2)}) collective-permute-start(bf16[128,256]{1,0:T(8,128)(2,1)S(1)} %get-tuple-element.9), channel_id=1, source_target_pairs={{0,16},{8,24},{16,0},{24,8},{1,17},{9,25},{17,1},{25,9},{2,18},{10... | collective-permute-start | bytes 196616 | tf_op jit(solution)/shard_map/ppermute | solution.py:194
  29.7 5.2 %collective-permute-start.2 = (bf16[128,256]{1,0:T(8,128)(2,1)S(1)}, bf16[128,256]{1,0:T(8,128)(2,1)S(1)}, u32[]{:S(2)}, u32[]{:S(2)}) collective-permute-start(bf16[128,256]{1,0:T(8,128)(2,1)S(1)} %get-tuple-element.8), channel_id=1, source_target_pairs={{0,8},{8,16},{16,24},{24,0},{1,9},{9,17},{17,25},{25,1},{2,10},{10... | collective-permute-start | bytes 196616 | tf_op jit(solution)/shard_map/ppermute | solution.py:194

commit v12 on v11

--- a/solution.py
+++ b/solution.py
@@ -53,7 +53,7 @@
     )
 
 
-def delta_kernel(head_ref, feats_ref, *refs):
+def delta_kernel(count, head_ref, feats_ref, *refs):
     slots = (len(refs) - 9) // 4
     weight_refs = refs[: 3 * slots]
     bw_ref, bias_ref = refs[3 * slots], refs[3 * slots + 1]
@@ -122,7 +122,9 @@
     span = 2 * GROUP
 
     def step(c, carry):
-        rows = pl.ds(pl.multiple_of(c * span, span), span)
+        block = frames // count
+        owner = ((c * span) // block - head_ref[slots] + count) % count
+        place = pl.ds(pl.multiple_of(owner * block + (c * span) % block, span), span)
         for h in range(slots):
             state = state_ref[h]
             both = mm(w_ref[h, c], state)
@@ -130,7 +132,7 @@
             state_ref[h] = state + mm(k_ref[h, c], residual)
             output = both[span:] + mm(p_ref[h, c], residual)
             power_mean = jnp.mean(output * output, -1, keepdims=True) + 1e-06
-            out_ref[rows, pl.ds(h * HD, HD)] = (output * lax.rsqrt(power_mean) * gain_refs[h][...]).astype(
+            out_ref[place, pl.ds(h * HD, HD)] = (output * lax.rsqrt(power_mean) * gain_refs[h][...]).astype(
                 out_ref.dtype
             )
         return carry
@@ -138,9 +140,9 @@
     lax.fori_loop(0, pairs, step, 0, unroll=pairs <= 8)
 
 
-def delta_layer(heads, full, qkv_weight, beta_weight, beta_bias, out_gain):
+def delta_layer(heads, full, qkv_weight, beta_weight, beta_bias, out_gain, count):
     channels, frames = full.shape
-    slots = heads.shape[0]
+    slots = heads.shape[0] - 1
     whole = lambda shape: pl.BlockSpec(shape, lambda i, head: (0,) * len(shape))
     weight_specs = [
         pl.BlockSpec((channels, HD), lambda i, head, p=p, j=j: (0, p * HEADS + head[j]))
@@ -169,7 +171,7 @@
     )
     gains = out_gain
     return pl.pallas_call(
-        delta_kernel,
+        functools.partial(delta_kernel, count),
         out_shape=jax.ShapeDtypeStruct((frames, slots * HD), jnp.bfloat16),
         grid_spec=grid_spec,
     )(
@@ -183,15 +185,15 @@
     mine = lax.axis_index("seq")
     slots = -(-HEADS // count)
     heads = jnp.minimum(mine * slots + jnp.arange(slots, dtype=jnp.int32), HEADS - 1)
+    meta = jnp.concatenate([heads, mine.astype(jnp.int32).reshape(1)])
     full = lax.all_gather(feats, "seq", axis=0, tiled=True)
-    mixed = delta_layer(heads, full, qkv_weight, beta_weight, beta_bias, out_gain)
+    mixed = delta_layer(meta, full, qkv_weight, beta_weight, beta_bias, out_gain, count)
     frames = mixed.shape[0]
     rows = frames // count
     blocks = mixed.reshape(count, rows, slots * HD)
-    got = [lax.dynamic_index_in_dim(blocks, mine, 0, keepdims=False)]
+    got = [blocks[0]]
     for d in range(1, count):
-        part = lax.dynamic_index_in_dim(blocks, (mine + d) % count, 0, keepdims=False)
-        got.append(lax.ppermute(part, "seq", [(s, (s + d) % count) for s in range(count)]))
+        got.append(lax.ppermute(blocks[d], "seq", [(s, (s + d) % count) for s in range(count)]))
     needed = -(-HEADS // slots)
     placed = []
     for k in range(needed):

time: 36.7 us -> 36.8 us (level)
    slice x0 -> x1, local copies, waits for them, and re-layouts: none -> 0.92 us  [body(): blocks[d]]
    squeeze x1 -> x0, local copies, waits for them, and re-layouts: 0.92 us -> none  [body(): lax.dynamic_index_in_dim(blocks, (mine + d) % count, 0, keepdims=False)]
    concatenate x0 -> x1, other arithmetic: none -> 0.66 us  [body(): meta = jnp.concatenate([heads, mine.astype(jnp.int32).reshape(1)])]
    min x1, other arithmetic: 0.51 us -> 0.01 us  [body(): jnp.minimum(mine * slots + jnp.arange(slots, dtype=jnp.int32), HEADS - 1)]
where the time goes in v12:
time: 36.8 us; the launch traced here: 36.5 us
  blocking collectives  15.1 us (41%)
  Pallas kernels  11 us (30%)
  waiting for transfers between devices  4.6 us (12%)
  starting transfers between devices  2.64 us (7%)
  other arithmetic  2.22 us (6%)
  local copies, waits for them, and re-layouts  0.92 us (2%)
    all_gather x1, blocking collectives, body(): full = lax.all_gather(feats, 'seq', axis=0, tiled=True)  15.1 us
    pallas_call x1, Pallas kernels, delta_layer(): pl.pallas_call(functools.partial(delta_kernel, count), out_shape=jax.Shap...  11 us
    ppermute x3, waiting for transfers between devices, body(): lax.ppermute(blocks[d], 'seq', [(s, (s + d) % count) for s in range(count)])  4.6 us
    ppermute x3, starting transfers between devices, body(): lax.ppermute(blocks[d], 'seq', [(s, (s + d) % count) for s in range(count)])  2.64 us
    slice x1, local copies, waits for them, and re-layouts, body(): blocks[d]  0.92 us
    select_n x1, other arithmetic, body(): pick = jnp.where((mine - d) % count == k, got[d], pick)  0.87 us
  transfers between devices with their start and end apart: 3, of which 3 were waited for; matrix products, arithmetic and copies ran while one was open for 0% of the time, Pallas kernels for 0%

profile of v12, /device:TPU:0, one launch (start us, length us, event | category | flops | bytes accessed | tf_op | source)
XLA Modules:
  0.0 36.5 jit_solution(17862816316666419774)
XLA Ops:
  0.0 15.1 %all_gather.3.feats_ref = bf16[768,512]{1,0:T(8,128)(2,1)} all-gather(bf16[192,512]{1,0:T(8,128)(2,1)} %param.5), channel_id=1, replica_groups=mesh['seq'=4,'batch'=8] {'seq'}, dimensions={0}, use_global_device_ids=true | all-gather | bytes 983040 | tf_op jit(solution)/shard_map/all_gather | solution.py:189
  15.1 0.7 %pad_add_fusion.head_ref = s32[3]{0:T(128)} fusion(s32[1]{0:T(128)} %bitcast, s32[2]{0:T(128)S(1)} %add_minimum_fusion), kind=kLoop, calls=%fused_computation.4 | loop fusion | flops 3 | bytes 24 | tf_op jit(solution)/shard_map/concatenate | solution.py:188
  15.8 11.0 %shard_map.55 = bf16[512,256]{1,0:T(8,128)(2,1)} custom-call(s32[3]{0:T(128)} %pad_add_fusion.head_ref, bf16[768,512]{1,0:T(8,128)(2,1)} %all_gather.3.feats_ref, bf16[768,2304]{1,0:T(8,128)(2,1)} %refs_5_.1, bf16[768,2304]{1,0:T(8,128)(2,1)} %refs_5_.1, bf16[768,2304]{1,0:T(8,128)(2,1)} %refs_5_.1, bf16[768,2304]{1,0:T(8,128)(2,1)} %refs_5_.1, ...), custom_call_target="tpu_custom_call" | custom-call | tf_op jit(solution)/shard_map/pallas_call | solution.py:173
  26.8 0.9 %fusion = (bf16[128,256]{1,0:T(8,128)(2,1)S(1)}, bf16[128,256]{1,0:T(8,128)(2,1)S(1)}, bf16[128,256]{1,0:T(8,128)(2,1)S(1)}) fusion(bf16[512,256]{1,0:T(8,128)(2,1)} %shard_map.55), kind=kLoop, calls=%fused_computation.6 | loop fusion | bytes 393216 | tf_op jit(solution)/shard_map/slice | solution.py:196
  27.8 1.5 %collective-permute-start = (bf16[128,256]{1,0:T(8,128)(2,1)S(1)}, bf16[128,256]{1,0:T(8,128)(2,1)S(1)}, u32[]{:S(2)}, u32[]{:S(2)}) collective-permute-start(bf16[128,256]{1,0:T(8,128)(2,1)S(1)} %get-tuple-element.10), channel_id=1, source_target_pairs={{0,24},{8,0},{16,8},{24,16},{1,25},{9,1},{17,9},{25,17},{2,26},{10... | collective-permute-start | bytes 196616 | tf_op jit(solution)/shard_map/ppermute | solution.py:196
  29.3 0.6 %collective-permute-start.1 = (bf16[128,256]{1,0:T(8,128)(2,1)S(1)}, bf16[128,256]{1,0:T(8,128)(2,1)S(1)}, u32[]{:S(2)}, u32[]{:S(2)}) collective-permute-start(bf16[128,256]{1,0:T(8,128)(2,1)S(1)} %get-tuple-element.9), channel_id=1, source_target_pairs={{0,16},{8,24},{16,0},{24,8},{1,17},{9,25},{17,1},{25,9},{2,18},{10... | collective-permute-start | bytes 196616 | tf_op jit(solution)/shard_map/ppermute | solution.py:196
  29.8 0.6 %collective-permute-start.2 = (bf16[128,256]{1,0:T(8,128)(2,1)S(1)}, bf16[128,256]{1,0:T(8,128)(2,1)S(1)}, u32[]{:S(2)}, u32[]{:S(2)}) collective-permute-start(bf16[128,256]{1,0:T(8,128)(2,1)S(1)} %get-tuple-element.8), channel_id=1, source_target_pairs={{0,8},{8,16},{16,24},{24,0},{1,9},{9,17},{17,25},{25,1},{2,10},{10... | collective-permute-start | bytes 196616 | tf_op jit(solution)/shard_map/ppermute | solution.py:196
  30.4 2.3 %collective-permute-done = bf16[128,256]{1,0:T(8,128)(2,1)S(1)} collective-permute-done((bf16[128,256]{1,0:T(8,128)(2,1)S(1)}, bf16[128,256]{1,0:T(8,128)(2,1)S(1)}, u32[]{:S(2)}, u32[]{:S(2)}) %collective-permute-start) | collective-permute-done | bytes 65568 | tf_op jit(solution)/shard_map/ppermute | solution.py:196
  32.7 0.8 %collective-permute-done.1 = bf16[128,256]{1,0:T(8,128)(2,1)S(1)} collective-permute-done((bf16[128,256]{1,0:T(8,128)(2,1)S(1)}, bf16[128,256]{1,0:T(8,128)(2,1)S(1)}, u32[]{:S(2)}, u32[]{:S(2)}) %collective-permute-start.1) | collective-permute-done | bytes 65568 | tf_op jit(solution)/shard_map/ppermute | solution.py:196
  33.5 1.4 %collective-permute-done.2 = bf16[128,256]{1,0:T(8,128)(2,1)S(1)} collective-permute-done((bf16[128,256]{1,0:T(8,128)(2,1)S(1)}, bf16[128,256]{1,0:T(8,128)(2,1)S(1)}, u32[]{:S(2)}, u32[]{:S(2)}) %collective-permute-start.2) | collective-permute-done | bytes 65568 | tf_op jit(solution)/shard_map/ppermute | solution.py:196
  35.0 0.9 %select_select_fusion.2 = (bf16[128,256]{1,0:T(8,128)(2,1)S(1)}, bf16[128,256]{1,0:T(8,128)(2,1)S(1)}, bf16[128,256]{1,0:T(8,128)(2,1)S(1)}) fusion(bf16[128,256]{1,0:T(8,128)(2,1)S(1)} %collective-permute-done, bf16[128,256]{1,0:T(8,128)(2,1)S(1)} %collective-permute-done.1, bf16[128,256]{1,0:T(8,128)(2,1)S(1)} %collective-permute-done.2, pred[]{:T(512)S(6)} %eq.39, ...), kind=kLoop, calls=%fused_computation.3 | loop fusion | flops 294912 | bytes 458761 | tf_op jit(solution)/shard_map/jit(_where)/select_n | solution.py:202
  35.9 0.7 %pad_maximum_fusion = bf16[128,768]{1,0:T(8,128)(2,1)} fusion(bf16[128,256]{1,0:T(8,128)(2,1)S(1)} %get-tuple-element.6, bf16[128,256]{1,0:T(8,128)(2,1)S(1)} %get-tuple-element.7, bf16[128,256]{1,0:T(8,128)(2,1)S(1)} %get-tuple-element.5), kind=kLoop, calls=%fused_computation | loop fusion | flops 589824 | bytes 393216 | tf_op jit(solution)/shard_map/concatenate | solution.py:204
  (1 shorter events, 0.0 us)
Async XLA Ops:
  27.8 4.9 %collective-permute-start = (bf16[128,256]{1,0:T(8,128)(2,1)S(1)}, bf16[128,256]{1,0:T(8,128)(2,1)S(1)}, u32[]{:S(2)}, u32[]{:S(2)}) collective-permute-start(bf16[128,256]{1,0:T(8,128)(2,1)S(1)} %get-tuple-element.10), channel_id=1, source_target_pairs={{0,24},{8,0},{16,8},{24,16},{1,25},{9,1},{17,9},{25,17},{2,26},{10... | collective-permute-start | bytes 196616 | tf_op jit(solution)/shard_map/ppermute | solution.py:196
  29.3 4.3 %collective-permute-start.1 = (bf16[128,256]{1,0:T(8,128)(2,1)S(1)}, bf16[128,256]{1,0:T(8,128)(2,1)S(1)}, u32[]{:S(2)}, u32[]{:S(2)}) collective-permute-start(bf16[128,256]{1,0:T(8,128)(2,1)S(1)} %get-tuple-element.9), channel_id=1, source_target_pairs={{0,16},{8,24},{16,0},{24,8},{1,17},{9,25},{17,1},{25,9},{2,18},{10... | collective-permute-start | bytes 196616 | tf_op jit(solution)/shard_map/ppermute | solution.py:196
  29.8 5.2 %collective-permute-start.2 = (bf16[128,256]{1,0:T(8,128)(2,1)S(1)}, bf16[128,256]{1,0:T(8,128)(2,1)S(1)}, u32[]{:S(2)}, u32[]{:S(2)}) collective-permute-start(bf16[128,256]{1,0:T(8,128)(2,1)S(1)} %get-tuple-element.8), channel_id=1, source_target_pairs={{0,8},{8,16},{16,24},{24,0},{1,9},{9,17},{17,25},{25,1},{2,10},{10... | collective-permute-start | bytes 196616 | tf_op jit(solution)/shard_map/ppermute | solution.py:196

commit v13 on v12

--- a/solution.py
+++ b/solution.py
@@ -53,7 +53,7 @@
     )
 
 
-def delta_kernel(count, head_ref, feats_ref, *refs):
+def delta_kernel(count, head_ref, mine_ref, feats_ref, *refs):
     slots = (len(refs) - 9) // 4
     weight_refs = refs[: 3 * slots]
     bw_ref, bias_ref = refs[3 * slots], refs[3 * slots + 1]
@@ -123,7 +123,7 @@
 
     def step(c, carry):
         block = frames // count
-        owner = ((c * span) // block - head_ref[slots] + count) % count
+        owner = ((c * span) // block - mine_ref[0] + count) % count
         place = pl.ds(pl.multiple_of(owner * block + (c * span) % block, span), span)
         for h in range(slots):
             state = state_ref[h]
@@ -140,20 +140,20 @@
     lax.fori_loop(0, pairs, step, 0, unroll=pairs <= 8)
 
 
-def delta_layer(heads, full, qkv_weight, beta_weight, beta_bias, out_gain, count):
+def delta_layer(heads, mine, full, qkv_weight, beta_weight, beta_bias, out_gain, count):
     channels, frames = full.shape
-    slots = heads.shape[0] - 1
-    whole = lambda shape: pl.BlockSpec(shape, lambda i, head: (0,) * len(shape))
+    slots = heads.shape[0]
+    whole = lambda shape: pl.BlockSpec(shape, lambda i, head, mine: (0,) * len(shape))
     weight_specs = [
-        pl.BlockSpec((channels, HD), lambda i, head, p=p, j=j: (0, p * HEADS + head[j]))
+        pl.BlockSpec((channels, HD), lambda i, head, mine, p=p, j=j: (0, p * HEADS + head[j]))
         for p in range(3)
         for j in range(slots)
     ]
     gain_specs = [
-        pl.BlockSpec((HD,), lambda i, head, j=j: (head[j],)) for j in range(slots)
+        pl.BlockSpec((HD,), lambda i, head, mine, j=j: (head[j],)) for j in range(slots)
     ]
     grid_spec = pltpu.PrefetchScalarGridSpec(
-        num_scalar_prefetch=1,
+        num_scalar_prefetch=2,
         grid=(1,),
         in_specs=[whole((channels, frames))]
         + weight_specs
@@ -175,7 +175,7 @@
         out_shape=jax.ShapeDtypeStruct((frames, slots * HD), jnp.bfloat16),
         grid_spec=grid_spec,
     )(
-        heads, full, *([qkv_weight] * (3 * slots)), beta_weight.T, beta_bias.reshape(1, HEADS),
+        heads, mine, full, *([qkv_weight] * (3 * slots)), beta_weight.T, beta_bias.reshape(1, HEADS),
         *([gains] * slots),
     )
 
@@ -185,9 +185,11 @@
     mine = lax.axis_index("seq")
     slots = -(-HEADS // count)
     heads = jnp.minimum(mine * slots + jnp.arange(slots, dtype=jnp.int32), HEADS - 1)
-    meta = jnp.concatenate([heads, mine.astype(jnp.int32).reshape(1)])
     full = lax.all_gather(feats, "seq", axis=0, tiled=True)
-    mixed = delta_layer(meta, full, qkv_weight, beta_weight, beta_bias, out_gain, count)
+    mixed = delta_layer(
+        heads, mine.astype(jnp.int32).reshape(1), full, qkv_weight, beta_weight, beta_bias,
+        out_gain, count,
+    )
     frames = mixed.shape[0]
     rows = frames // count
     blocks = mixed.reshape(count, rows, slots * HD)

time: 36.8 us -> 36.8 us (level)
    concatenate x1 -> x0, other arithmetic: 0.66 us -> none  [body(): meta = jnp.concatenate([heads, mine.astype(jnp.int32).reshape(1)])]
    min x1, other arithmetic: 0.01 us -> 0.58 us  [body(): jnp.minimum(mine * slots + jnp.arange(slots, dtype=jnp.int32), HEADS - 1)]
where the time goes in v13:
time: 36.8 us; the launch traced here: 36.5 us
  blocking collectives  15.1 us (41%)
  Pallas kernels  11 us (30%)
  waiting for transfers between devices  4.6 us (12%)
  starting transfers between devices  2.63 us (7%)
  other arithmetic  2.14 us (6%)
  local copies, waits for them, and re-layouts  0.92 us (2%)
    all_gather x1, blocking collectives, body(): full = lax.all_gather(feats, 'seq', axis=0, tiled=True)  15.1 us
    pallas_call x1, Pallas kernels, delta_layer(): pl.pallas_call(functools.partial(delta_kernel, count), out_shape=jax.Shap...  11 us
    ppermute x3, waiting for transfers between devices, body(): lax.ppermute(blocks[d], 'seq', [(s, (s + d) % count) for s in range(count)])  4.6 us
    ppermute x3, starting transfers between devices, body(): lax.ppermute(blocks[d], 'seq', [(s, (s + d) % count) for s in range(count)])  2.63 us
    slice x1, local copies, waits for them, and re-layouts, body(): blocks[d]  0.92 us
    select_n x1, other arithmetic, body(): pick = jnp.where((mine - d) % count == k, got[d], pick)  0.87 us
  transfers between devices with their start and end apart: 3, of which 3 were waited for; matrix products, arithmetic and copies ran while one was open for 0% of the time, Pallas kernels for 0%

profile of v13, /device:TPU:0, one launch (start us, length us, event | category | flops | bytes accessed | tf_op | source)
XLA Modules:
  0.0 36.5 jit_solution(968735710530021766)
XLA Ops:
  0.0 0.6 %add_minimum_fusion.head_ref = s32[2]{0:T(128)} fusion(s32[]{:T(128)S(6)} %mul.3), kind=kLoop, calls=%fused_computation.4 | loop fusion | flops 4 | bytes 12 | tf_op jit(solution)/shard_map/min | solution.py:187
  0.6 15.1 %all_gather.3.feats_ref = bf16[768,512]{1,0:T(8,128)(2,1)} all-gather(bf16[192,512]{1,0:T(8,128)(2,1)} %param.5), channel_id=1, replica_groups=mesh['seq'=4,'batch'=8] {'seq'}, dimensions={0}, use_global_device_ids=true | all-gather | bytes 983040 | tf_op jit(solution)/shard_map/all_gather | solution.py:188
  15.7 11.0 %shard_map.55 = bf16[512,256]{1,0:T(8,128)(2,1)} custom-call(s32[2]{0:T(128)} %add_minimum_fusion.head_ref, s32[1]{0:T(128)} %bitcast.mine_ref, bf16[768,512]{1,0:T(8,128)(2,1)} %all_gather.3.feats_ref, bf16[768,2304]{1,0:T(8,128)(2,1)} %refs_5_.1, bf16[768,2304]{1,0:T(8,128)(2,1)} %refs_5_.1, bf16[768,2304]{1,0:T(8,128)(2,1)} %refs_5_.1, ...), custom_call_target="tpu_custom_call" | custom-call | tf_op jit(solution)/shard_map/pallas_call | solution.py:173
  26.8 0.9 %fusion = (bf16[128,256]{1,0:T(8,128)(2,1)S(1)}, bf16[128,256]{1,0:T(8,128)(2,1)S(1)}, bf16[128,256]{1,0:T(8,128)(2,1)S(1)}) fusion(bf16[512,256]{1,0:T(8,128)(2,1)} %shard_map.55), kind=kLoop, calls=%fused_computation.5 | loop fusion | bytes 393216 | tf_op jit(solution)/shard_map/slice | solution.py:198
  27.7 1.5 %collective-permute-start = (bf16[128,256]{1,0:T(8,128)(2,1)S(1)}, bf16[128,256]{1,0:T(8,128)(2,1)S(1)}, u32[]{:S(2)}, u32[]{:S(2)}) collective-permute-start(bf16[128,256]{1,0:T(8,128)(2,1)S(1)} %get-tuple-element.10), channel_id=1, source_target_pairs={{0,24},{8,0},{16,8},{24,16},{1,25},{9,1},{17,9},{25,17},{2,26},{10... | collective-permute-start | bytes 196616 | tf_op jit(solution)/shard_map/ppermute | solution.py:198
  29.2 0.6 %collective-permute-start.1 = (bf16[128,256]{1,0:T(8,128)(2,1)S(1)}, bf16[128,256]{1,0:T(8,128)(2,1)S(1)}, u32[]{:S(2)}, u32[]{:S(2)}) collective-permute-start(bf16[128,256]{1,0:T(8,128)(2,1)S(1)} %get-tuple-element.9), channel_id=1, source_target_pairs={{0,16},{8,24},{16,0},{24,8},{1,17},{9,25},{17,1},{25,9},{2,18},{10... | collective-permute-start | bytes 196616 | tf_op jit(solution)/shard_map/ppermute | solution.py:198
  29.7 0.6 %collective-permute-start.2 = (bf16[128,256]{1,0:T(8,128)(2,1)S(1)}, bf16[128,256]{1,0:T(8,128)(2,1)S(1)}, u32[]{:S(2)}, u32[]{:S(2)}) collective-permute-start(bf16[128,256]{1,0:T(8,128)(2,1)S(1)} %get-tuple-element.8), channel_id=1, source_target_pairs={{0,8},{8,16},{16,24},{24,0},{1,9},{9,17},{17,25},{25,1},{2,10},{10... | collective-permute-start | bytes 196616 | tf_op jit(solution)/shard_map/ppermute | solution.py:198
  30.3 2.3 %collective-permute-done = bf16[128,256]{1,0:T(8,128)(2,1)S(1)} collective-permute-done((bf16[128,256]{1,0:T(8,128)(2,1)S(1)}, bf16[128,256]{1,0:T(8,128)(2,1)S(1)}, u32[]{:S(2)}, u32[]{:S(2)}) %collective-permute-start) | collective-permute-done | bytes 65568 | tf_op jit(solution)/shard_map/ppermute | solution.py:198
  32.6 0.8 %collective-permute-done.1 = bf16[128,256]{1,0:T(8,128)(2,1)S(1)} collective-permute-done((bf16[128,256]{1,0:T(8,128)(2,1)S(1)}, bf16[128,256]{1,0:T(8,128)(2,1)S(1)}, u32[]{:S(2)}, u32[]{:S(2)}) %collective-permute-start.1) | collective-permute-done | bytes 65568 | tf_op jit(solution)/shard_map/ppermute | solution.py:198
  33.5 1.4 %collective-permute-done.2 = bf16[128,256]{1,0:T(8,128)(2,1)S(1)} collective-permute-done((bf16[128,256]{1,0:T(8,128)(2,1)S(1)}, bf16[128,256]{1,0:T(8,128)(2,1)S(1)}, u32[]{:S(2)}, u32[]{:S(2)}) %collective-permute-start.2) | collective-permute-done | bytes 65568 | tf_op jit(solution)/shard_map/ppermute | solution.py:198
  34.9 0.9 %select_select_fusion.2 = (bf16[128,256]{1,0:T(8,128)(2,1)S(1)}, bf16[128,256]{1,0:T(8,128)(2,1)S(1)}, bf16[128,256]{1,0:T(8,128)(2,1)S(1)}) fusion(bf16[128,256]{1,0:T(8,128)(2,1)S(1)} %collective-permute-done, bf16[128,256]{1,0:T(8,128)(2,1)S(1)} %collective-permute-done.1, bf16[128,256]{1,0:T(8,128)(2,1)S(1)} %collective-permute-done.2, pred[]{:T(512)S(6)} %eq.39, ...), kind=kLoop, calls=%fused_computation.3 | loop fusion | flops 294912 | bytes 458761 | tf_op jit(solution)/shard_map/jit(_where)/select_n | solution.py:204
  35.8 0.7 %pad_maximum_fusion = bf16[128,768]{1,0:T(8,128)(2,1)} fusion(bf16[128,256]{1,0:T(8,128)(2,1)S(1)} %get-tuple-element.6, bf16[128,256]{1,0:T(8,128)(2,1)S(1)} %get-tuple-element.7, bf16[128,256]{1,0:T(8,128)(2,1)S(1)} %get-tuple-element.5), kind=kLoop, calls=%fused_computation | loop fusion | flops 589824 | bytes 393216 | tf_op jit(solution)/shard_map/concatenate | solution.py:206
Async XLA Ops:
  27.7 4.9 %collective-permute-start = (bf16[128,256]{1,0:T(8,128)(2,1)S(1)}, bf16[128,256]{1,0:T(8,128)(2,1)S(1)}, u32[]{:S(2)}, u32[]{:S(2)}) collective-permute-start(bf16[128,256]{1,0:T(8,128)(2,1)S(1)} %get-tuple-element.10), channel_id=1, source_target_pairs={{0,24},{8,0},{16,8},{24,16},{1,25},{9,1},{17,9},{25,17},{2,26},{10... | collective-permute-start | bytes 196616 | tf_op jit(solution)/shard_map/ppermute | solution.py:198
  29.2 4.3 %collective-permute-start.1 = (bf16[128,256]{1,0:T(8,128)(2,1)S(1)}, bf16[128,256]{1,0:T(8,128)(2,1)S(1)}, u32[]{:S(2)}, u32[]{:S(2)}) collective-permute-start(bf16[128,256]{1,0:T(8,128)(2,1)S(1)} %get-tuple-element.9), channel_id=1, source_target_pairs={{0,16},{8,24},{16,0},{24,8},{1,17},{9,25},{17,1},{25,9},{2,18},{10... | collective-permute-start | bytes 196616 | tf_op jit(solution)/shard_map/ppermute | solution.py:198
  29.7 5.2 %collective-permute-start.2 = (bf16[128,256]{1,0:T(8,128)(2,1)S(1)}, bf16[128,256]{1,0:T(8,128)(2,1)S(1)}, u32[]{:S(2)}, u32[]{:S(2)}) collective-permute-start(bf16[128,256]{1,0:T(8,128)(2,1)S(1)} %get-tuple-element.8), channel_id=1, source_target_pairs={{0,8},{8,16},{16,24},{24,0},{1,9},{9,17},{17,25},{25,1},{2,10},{10... | collective-permute-start | bytes 196616 | tf_op jit(solution)/shard_map/ppermute | solution.py:198

commit v14 on v13

--- a/solution.py
+++ b/solution.py
@@ -106,25 +106,46 @@
         q2 = query[:, 1]
         carry = bmm_nt(w2, k1)
         cross = bmm_nt(q2, k1)
-        w_ref[h] = jnp.concatenate([w1, w2 - bmm(carry, w1), query[:, 0], q2], axis=1)
-        u_ref[h] = jnp.concatenate([u1, u2 - bmm(carry, u1)], axis=1)
-        k_ref[h] = jnp.swapaxes(keys.reshape(pairs, 2 * GROUP, HD), 1, 2)
+        wp = jnp.concatenate([w1, w2 - bmm(carry, w1)], axis=1)
+        up = jnp.concatenate([u1, u2 - bmm(carry, u1)], axis=1)
+        kp = keys.reshape(pairs, 2 * GROUP, HD)
+        qp = query.reshape(pairs, 2 * GROUP, HD)
         zero = jnp.zeros_like(cross)
-        p_ref[h] = jnp.concatenate(
+        pp = jnp.concatenate(
             [
                 jnp.concatenate([scores[:, 0], zero], axis=2),
                 jnp.concatenate([cross, scores[:, 1]], axis=2),
             ],
             axis=1,
         )
+        quads = pairs // 2
+        wp = wp.reshape(quads, 2, 2 * GROUP, HD)
+        up = up.reshape(quads, 2, 2 * GROUP, HD)
+        kp = kp.reshape(quads, 2, 2 * GROUP, HD)
+        qp = qp.reshape(quads, 2, 2 * GROUP, HD)
+        pp = pp.reshape(quads, 2, 2 * GROUP, 2 * GROUP)
+        carry2 = bmm_nt(wp[:, 1], kp[:, 0])
+        cross2 = bmm_nt(qp[:, 1], kp[:, 0])
+        w_ref[h] = jnp.concatenate(
+            [wp[:, 0], wp[:, 1] - bmm(carry2, wp[:, 0]), qp[:, 0], qp[:, 1]], axis=1
+        )
+        u_ref[h] = jnp.concatenate([up[:, 0], up[:, 1] - bmm(carry2, up[:, 0])], axis=1)
+        k_ref[h] = jnp.swapaxes(kp.reshape(quads, 4 * GROUP, HD), 1, 2)
+        zero2 = jnp.zeros_like(cross2)
+        p_ref[h] = jnp.concatenate(
+            [
+                jnp.concatenate([pp[:, 0], zero2], axis=2),
+                jnp.concatenate([cross2, pp[:, 1]], axis=2),
+            ],
+            axis=1,
+        )
 
     state_ref[...] = jnp.zeros_like(state_ref)
-    span = 2 * GROUP
+    span = 4 * GROUP
+    piece = 2 * GROUP
 
     def step(c, carry):
         block = frames // count
-        owner = ((c * span) // block - mine_ref[0] + count) % count
-        place = pl.ds(pl.multiple_of(owner * block + (c * span) % block, span), span)
         for h in range(slots):
             state = state_ref[h]
             both = mm(w_ref[h, c], state)
@@ -132,12 +153,15 @@
             state_ref[h] = state + mm(k_ref[h, c], residual)
             output = both[span:] + mm(p_ref[h, c], residual)
             power_mean = jnp.mean(output * output, -1, keepdims=True) + 1e-06
-            out_ref[place, pl.ds(h * HD, HD)] = (output * lax.rsqrt(power_mean) * gain_refs[h][...]).astype(
-                out_ref.dtype
-            )
+            mixed = (output * lax.rsqrt(power_mean) * gain_refs[h][...]).astype(out_ref.dtype)
+            for e in range(span // piece):
+                first = c * span + e * piece
+                owner = (first // block - mine_ref[0] + count) % count
+                place = pl.ds(pl.multiple_of(owner * block + first % block, piece), piece)
+                out_ref[place, pl.ds(h * HD, HD)] = mixed[e * piece : (e + 1) * piece]
         return carry
 
-    lax.fori_loop(0, pairs, step, 0, unroll=pairs <= 8)
+    lax.fori_loop(0, chunks // 4, step, 0, unroll=chunks <= 16)
 
 
 def delta_layer(heads, mine, full, qkv_weight, beta_weight, beta_bias, out_gain, count):
@@ -162,10 +186,10 @@
         out_specs=whole((frames, slots * HD)),
         scratch_shapes=[
             pltpu.VMEM((frames, 3 * slots * HD), jnp.bfloat16),
-            pltpu.VMEM((slots, frames // (2 * GROUP), HD, 2 * GROUP), jnp.float32),
-            pltpu.VMEM((slots, frames // (2 * GROUP), 4 * GROUP, HD), jnp.float32),
-            pltpu.VMEM((slots, frames // (2 * GROUP), 2 * GROUP, HD), jnp.float32),
-            pltpu.VMEM((slots, frames // (2 * GROUP), 2 * GROUP, 2 * GROUP), jnp.float32),
+            pltpu.VMEM((slots, frames // (4 * GROUP), HD, 4 * GROUP), jnp.float32),
+            pltpu.VMEM((slots, frames // (4 * GROUP), 8 * GROUP, HD), jnp.float32),
+            pltpu.VMEM((slots, frames // (4 * GROUP), 4 * GROUP, HD), jnp.float32),
+            pltpu.VMEM((slots, frames // (4 * GROUP), 4 * GROUP, 4 * GROUP), jnp.float32),
             pltpu.VMEM((slots, HD, HD), jnp.float32),
         ],
     )

time: 36.8 us -> 36.8 us (level)
  no operation moved by 1% of the time
where the time goes in v14:
time: 36.8 us; the launch traced here: 36.5 us
  blocking collectives  15.1 us (41%)
  Pallas kernels  11.1 us (30%)
  waiting for transfers between devices  4.6 us (12%)
  starting transfers between devices  2.63 us (7%)
  other arithmetic  2.14 us (6%)
  local copies, waits for them, and re-layouts  0.92 us (2%)
    all_gather x1, blocking collectives, body(): full = lax.all_gather(feats, 'seq', axis=0, tiled=True)  15.1 us
    pallas_call x1, Pallas kernels, delta_layer(): pl.pallas_call(functools.partial(delta_kernel, count), out_shape=jax.Shap...  11.1 us
    ppermute x3, waiting for transfers between devices, body(): lax.ppermute(blocks[d], 'seq', [(s, (s + d) % count) for s in range(count)])  4.6 us
    ppermute x3, starting transfers between devices, body(): lax.ppermute(blocks[d], 'seq', [(s, (s + d) % count) for s in range(count)])  2.63 us
    slice x1, local copies, waits for them, and re-layouts, body(): blocks[d]  0.92 us
    select_n x1, other arithmetic, body(): pick = jnp.where((mine - d) % count == k, got[d], pick)  0.87 us
  transfers between devices with their start and end apart: 3, of which 3 were waited for; matrix products, arithmetic and copies ran while one was open for 0% of the time, Pallas kernels for 0%

profile of v14, /device:TPU:0, one launch (start us, length us, event | category | flops | bytes accessed | tf_op | source)
XLA Modules:
  0.0 36.5 jit_solution(12415199950348984732)
XLA Ops:
  0.0 0.6 %add_minimum_fusion.head_ref = s32[2]{0:T(128)} fusion(s32[]{:T(128)S(6)} %mul.3), kind=kLoop, calls=%fused_computation.4 | loop fusion | flops 4 | bytes 12 | tf_op jit(solution)/shard_map/min | solution.py:211
  0.6 15.1 %all_gather.3.feats_ref = bf16[768,512]{1,0:T(8,128)(2,1)} all-gather(bf16[192,512]{1,0:T(8,128)(2,1)} %param.5), channel_id=1, replica_groups=mesh['seq'=4,'batch'=8] {'seq'}, dimensions={0}, use_global_device_ids=true | all-gather | bytes 983040 | tf_op jit(solution)/shard_map/all_gather | solution.py:212
  15.7 11.1 %shard_map.55 = bf16[512,256]{1,0:T(8,128)(2,1)} custom-call(s32[2]{0:T(128)} %add_minimum_fusion.head_ref, s32[1]{0:T(128)} %bitcast.mine_ref, bf16[768,512]{1,0:T(8,128)(2,1)} %all_gather.3.feats_ref, bf16[768,2304]{1,0:T(8,128)(2,1)} %refs_5_.1, bf16[768,2304]{1,0:T(8,128)(2,1)} %refs_5_.1, bf16[768,2304]{1,0:T(8,128)(2,1)} %refs_5_.1, ...), custom_call_target="tpu_custom_call" | custom-call | tf_op jit(solution)/shard_map/pallas_call | solution.py:197
  26.8 0.9 %fusion = (bf16[128,256]{1,0:T(8,128)(2,1)S(1)}, bf16[128,256]{1,0:T(8,128)(2,1)S(1)}, bf16[128,256]{1,0:T(8,128)(2,1)S(1)}) fusion(bf16[512,256]{1,0:T(8,128)(2,1)} %shard_map.55), kind=kLoop, calls=%fused_computation.5 | loop fusion | bytes 393216 | tf_op jit(solution)/shard_map/slice | solution.py:222
  27.7 1.5 %collective-permute-start = (bf16[128,256]{1,0:T(8,128)(2,1)S(1)}, bf16[128,256]{1,0:T(8,128)(2,1)S(1)}, u32[]{:S(2)}, u32[]{:S(2)}) collective-permute-start(bf16[128,256]{1,0:T(8,128)(2,1)S(1)} %get-tuple-element.10), channel_id=1, source_target_pairs={{0,24},{8,0},{16,8},{24,16},{1,25},{9,1},{17,9},{25,17},{2,26},{10... | collective-permute-start | bytes 196616 | tf_op jit(solution)/shard_map/ppermute | solution.py:222
  29.2 0.6 %collective-permute-start.1 = (bf16[128,256]{1,0:T(8,128)(2,1)S(1)}, bf16[128,256]{1,0:T(8,128)(2,1)S(1)}, u32[]{:S(2)}, u32[]{:S(2)}) collective-permute-start(bf16[128,256]{1,0:T(8,128)(2,1)S(1)} %get-tuple-element.9), channel_id=1, source_target_pairs={{0,16},{8,24},{16,0},{24,8},{1,17},{9,25},{17,1},{25,9},{2,18},{10... | collective-permute-start | bytes 196616 | tf_op jit(solution)/shard_map/ppermute | solution.py:222
  29.8 0.6 %collective-permute-start.2 = (bf16[128,256]{1,0:T(8,128)(2,1)S(1)}, bf16[128,256]{1,0:T(8,128)(2,1)S(1)}, u32[]{:S(2)}, u32[]{:S(2)}) collective-permute-start(bf16[128,256]{1,0:T(8,128)(2,1)S(1)} %get-tuple-element.8), channel_id=1, source_target_pairs={{0,8},{8,16},{16,24},{24,0},{1,9},{9,17},{17,25},{25,1},{2,10},{10... | collective-permute-start | bytes 196616 | tf_op jit(solution)/shard_map/ppermute | solution.py:222
  30.3 2.3 %collective-permute-done = bf16[128,256]{1,0:T(8,128)(2,1)S(1)} collective-permute-done((bf16[128,256]{1,0:T(8,128)(2,1)S(1)}, bf16[128,256]{1,0:T(8,128)(2,1)S(1)}, u32[]{:S(2)}, u32[]{:S(2)}) %collective-permute-start) | collective-permute-done | bytes 65568 | tf_op jit(solution)/shard_map/ppermute | solution.py:222
  32.6 0.8 %collective-permute-done.1 = bf16[128,256]{1,0:T(8,128)(2,1)S(1)} collective-permute-done((bf16[128,256]{1,0:T(8,128)(2,1)S(1)}, bf16[128,256]{1,0:T(8,128)(2,1)S(1)}, u32[]{:S(2)}, u32[]{:S(2)}) %collective-permute-start.1) | collective-permute-done | bytes 65568 | tf_op jit(solution)/shard_map/ppermute | solution.py:222
  33.5 1.5 %collective-permute-done.2 = bf16[128,256]{1,0:T(8,128)(2,1)S(1)} collective-permute-done((bf16[128,256]{1,0:T(8,128)(2,1)S(1)}, bf16[128,256]{1,0:T(8,128)(2,1)S(1)}, u32[]{:S(2)}, u32[]{:S(2)}) %collective-permute-start.2) | collective-permute-done | bytes 65568 | tf_op jit(solution)/shard_map/ppermute | solution.py:222
  34.9 0.9 %select_select_fusion.2 = (bf16[128,256]{1,0:T(8,128)(2,1)S(1)}, bf16[128,256]{1,0:T(8,128)(2,1)S(1)}, bf16[128,256]{1,0:T(8,128)(2,1)S(1)}) fusion(bf16[128,256]{1,0:T(8,128)(2,1)S(1)} %collective-permute-done, bf16[128,256]{1,0:T(8,128)(2,1)S(1)} %collective-permute-done.1, bf16[128,256]{1,0:T(8,128)(2,1)S(1)} %collective-permute-done.2, pred[]{:T(512)S(6)} %eq.39, ...), kind=kLoop, calls=%fused_computation.3 | loop fusion | flops 294912 | bytes 458761 | tf_op jit(solution)/shard_map/jit(_where)/select_n | solution.py:228
  35.8 0.7 %pad_maximum_fusion = bf16[128,768]{1,0:T(8,128)(2,1)} fusion(bf16[128,256]{1,0:T(8,128)(2,1)S(1)} %get-tuple-element.6, bf16[128,256]{1,0:T(8,128)(2,1)S(1)} %get-tuple-element.7, bf16[128,256]{1,0:T(8,128)(2,1)S(1)} %get-tuple-element.5), kind=kLoop, calls=%fused_computation | loop fusion | flops 589824 | bytes 393216 | tf_op jit(solution)/shard_map/concatenate | solution.py:230
Async XLA Ops:
  27.7 4.9 %collective-permute-start = (bf16[128,256]{1,0:T(8,128)(2,1)S(1)}, bf16[128,256]{1,0:T(8,128)(2,1)S(1)}, u32[]{:S(2)}, u32[]{:S(2)}) collective-permute-start(bf16[128,256]{1,0:T(8,128)(2,1)S(1)} %get-tuple-element.10), channel_id=1, source_target_pairs={{0,24},{8,0},{16,8},{24,16},{1,25},{9,1},{17,9},{25,17},{2,26},{10... | collective-permute-start | bytes 196616 | tf_op jit(solution)/shard_map/ppermute | solution.py:222
  29.2 4.3 %collective-permute-start.1 = (bf16[128,256]{1,0:T(8,128)(2,1)S(1)}, bf16[128,256]{1,0:T(8,128)(2,1)S(1)}, u32[]{:S(2)}, u32[]{:S(2)}) collective-permute-start(bf16[128,256]{1,0:T(8,128)(2,1)S(1)} %get-tuple-element.9), channel_id=1, source_target_pairs={{0,16},{8,24},{16,0},{24,8},{1,17},{9,25},{17,1},{25,9},{2,18},{10... | collective-permute-start | bytes 196616 | tf_op jit(solution)/shard_map/ppermute | solution.py:222
  29.8 5.2 %collective-permute-start.2 = (bf16[128,256]{1,0:T(8,128)(2,1)S(1)}, bf16[128,256]{1,0:T(8,128)(2,1)S(1)}, u32[]{:S(2)}, u32[]{:S(2)}) collective-permute-start(bf16[128,256]{1,0:T(8,128)(2,1)S(1)} %get-tuple-element.8), channel_id=1, source_target_pairs={{0,8},{8,16},{16,24},{24,0},{1,9},{9,17},{17,25},{25,1},{2,10},{10... | collective-permute-start | bytes 196616 | tf_op jit(solution)/shard_map/ppermute | solution.py:222

commit v15 on v13

--- a/solution.py
+++ b/solution.py
@@ -53,7 +53,7 @@
     )
 
 
-def delta_kernel(count, head_ref, mine_ref, feats_ref, *refs):
+def delta_kernel(count, slots_arg, mine_ref, feats_ref, *refs):
     slots = (len(refs) - 9) // 4
     weight_refs = refs[: 3 * slots]
     bw_ref, bias_ref = refs[3 * slots], refs[3 * slots + 1]
@@ -83,7 +83,8 @@
         query = unit_normed(qkv_ref[:, pl.ds(h * HD, HD)].astype(jnp.float32))
         keys = unit_normed(qkv_ref[:, pl.ds(width + h * HD, HD)].astype(jnp.float32))
         values = qkv_ref[:, pl.ds(2 * width + h * HD, HD)].astype(jnp.float32)
-        rates = jnp.sum(jnp.where(lane == head_ref[h], beta_all, 0.0), -1, keepdims=True)
+        head = jnp.minimum(mine_ref[0] * slots + h, HEADS - 1)
+        rates = jnp.sum(jnp.where(lane == head, beta_all, 0.0), -1, keepdims=True)
         weighted = (keys * rates).reshape(chunks, GROUP, HD)
         scaled = (values * rates).reshape(chunks, GROUP, HD)
         query = query.reshape(chunks, GROUP, HD)
@@ -140,20 +141,20 @@
     lax.fori_loop(0, pairs, step, 0, unroll=pairs <= 8)
 
 
-def delta_layer(heads, mine, full, qkv_weight, beta_weight, beta_bias, out_gain, count):
+def delta_layer(slots, mine, full, qkv_weight, beta_weight, beta_bias, out_gain, count):
     channels, frames = full.shape
-    slots = heads.shape[0]
-    whole = lambda shape: pl.BlockSpec(shape, lambda i, head, mine: (0,) * len(shape))
+    pick = lambda mine, j: jnp.minimum(mine[0] * slots + j, HEADS - 1)
+    whole = lambda shape: pl.BlockSpec(shape, lambda i, mine: (0,) * len(shape))
     weight_specs = [
-        pl.BlockSpec((channels, HD), lambda i, head, mine, p=p, j=j: (0, p * HEADS + head[j]))
+        pl.BlockSpec((channels, HD), lambda i, mine, p=p, j=j: (0, p * HEADS + pick(mine, j)))
         for p in range(3)
         for j in range(slots)
     ]
     gain_specs = [
-        pl.BlockSpec((HD,), lambda i, head, mine, j=j: (head[j],)) for j in range(slots)
+        pl.BlockSpec((HD,), lambda i, mine, j=j: (pick(mine, j),)) for j in range(slots)
     ]
     grid_spec = pltpu.PrefetchScalarGridSpec(
-        num_scalar_prefetch=2,
+        num_scalar_prefetch=1,
         grid=(1,),
         in_specs=[whole((channels, frames))]
         + weight_specs
@@ -171,11 +172,11 @@
     )
     gains = out_gain
     return pl.pallas_call(
-        functools.partial(delta_kernel, count),
+        functools.partial(delta_kernel, count, slots),
         out_shape=jax.ShapeDtypeStruct((frames, slots * HD), jnp.bfloat16),
         grid_spec=grid_spec,
     )(
-        heads, mine, full, *([qkv_weight] * (3 * slots)), beta_weight.T, beta_bias.reshape(1, HEADS),
+        mine, full, *([qkv_weight] * (3 * slots)), beta_weight.T, beta_bias.reshape(1, HEADS),
         *([gains] * slots),
     )
 
@@ -184,10 +185,9 @@
     count = lax.axis_size("seq")
     mine = lax.axis_index("seq")
     slots = -(-HEADS // count)
-    heads = jnp.minimum(mine * slots + jnp.arange(slots, dtype=jnp.int32), HEADS - 1)
     full = lax.all_gather(feats, "seq", axis=0, tiled=True)
     mixed = delta_layer(
-        heads, mine.astype(jnp.int32).reshape(1), full, qkv_weight, beta_weight, beta_bias,
+        slots, mine.astype(jnp.int32).reshape(1), full, qkv_weight, beta_weight, beta_bias,
         out_gain, count,
     )
     frames = mixed.shape[0]

time: 36.8 us -> 35.5 us (0.965)
  Pallas kernels: 11 us -> 10.4 us
  other arithmetic: 2.14 us -> 1.56 us
    pallas_call x1, Pallas kernels: 11 us -> 10.4 us  [delta_layer(): pl.pallas_call(functools.partial(delta_kernel, count, slots), out_shape=j...]
    min x1 -> x0, other arithmetic: 0.58 us -> none  [body(): jnp.minimum(mine * slots + jnp.arange(slots, dtype=jnp.int32), HEADS - 1)]
where the time goes in v15:
time: 35.5 us; the launch traced here: 35.2 us
  blocking collectives  15.1 us (43%)
  Pallas kernels  10.4 us (29%)
  waiting for transfers between devices  4.6 us (13%)
  starting transfers between devices  2.64 us (7%)
  other arithmetic  1.56 us (4%)
  local copies, waits for them, and re-layouts  0.92 us (3%)
    all_gather x1, blocking collectives, body(): full = lax.all_gather(feats, 'seq', axis=0, tiled=True)  15.1 us
    pallas_call x1, Pallas kernels, delta_layer(): pl.pallas_call(functools.partial(delta_kernel, count, slots), out_shape=j...  10.4 us
    ppermute x3, waiting for transfers between devices, body(): lax.ppermute(blocks[d], 'seq', [(s, (s + d) % count) for s in range(count)])  4.6 us
    ppermute x3, starting transfers between devices, body(): lax.ppermute(blocks[d], 'seq', [(s, (s + d) % count) for s in range(count)])  2.64 us
    slice x1, local copies, waits for them, and re-layouts, body(): blocks[d]  0.92 us
    select_n x1, other arithmetic, body(): pick = jnp.where((mine - d) % count == k, got[d], pick)  0.87 us
  transfers between devices with their start and end apart: 3, of which 3 were waited for; matrix products, arithmetic and copies ran while one was open for 0% of the time, Pallas kernels for 0%

profile of v15, /device:TPU:0, one launch (start us, length us, event | category | flops | bytes accessed | tf_op | source)
XLA Modules:
  0.0 35.2 jit_solution(16462764519812964913)
XLA Ops:
  0.0 15.1 %all_gather.3.feats_ref = bf16[768,512]{1,0:T(8,128)(2,1)} all-gather(bf16[192,512]{1,0:T(8,128)(2,1)} %param.5), channel_id=1, replica_groups=mesh['seq'=4,'batch'=8] {'seq'}, dimensions={0}, use_global_device_ids=true | all-gather | bytes 983040 | tf_op jit(solution)/shard_map/all_gather | solution.py:188
  15.1 10.4 %shard_map.55 = bf16[512,256]{1,0:T(8,128)(2,1)} custom-call(s32[1]{0:T(128)} %bitcast.mine_ref, bf16[768,512]{1,0:T(8,128)(2,1)} %all_gather.3.feats_ref, bf16[768,2304]{1,0:T(8,128)(2,1)} %refs_5_.1, bf16[768,2304]{1,0:T(8,128)(2,1)} %refs_5_.1, bf16[768,2304]{1,0:T(8,128)(2,1)} %refs_5_.1, bf16[768,2304]{1,0:T(8,128)(2,1)} %refs_5_.1, ...), custom_call_target="tpu_custom_call" | custom-call | tf_op jit(solution)/shard_map/pallas_call | solution.py:174
  25.5 0.9 %fusion = (bf16[128,256]{1,0:T(8,128)(2,1)S(1)}, bf16[128,256]{1,0:T(8,128)(2,1)S(1)}, bf16[128,256]{1,0:T(8,128)(2,1)S(1)}) fusion(bf16[512,256]{1,0:T(8,128)(2,1)} %shard_map.55), kind=kLoop, calls=%fused_computation.4 | loop fusion | bytes 393216 | tf_op jit(solution)/shard_map/slice | solution.py:198
  26.4 1.5 %collective-permute-start = (bf16[128,256]{1,0:T(8,128)(2,1)S(1)}, bf16[128,256]{1,0:T(8,128)(2,1)S(1)}, u32[]{:S(2)}, u32[]{:S(2)}) collective-permute-start(bf16[128,256]{1,0:T(8,128)(2,1)S(1)} %get-tuple-element.10), channel_id=1, source_target_pairs={{0,24},{8,0},{16,8},{24,16},{1,25},{9,1},{17,9},{25,17},{2,26},{10... | collective-permute-start | bytes 196616 | tf_op jit(solution)/shard_map/ppermute | solution.py:198
  27.9 0.6 %collective-permute-start.1 = (bf16[128,256]{1,0:T(8,128)(2,1)S(1)}, bf16[128,256]{1,0:T(8,128)(2,1)S(1)}, u32[]{:S(2)}, u32[]{:S(2)}) collective-permute-start(bf16[128,256]{1,0:T(8,128)(2,1)S(1)} %get-tuple-element.9), channel_id=1, source_target_pairs={{0,16},{8,24},{16,0},{24,8},{1,17},{9,25},{17,1},{25,9},{2,18},{10... | collective-permute-start | bytes 196616 | tf_op jit(solution)/shard_map/ppermute | solution.py:198
  28.5 0.6 %collective-permute-start.2 = (bf16[128,256]{1,0:T(8,128)(2,1)S(1)}, bf16[128,256]{1,0:T(8,128)(2,1)S(1)}, u32[]{:S(2)}, u32[]{:S(2)}) collective-permute-start(bf16[128,256]{1,0:T(8,128)(2,1)S(1)} %get-tuple-element.8), channel_id=1, source_target_pairs={{0,8},{8,16},{16,24},{24,0},{1,9},{9,17},{17,25},{25,1},{2,10},{10... | collective-permute-start | bytes 196616 | tf_op jit(solution)/shard_map/ppermute | solution.py:198
  29.1 2.3 %collective-permute-done = bf16[128,256]{1,0:T(8,128)(2,1)S(1)} collective-permute-done((bf16[128,256]{1,0:T(8,128)(2,1)S(1)}, bf16[128,256]{1,0:T(8,128)(2,1)S(1)}, u32[]{:S(2)}, u32[]{:S(2)}) %collective-permute-start) | collective-permute-done | bytes 65568 | tf_op jit(solution)/shard_map/ppermute | solution.py:198
  31.4 0.8 %collective-permute-done.1 = bf16[128,256]{1,0:T(8,128)(2,1)S(1)} collective-permute-done((bf16[128,256]{1,0:T(8,128)(2,1)S(1)}, bf16[128,256]{1,0:T(8,128)(2,1)S(1)}, u32[]{:S(2)}, u32[]{:S(2)}) %collective-permute-start.1) | collective-permute-done | bytes 65568 | tf_op jit(solution)/shard_map/ppermute | solution.py:198
  32.2 1.4 %collective-permute-done.2 = bf16[128,256]{1,0:T(8,128)(2,1)S(1)} collective-permute-done((bf16[128,256]{1,0:T(8,128)(2,1)S(1)}, bf16[128,256]{1,0:T(8,128)(2,1)S(1)}, u32[]{:S(2)}, u32[]{:S(2)}) %collective-permute-start.2) | collective-permute-done | bytes 65568 | tf_op jit(solution)/shard_map/ppermute | solution.py:198
  33.7 0.9 %select_select_fusion.2 = (bf16[128,256]{1,0:T(8,128)(2,1)S(1)}, bf16[128,256]{1,0:T(8,128)(2,1)S(1)}, bf16[128,256]{1,0:T(8,128)(2,1)S(1)}) fusion(bf16[128,256]{1,0:T(8,128)(2,1)S(1)} %collective-permute-done, bf16[128,256]{1,0:T(8,128)(2,1)S(1)} %collective-permute-done.1, bf16[128,256]{1,0:T(8,128)(2,1)S(1)} %collective-permute-done.2, pred[]{:T(512)S(6)} %eq.39, ...), kind=kLoop, calls=%fused_computation.3 | loop fusion | flops 294912 | bytes 458761 | tf_op jit(solution)/shard_map/jit(_where)/select_n | solution.py:204
  34.5 0.7 %pad_maximum_fusion = bf16[128,768]{1,0:T(8,128)(2,1)} fusion(bf16[128,256]{1,0:T(8,128)(2,1)S(1)} %get-tuple-element.6, bf16[128,256]{1,0:T(8,128)(2,1)S(1)} %get-tuple-element.7, bf16[128,256]{1,0:T(8,128)(2,1)S(1)} %get-tuple-element.5), kind=kLoop, calls=%fused_computation | loop fusion | flops 589824 | bytes 393216 | tf_op jit(solution)/shard_map/concatenate | solution.py:206
Async XLA Ops:
  26.4 4.9 %collective-permute-start = (bf16[128,256]{1,0:T(8,128)(2,1)S(1)}, bf16[128,256]{1,0:T(8,128)(2,1)S(1)}, u32[]{:S(2)}, u32[]{:S(2)}) collective-permute-start(bf16[128,256]{1,0:T(8,128)(2,1)S(1)} %get-tuple-element.10), channel_id=1, source_target_pairs={{0,24},{8,0},{16,8},{24,16},{1,25},{9,1},{17,9},{25,17},{2,26},{10... | collective-permute-start | bytes 196616 | tf_op jit(solution)/shard_map/ppermute | solution.py:198
  27.9 4.3 %collective-permute-start.1 = (bf16[128,256]{1,0:T(8,128)(2,1)S(1)}, bf16[128,256]{1,0:T(8,128)(2,1)S(1)}, u32[]{:S(2)}, u32[]{:S(2)}) collective-permute-start(bf16[128,256]{1,0:T(8,128)(2,1)S(1)} %get-tuple-element.9), channel_id=1, source_target_pairs={{0,16},{8,24},{16,0},{24,8},{1,17},{9,25},{17,1},{25,9},{2,18},{10... | collective-permute-start | bytes 196616 | tf_op jit(solution)/shard_map/ppermute | solution.py:198
  28.5 5.2 %collective-permute-start.2 = (bf16[128,256]{1,0:T(8,128)(2,1)S(1)}, bf16[128,256]{1,0:T(8,128)(2,1)S(1)}, u32[]{:S(2)}, u32[]{:S(2)}) collective-permute-start(bf16[128,256]{1,0:T(8,128)(2,1)S(1)} %get-tuple-element.8), channel_id=1, source_target_pairs={{0,8},{8,16},{16,24},{24,0},{1,9},{9,17},{17,25},{25,1},{2,10},{10... | collective-permute-start | bytes 196616 | tf_op jit(solution)/shard_map/ppermute | solution.py:198

commit v16 on v15

--- a/solution.py
+++ b/solution.py
@@ -131,7 +131,9 @@
             both = mm(w_ref[h, c], state)
             residual = u_ref[h, c] - both[:span]
             state_ref[h] = state + mm(k_ref[h, c], residual)
-            output = both[span:] + mm(p_ref[h, c], residual)
+            output = both[span:] + jnp.dot(
+                p_ref[h, c], residual, preferred_element_type=jnp.float32
+            )
             power_mean = jnp.mean(output * output, -1, keepdims=True) + 1e-06
             out_ref[place, pl.ds(h * HD, HD)] = (output * lax.rsqrt(power_mean) * gain_refs[h][...]).astype(
                 out_ref.dtype

time: 35.5 us -> 35.3 us (level)
  no operation moved by 1% of the time
where the time goes in v16:
time: 35.3 us; the launch traced here: 35.1 us
  blocking collectives  15.1 us (43%)
  Pallas kernels  10.2 us (29%)
  waiting for transfers between devices  4.6 us (13%)
  starting transfers between devices  2.64 us (7%)
  other arithmetic  1.56 us (4%)
  local copies, waits for them, and re-layouts  0.92 us (3%)
    all_gather x1, blocking collectives, body(): full = lax.all_gather(feats, 'seq', axis=0, tiled=True)  15.1 us
    pallas_call x1, Pallas kernels, delta_layer(): pl.pallas_call(functools.partial(delta_kernel, count, slots), out_shape=j...  10.2 us
    ppermute x3, waiting for transfers between devices, body(): lax.ppermute(blocks[d], 'seq', [(s, (s + d) % count) for s in range(count)])  4.6 us
    ppermute x3, starting transfers between devices, body(): lax.ppermute(blocks[d], 'seq', [(s, (s + d) % count) for s in range(count)])  2.64 us
    slice x1, local copies, waits for them, and re-layouts, body(): blocks[d]  0.92 us
    select_n x1, other arithmetic, body(): pick = jnp.where((mine - d) % count == k, got[d], pick)  0.87 us
  transfers between devices with their start and end apart: 3, of which 3 were waited for; matrix products, arithmetic and copies ran while one was open for 0% of the time, Pallas kernels for 0%

profile of v16, /device:TPU:0, one launch (start us, length us, event | category | flops | bytes accessed | tf_op | source)
XLA Modules:
  0.0 35.1 jit_solution(10742546635282439303)
XLA Ops:
  0.0 15.1 %all_gather.3.feats_ref = bf16[768,512]{1,0:T(8,128)(2,1)} all-gather(bf16[192,512]{1,0:T(8,128)(2,1)} %param.5), channel_id=1, replica_groups=mesh['seq'=4,'batch'=8] {'seq'}, dimensions={0}, use_global_device_ids=true | all-gather | bytes 983040 | tf_op jit(solution)/shard_map/all_gather | solution.py:190
  15.1 10.2 %shard_map.55 = bf16[512,256]{1,0:T(8,128)(2,1)} custom-call(s32[1]{0:T(128)} %bitcast.mine_ref, bf16[768,512]{1,0:T(8,128)(2,1)} %all_gather.3.feats_ref, bf16[768,2304]{1,0:T(8,128)(2,1)} %refs_5_.1, bf16[768,2304]{1,0:T(8,128)(2,1)} %refs_5_.1, bf16[768,2304]{1,0:T(8,128)(2,1)} %refs_5_.1, bf16[768,2304]{1,0:T(8,128)(2,1)} %refs_5_.1, ...), custom_call_target="tpu_custom_call" | custom-call | tf_op jit(solution)/shard_map/pallas_call | solution.py:176
  25.3 0.9 %fusion = (bf16[128,256]{1,0:T(8,128)(2,1)S(1)}, bf16[128,256]{1,0:T(8,128)(2,1)S(1)}, bf16[128,256]{1,0:T(8,128)(2,1)S(1)}) fusion(bf16[512,256]{1,0:T(8,128)(2,1)} %shard_map.55), kind=kLoop, calls=%fused_computation.4 | loop fusion | bytes 393216 | tf_op jit(solution)/shard_map/slice | solution.py:200
  26.3 1.5 %collective-permute-start = (bf16[128,256]{1,0:T(8,128)(2,1)S(1)}, bf16[128,256]{1,0:T(8,128)(2,1)S(1)}, u32[]{:S(2)}, u32[]{:S(2)}) collective-permute-start(bf16[128,256]{1,0:T(8,128)(2,1)S(1)} %get-tuple-element.10), channel_id=1, source_target_pairs={{0,24},{8,0},{16,8},{24,16},{1,25},{9,1},{17,9},{25,17},{2,26},{10... | collective-permute-start | bytes 196616 | tf_op jit(solution)/shard_map/ppermute | solution.py:200
  27.8 0.6 %collective-permute-start.1 = (bf16[128,256]{1,0:T(8,128)(2,1)S(1)}, bf16[128,256]{1,0:T(8,128)(2,1)S(1)}, u32[]{:S(2)}, u32[]{:S(2)}) collective-permute-start(bf16[128,256]{1,0:T(8,128)(2,1)S(1)} %get-tuple-element.9), channel_id=1, source_target_pairs={{0,16},{8,24},{16,0},{24,8},{1,17},{9,25},{17,1},{25,9},{2,18},{10... | collective-permute-start | bytes 196616 | tf_op jit(solution)/shard_map/ppermute | solution.py:200
  28.3 0.6 %collective-permute-start.2 = (bf16[128,256]{1,0:T(8,128)(2,1)S(1)}, bf16[128,256]{1,0:T(8,128)(2,1)S(1)}, u32[]{:S(2)}, u32[]{:S(2)}) collective-permute-start(bf16[128,256]{1,0:T(8,128)(2,1)S(1)} %get-tuple-element.8), channel_id=1, source_target_pairs={{0,8},{8,16},{16,24},{24,0},{1,9},{9,17},{17,25},{25,1},{2,10},{10... | collective-permute-start | bytes 196616 | tf_op jit(solution)/shard_map/ppermute | solution.py:200
  28.9 2.3 %collective-permute-done = bf16[128,256]{1,0:T(8,128)(2,1)S(1)} collective-permute-done((bf16[128,256]{1,0:T(8,128)(2,1)S(1)}, bf16[128,256]{1,0:T(8,128)(2,1)S(1)}, u32[]{:S(2)}, u32[]{:S(2)}) %collective-permute-start) | collective-permute-done | bytes 65568 | tf_op jit(solution)/shard_map/ppermute | solution.py:200
  31.2 0.8 %collective-permute-done.1 = bf16[128,256]{1,0:T(8,128)(2,1)S(1)} collective-permute-done((bf16[128,256]{1,0:T(8,128)(2,1)S(1)}, bf16[128,256]{1,0:T(8,128)(2,1)S(1)}, u32[]{:S(2)}, u32[]{:S(2)}) %collective-permute-start.1) | collective-permute-done | bytes 65568 | tf_op jit(solution)/shard_map/ppermute | solution.py:200
  32.0 1.4 %collective-permute-done.2 = bf16[128,256]{1,0:T(8,128)(2,1)S(1)} collective-permute-done((bf16[128,256]{1,0:T(8,128)(2,1)S(1)}, bf16[128,256]{1,0:T(8,128)(2,1)S(1)}, u32[]{:S(2)}, u32[]{:S(2)}) %collective-permute-start.2) | collective-permute-done | bytes 65568 | tf_op jit(solution)/shard_map/ppermute | solution.py:200
  33.5 0.9 %select_select_fusion.2 = (bf16[128,256]{1,0:T(8,128)(2,1)S(1)}, bf16[128,256]{1,0:T(8,128)(2,1)S(1)}, bf16[128,256]{1,0:T(8,128)(2,1)S(1)}) fusion(bf16[128,256]{1,0:T(8,128)(2,1)S(1)} %collective-permute-done, bf16[128,256]{1,0:T(8,128)(2,1)S(1)} %collective-permute-done.1, bf16[128,256]{1,0:T(8,128)(2,1)S(1)} %collective-permute-done.2, pred[]{:T(512)S(6)} %eq.39, ...), kind=kLoop, calls=%fused_computation.3 | loop fusion | flops 294912 | bytes 458761 | tf_op jit(solution)/shard_map/jit(_where)/select_n | solution.py:206
  34.4 0.7 %pad_maximum_fusion = bf16[128,768]{1,0:T(8,128)(2,1)} fusion(bf16[128,256]{1,0:T(8,128)(2,1)S(1)} %get-tuple-element.6, bf16[128,256]{1,0:T(8,128)(2,1)S(1)} %get-tuple-element.7, bf16[128,256]{1,0:T(8,128)(2,1)S(1)} %get-tuple-element.5), kind=kLoop, calls=%fused_computation | loop fusion | flops 589824 | bytes 393216 | tf_op jit(solution)/shard_map/concatenate | solution.py:208
Async XLA Ops:
  26.3 4.9 %collective-permute-start = (bf16[128,256]{1,0:T(8,128)(2,1)S(1)}, bf16[128,256]{1,0:T(8,128)(2,1)S(1)}, u32[]{:S(2)}, u32[]{:S(2)}) collective-permute-start(bf16[128,256]{1,0:T(8,128)(2,1)S(1)} %get-tuple-element.10), channel_id=1, source_target_pairs={{0,24},{8,0},{16,8},{24,16},{1,25},{9,1},{17,9},{25,17},{2,26},{10... | collective-permute-start | bytes 196616 | tf_op jit(solution)/shard_map/ppermute | solution.py:200
  27.8 4.3 %collective-permute-start.1 = (bf16[128,256]{1,0:T(8,128)(2,1)S(1)}, bf16[128,256]{1,0:T(8,128)(2,1)S(1)}, u32[]{:S(2)}, u32[]{:S(2)}) collective-permute-start(bf16[128,256]{1,0:T(8,128)(2,1)S(1)} %get-tuple-element.9), channel_id=1, source_target_pairs={{0,16},{8,24},{16,0},{24,8},{1,17},{9,25},{17,1},{25,9},{2,18},{10... | collective-permute-start | bytes 196616 | tf_op jit(solution)/shard_map/ppermute | solution.py:200
  28.3 5.2 %collective-permute-start.2 = (bf16[128,256]{1,0:T(8,128)(2,1)S(1)}, bf16[128,256]{1,0:T(8,128)(2,1)S(1)}, u32[]{:S(2)}, u32[]{:S(2)}) collective-permute-start(bf16[128,256]{1,0:T(8,128)(2,1)S(1)} %get-tuple-element.8), channel_id=1, source_target_pairs={{0,8},{8,16},{16,24},{24,0},{1,9},{9,17},{17,25},{25,1},{2,10},{10... | collective-permute-start | bytes 196616 | tf_op jit(solution)/shard_map/ppermute | solution.py:200
